TPU v7x, 32 devices: a whole 2x2x4 slice. The times are simulated.
32 devices in a mesh: row: 8 (over z, y), col: 4 (over x, core).
Axes of the slice: x: 2, y: 2, z: 4, core: 2. Of those that a mesh axis runs over, the one named last changes fastest.
Arguments:
- design: bfloat16 [256, 24576], P('row', 'col'), may hold values from -0.375 to 0.375
- filter_taps: float32 [256], replicated, may hold values from -0.21875 to 0.21875
- probes: float32 [24576, 128], P('row', 'col'), may hold values from -576 to 576
- lower_bound: float32 [1], replicated, may hold values from 6 to 24
- upper_bound: float32 [1], replicated, may hold values from 192 to 288
Outputs:
- normal: float32 [24576, 24576], P('row', 'col')
- solution: float32 [24576, 128], P('row', 'col')
All inputs are finite; a program needn't handle non-finite values.
Results may differ from a plain program's by a relative error of at most 0.0072.
The roundings to bfloat16 on the way count: a program that leaves them out, or rounds other values in their place, can miss the bound.
Values may be sent and summed in bfloat16 or wider, within the bound.
No kernel may reach another device: no remote copies, remote signals or barrier semaphores. Data moves between devices by JAX's collectives and lax.ppermute only.
A program may use at most 128 MiB of HBM per device.

v0:
```python
import jax
import jax.numpy as jnp
from jax import lax
from jax.sharding import PartitionSpec as P

SWEEPS = 2


def broadcast(block, axis, owner):
    block = jnp.where(lax.axis_index(axis) == owner, block, jnp.zeros_like(block))
    return lax.psum(block, axis)


def whitening(filter_taps):
    count = filter_taps.shape[0]
    padded = jnp.concatenate([filter_taps, jnp.zeros_like(filter_taps)])
    repeated = jnp.tile(padded, count)[: count * (2 * count - 1)]
    upper = repeated.reshape(count, 2 * count - 1)[:, :count]
    matrix = upper.T + jnp.eye(count, dtype=filter_taps.dtype)
    return matrix.astype(jnp.bfloat16)


def body(design, filter_taps, probes, lower_bound, upper_bound):
    row_count = lax.axis_size("row")
    col_count = lax.axis_size("col")
    fold_ratio = row_count // col_count
    row_index = lax.axis_index("row")
    panel_width = design.shape[1]
    row_width = panel_width // fold_ratio
    filter_matrix = whitening(filter_taps)
    whole_panel = lax.all_gather(design, "row", axis=0, tiled=True)
    white = jnp.dot(filter_matrix, whole_panel, preferred_element_type=jnp.float32).astype(
        jnp.bfloat16
    )
    own_slice = lax.dynamic_slice_in_dim(white, row_index % fold_ratio * row_width, row_width, 1)
    panel = broadcast(own_slice, "col", row_index // fold_ratio)
    normal_tile = lax.dot_general(
        panel, white, (((0,), (0,)), ((), ())), preferred_element_type=jnp.float32
    )
    panel_wide = panel.astype(jnp.float32)
    jacobi = (jnp.sum(jnp.square(panel_wide), axis=0) + 1e-06)[:, None]
    center_value = (lower_bound[0] + upper_bound[0]) / 2.0
    half_width = (upper_bound[0] - lower_bound[0]) / 2.0
    sigma_value = center_value / half_width
    weight_now = 1.0 / sigma_value
    residual = probes
    direction = residual / jacobi / center_value
    solution = jnp.zeros_like(residual)
    for sweep_index in range(SWEEPS):
        solution = solution + direction
        image_part = jnp.dot(panel_wide, direction, precision=lax.Precision.HIGHEST)
        image = lax.psum(image_part, "row")
        applied = lax.dot_general(
            panel_wide, image, (((0,), (0,)), ((), ())), precision=lax.Precision.HIGHEST
        )
        residual = residual - applied
        weight_next = 1.0 / (2.0 * sigma_value - weight_now)
        direction = weight_next * weight_now * direction + 2.0 * weight_next / half_width * (
            residual / jacobi
        )
        weight_now = weight_next
    solution = solution + direction
    return (normal_tile, solution)


def solution(mesh):
    placed = (P("row", "col"), P(), P("row", "col"), P(), P())
    return jax.shard_map(
        body,
        mesh=mesh,
        in_specs=placed,
        out_specs=(P("row", "col"), P("row", "col")),
        check_vma=False,
    )
```

profile of v0, /device:TPU:0, one launch (start us, length us, event | category | flops | bytes accessed | tf_op | source)
XLA Modules:
  0.0 242.3 jit_solution(15138177019820557356)
XLA Ops:
  7.2 0.0 all-gather.2.cloned.1.call-start
  7.2 0.7 all-gather.2.cloned.1.call-update
  7.9 0.0 all-reduce.3.cloned.1.call-start
  8.0 0.7 concatenate.3
  8.7 0.1 broadcast_bitcast_fusion
  8.7 0.1 copy.7
  8.9 1.2 reshape.17
  10.0 63.3 %all-gather.2.cloned.1.call-done = bf16[256,6144]{1,0:T(8,128)(2,1)} async-done(((bf16[32,6144]{1,0:T(8,128)(2,1)}), bf16[256,6144]{1,0:T(8,128)(2,1)}) %all-gather.2.cloned.1.call-update) | async-done | bytes 3145744 | tf_op jit(solution)/shard_map/all_gather | solution.py:31
  73.4 3.0 %convolution_convert_fusion = bf16[256,6144]{1,0:T(8,128)(2,1)S(1)} fusion(bf16[256,6144]{1,0:T(8,128)(2,1)} %all-gather.2.cloned.1.call-done, f32[256,511]{1,0:T(8,128)} %reshape.17), kind=kOutput, calls=%fused_computation | convolution fusion | flops 807141376 | bytes 6553600 | tf_op jit(solution)/shard_map/dot_general | solution.py:32
  76.4 1.5 dynamic-slice_select_fusion
  77.8 0.0 copy-start.2
  77.8 0.0 all-reduce.3.cloned.1.call-update
  79.5 40.0 %all-reduce.3.cloned.1.call-done = bf16[256,3072]{1,0:T(8,128)(2,1)} async-done(((bf16[256,3072]{1,0:T(8,128)(2,1)}), bf16[256,3072]{1,0:T(8,128)(2,1)}) %all-reduce.3.cloned.1.call-update) | async-done | bytes 1572880 | tf_op jit(solution)/shard_map/psum | solution.py:11
  119.5 0.0 copy-start
  119.5 1.9 multiply_reduce_fusion
  121.4 0.0 copy-start.6
  121.4 0.6 copy-done.6
  122.0 0.0 copy-done.2
  122.0 0.0 copy-done
  122.0 2.0 fusion.11
  124.0 0.0 copy-start.7
  124.0 39.0 %psum.22 = f32[256,32]{1,0:T(8,128)S(1)} all-reduce(f32[256,32]{1,0:T(8,128)} %fusion.11), channel_id=1, replica_groups=mesh['row'=8,'col'=4] {'row'}, use_global_device_ids=true, to_apply=%region_2.3 | all-reduce | flops 8192 | bytes 65536 | tf_op jit(solution)/shard_map/psum | solution.py:52
  163.0 0.0 copy-start.1
  163.0 0.0 copy-start.3
  163.1 2.5 %convolution_subtract_fusion.1 = f32[3072,32]{0,1:T(8,128)S(1)} fusion(f32[3072,32]{0,1:T(8,128)} %param.7, bf16[256,3072]{1,0:T(8,128)(2,1)} %all-reduce.3.cloned.1.call-done, f32[256,32]{1,0:T(8,128)S(1)} %psum.22), kind=kOutput, calls=%fused_computation.2 | convolution fusion | flops 302088192 | bytes 2392064 | tf_op jit(solution)/shard_map/dot_general | solution.py:53
  165.6 0.0 copy-start.5
  165.6 0.7 copy-done.5
  166.4 0.0 copy-done.7
  166.4 0.0 copy-done.1
  166.4 0.0 copy-done.3
  166.4 1.4 fusion.4
  167.8 34.8 %psum.23 = f32[256,32]{1,0:T(8,128)} all-reduce(f32[256,32]{1,0:T(8,128)S(1)} %fusion.4), channel_id=1, replica_groups=mesh['row'=8,'col'=4] {'row'}, use_global_device_ids=true, to_apply=%region_3.4 | all-reduce | flops 8192 | bytes 65536 | tf_op jit(solution)/shard_map/psum | solution.py:52
  202.6 0.0 copy-start.4
  202.6 29.7 %fusion.12 = f32[3072,6144]{1,0:T(8,128)} fusion(bf16[256,3072]{1,0:T(8,128)(2,1)} %all-reduce.3.cloned.1.call-done, bf16[256,6144]{1,0:T(8,128)(2,1)S(1)} %convolution_convert_fusion), kind=kOutput, calls=%fused_computation.23 | convolution fusion | flops 9663676416 | bytes 80216064 | tf_op jit(solution)/shard_map/dot_general | solution.py:37
  232.3 0.0 copy-done.4
  232.3 3.2 %fusion.3 = f32[3072,32]{0,1:T(8,128)} fusion(f32[3072,32]{0,1:T(8,128)} %copy-done.5, bf16[256,3072]{1,0:T(8,128)(2,1)} %all-reduce.3.cloned.1.call-done, f32[256,32]{1,0:T(8,128)} %psum.23, f32[]{:T(128)S(6)} %div.79, f32[]{:T(128)S(6)} %mul.51, f32[3072]{0:T(1024)S(1)} %get-tuple-element.2, f32[]{:T(128)S(6)} %div.75, f32[]{:T(128)S(6)} %mul.45, ...), kind=kOutput, calls=%fused_computation.6 | convolution fusion | flops 303169536 | bytes 2809872 | tf_op jit(solution)/shard_map/dot_general | solution.py:53
  (1 shorter events, 0.0 us)
Async XLA Ops:
  7.2 66.2 %all-gather.2.cloned.1.call-start = ((), (), s32[]{:S(2)}) async-start(), calls=%async_computation | async-start | bytes 3538944 | tf_op jit(solution)/shard_map/all_gather | solution.py:31
  7.9 111.6 %all-reduce.3.cloned.1.call-start = ((), (), s32[]{:S(2)}) async-start(), calls=%async_computation.1 | async-start | bytes 3145728 | tf_op jit(solution)/shard_map/psum | solution.py:11
  77.8 44.1 %copy-start.2 = (f32[3072,32]{0,1:T(8,128)S(1)}, f32[3072,32]{0,1:T(8,128)}, u32[]{:S(2)}) copy-start(f32[3072,32]{0,1:T(8,128)} %param.7) | copy-start | bytes 1179652
  119.5 2.5 %copy-start = (bf16[256,3072]{1,0:T(8,128)(2,1)S(1)}, bf16[256,3072]{1,0:T(8,128)(2,1)}, u32[]{:S(2)}) copy-start(bf16[256,3072]{1,0:T(8,128)(2,1)} %all-reduce.3.cloned.1.call-done) | copy-start | bytes 4718596
  121.4 0.6 copy-start.6
  124.0 42.4 %copy-start.7 = (f32[3072]{0:T(1024)S(1)}, f32[3072]{0:T(1024)}, u32[]{:S(2)}) copy-start(f32[3072]{0:T(1024)} %copy-done.6) | copy-start | bytes 36868
  163.0 3.3 %copy-start.1 = (bf16[256,3072]{1,0:T(8,128)(2,1)S(1)}, bf16[256,3072]{1,0:T(8,128)(2,1)}, u32[]{:S(2)}) copy-start(bf16[256,3072]{1,0:T(8,128)(2,1)} %all-reduce.3.cloned.1.call-done) | copy-start | bytes 4718596
  163.0 3.3 %copy-start.3 = (f32[3072,32]{0,1:T(8,128)S(1)}, f32[3072,32]{0,1:T(8,128)}, u32[]{:S(2)}) copy-start(f32[3072,32]{0,1:T(8,128)} %param.7) | copy-start | bytes 1179652
  165.6 0.7 copy-start.5
  202.6 29.7 %copy-start.4 = (f32[3072,32]{0,1:T(8,128)S(1)}, f32[3072,32]{0,1:T(8,128)}, u32[]{:S(2)}) copy-start(f32[3072,32]{0,1:T(8,128)} %param.7) | copy-start | bytes 1179652
Sparse Core Ops, SparseCore 0:
  10.2 63.1 all-gather.1
  78.0 41.4 all-reduce.2
where the time goes:
time: 243 us; the launch traced here: 242 us
  waiting for transfers between devices  104 us (43%)
  blocking collectives  73.8 us (30%)
  matrix products  41.9 us (17%)
  between operations  15.8 us (7%)
  local copies, waits for them, and re-layouts  3.41 us (1%)
  other arithmetic  3.33 us (1%)
    psum x2, blocking collectives, body(): image = lax.psum(image_part, 'row')  73.8 us
    all_gather x1, waiting for transfers between devices, body(): whole_panel = lax.all_gather(design, 'row', axis=0, tiled=True)  63.3 us
    psum x1, waiting for transfers between devices, broadcast(): return lax.psum(block, axis)  40 us
    dot_general x1, matrix products, body(): lax.dot_general(panel, white, (((0,), (0,)), ((), ())), preferred_element...  29.7 us
    dot_general x2, matrix products, body(): lax.dot_general(panel_wide, image, (((0,), (0,)), ((), ())), precision=la...  5.78 us
  transfers between devices with their start and end apart: 2, of which 2 were waited for; matrix products, arithmetic and copies ran while one was open for 1% of the time, Pallas kernels for 0%

commit v1 on v0

--- a/solution.py
+++ b/solution.py
@@ -4,11 +4,6 @@
 from jax.sharding import PartitionSpec as P
 
 SWEEPS = 2
-
-
-def broadcast(block, axis, owner):
-    block = jnp.where(lax.axis_index(axis) == owner, block, jnp.zeros_like(block))
-    return lax.psum(block, axis)
 
 
 def whitening(filter_taps):
@@ -18,6 +13,45 @@
     upper = repeated.reshape(count, 2 * count - 1)[:, :count]
     matrix = upper.T + jnp.eye(count, dtype=filter_taps.dtype)
     return matrix.astype(jnp.bfloat16)
+
+
+def is_power_of_two(count):
+    return count > 0 and count & (count - 1) == 0
+
+
+def swap(block, axis, count, bit):
+    return lax.ppermute(block, axis, [(i, i ^ bit) for i in range(count)])
+
+
+def tree_sum(block, axis):
+    count = lax.axis_size(axis)
+    if not is_power_of_two(count):
+        return lax.psum(block, axis)
+    bit = 1
+    while bit < count:
+        block = block + swap(block, axis, count, bit)
+        bit *= 2
+    return block
+
+
+def tree_broadcast(block, axis, owner):
+    count = lax.axis_size(axis)
+    offset = lax.axis_index(axis) ^ owner
+    if not is_power_of_two(count):
+        block = jnp.where(offset == 0, block, jnp.zeros_like(block))
+        return lax.psum(block, axis)
+    bit = 1
+    while bit < count:
+        arrived = swap(block, axis, count, bit)
+        block = jnp.where(offset // bit == 1, arrived, block)
+        bit *= 2
+    return block
+
+
+def contract_epochs(left, right):
+    return lax.dot_general(
+        left, right, (((0,), (0,)), ((), ())), precision=lax.Precision.HIGHEST
+    )
 
 
 def body(design, filter_taps, probes, lower_bound, upper_bound):
@@ -33,10 +67,16 @@
         jnp.bfloat16
     )
     own_slice = lax.dynamic_slice_in_dim(white, row_index % fold_ratio * row_width, row_width, 1)
-    panel = broadcast(own_slice, "col", row_index // fold_ratio)
+    panel = tree_broadcast(own_slice, "col", row_index // fold_ratio)
     normal_tile = lax.dot_general(
         panel, white, (((0,), (0,)), ((), ())), preferred_element_type=jnp.float32
     )
+    white_wide = white.astype(jnp.float32)
+    panel_jacobi = jnp.sum(jnp.square(white_wide), axis=0) + 1e-06
+    coupling = jnp.dot(
+        white_wide / panel_jacobi[None, :], white_wide.T, precision=lax.Precision.HIGHEST
+    )
+    coupling = tree_sum(coupling, "col")
     panel_wide = panel.astype(jnp.float32)
     jacobi = (jnp.sum(jnp.square(panel_wide), axis=0) + 1e-06)[:, None]
     center_value = (lower_bound[0] + upper_bound[0]) / 2.0
@@ -44,20 +84,23 @@
     sigma_value = center_value / half_width
     weight_now = 1.0 / sigma_value
     residual = probes
-    direction = residual / jacobi / center_value
+    scaled = residual / jacobi
+    direction = scaled / center_value
+    scaled_image = tree_sum(jnp.dot(panel_wide, scaled, precision=lax.Precision.HIGHEST), "row")
+    image = scaled_image / center_value
     solution = jnp.zeros_like(residual)
     for sweep_index in range(SWEEPS):
         solution = solution + direction
-        image_part = jnp.dot(panel_wide, direction, precision=lax.Precision.HIGHEST)
-        image = lax.psum(image_part, "row")
-        applied = lax.dot_general(
-            panel_wide, image, (((0,), (0,)), ((), ())), precision=lax.Precision.HIGHEST
-        )
-        residual = residual - applied
+        residual = residual - contract_epochs(panel_wide, image)
         weight_next = 1.0 / (2.0 * sigma_value - weight_now)
         direction = weight_next * weight_now * direction + 2.0 * weight_next / half_width * (
             residual / jacobi
         )
+        if sweep_index + 1 < SWEEPS:
+            scaled_image = scaled_image - jnp.dot(
+                coupling, image, precision=lax.Precision.HIGHEST
+            )
+            image = weight_next * weight_now * image + 2.0 * weight_next / half_width * scaled_image
         weight_now = weight_next
     solution = solution + direction
     return (normal_tile, solution)

time: 243 us -> 179 us (0.74)
  blocking collectives: 73.8 us -> 0 us
  starting transfers between devices: 0.08 us -> 7.01 us
    psum x2 -> x0, blocking collectives: 73.8 us -> none  [body(): image = lax.psum(image_part, 'row')]
    psum x1 -> x0, waiting for transfers between devices: 40 us -> none  [broadcast(): return lax.psum(block, axis)]
    ppermute x0 -> x7, waiting for transfers between devices: none -> 37.9 us  [swap(): return lax.ppermute(block, axis, [(i, i ^ bit) for i in range(count)])]
    ppermute x0 -> x7, starting transfers between devices: none -> 6.98 us  [swap(): return lax.ppermute(block, axis, [(i, i ^ bit) for i in range(count)])]
    dot_general x4 -> x5, matrix products: 9.21 us -> 11.6 us  [the longest x2 5.45 us: contract_epochs(): lax.dot_general(left, right, (((0,), (0,)), ((), ())), precision=lax.Prec...]
  transfers between devices with their start and end apart: 2 -> 8, of which waited for: 2 -> 4; matrix products, arithmetic and copies ran while one was open for 1% -> 24% of each run, Pallas kernels for 0% -> 0%
where the time goes in v1:
time: 179 us; the launch traced here: 178 us
  waiting for transfers between devices  102 us (57%)
  matrix products  44.2 us (25%)
  between operations  15.7 us (9%)
  starting transfers between devices  7.01 us (4%)
  other arithmetic  4.85 us (3%)
  local copies, waits for them, and re-layouts  4.49 us (3%)
    all_gather x1, waiting for transfers between devices, body(): whole_panel = lax.all_gather(design, 'row', axis=0, tiled=True)  63.4 us
    ppermute x7, waiting for transfers between devices, swap(): return lax.ppermute(block, axis, [(i, i ^ bit) for i in range(count)])  37.9 us
    dot_general x1, matrix products, body(): lax.dot_general(panel, white, (((0,), (0,)), ((), ())), preferred_element...  29.7 us
    ppermute x7, starting transfers between devices, swap(): return lax.ppermute(block, axis, [(i, i ^ bit) for i in range(count)])  6.98 us
    dot_general x2, matrix products, contract_epochs(): lax.dot_general(left, right, (((0,), (0,)), ((), ())), precision=lax.Prec...  5.45 us
  transfers between devices with their start and end apart: 8, of which 4 were waited for; matrix products, arithmetic and copies ran while one was open for 24% of the time, Pallas kernels for 0%

profile of v1, /device:TPU:0, one launch (start us, length us, event | category | flops | bytes accessed | tf_op | source)
XLA Modules:
  0.0 178.2 jit_solution(16239373397497172336)
XLA Ops:
  7.2 0.0 all-gather.2.cloned.1.call-start
  7.2 0.7 all-gather.2.cloned.1.call-update
  7.9 0.7 concatenate.3
  8.6 0.1 broadcast_bitcast_fusion
  8.7 0.1 copy.7
  8.8 1.2 reshape.20
  10.0 63.4 %all-gather.2.cloned.1.call-done = bf16[256,6144]{1,0:T(8,128)(2,1)} async-done(((bf16[32,6144]{1,0:T(8,128)(2,1)}), bf16[256,6144]{1,0:T(8,128)(2,1)}) %all-gather.2.cloned.1.call-update) | async-done | bytes 3145744 | tf_op jit(solution)/shard_map/all_gather | solution.py:65
  73.4 3.0 %fusion.1 = (f32[6144]{0:T(1024)S(1)}, bf16[256,6144]{1,0:T(8,128)(2,1)S(1)}) fusion(bf16[256,6144]{1,0:T(8,128)(2,1)} %all-gather.2.cloned.1.call-done, f32[256,511]{1,0:T(8,128)} %reshape.20), kind=kOutput, calls=%fused_computation.4 | convolution fusion | flops 811853824 | bytes 6578176 | tf_op jit(solution)/shard_map/dot_general | solution.py:66
  76.4 1.3 constant_dynamic-slice_fusion
  77.7 0.0 collective-permute-start
  77.7 3.7 %collective-permute-done = bf16[256,3072]{1,0:T(8,128)(2,1)} collective-permute-done((bf16[256,3072]{1,0:T(8,128)(2,1)}, bf16[256,3072]{1,0:T(8,128)(2,1)}, u32[]{:S(2)}, u32[]{:S(2)}) %collective-permute-start) | collective-permute-done | bytes 1572896 | tf_op jit(solution)/shard_map/ppermute | solution.py:23
  81.4 1.7 broadcast_select_fusion
  83.2 1.5 collective-permute-start.1
  86.0 3.4 %fusion = f32[256,256]{1,0:T(8,128)S(1)} fusion(bf16[256,6144]{1,0:T(8,128)(2,1)S(1)} %get-tuple-element.7, f32[6144]{0:T(1024)S(1)} %broadcast_add_fusion), kind=kOutput, calls=%fused_computation.2 | convolution fusion | flops 4834983936 | bytes 3432448 | tf_op jit(solution)/shard_map/dot_general | solution.py:76
  89.3 0.0 copy-start.2
  89.3 0.0 copy-start.1
  89.4 0.1 collective-permute-start.5
  89.5 30.7 %collective-permute-done.1 = bf16[256,3072]{1,0:T(8,128)(2,1)} collective-permute-done((bf16[256,3072]{1,0:T(8,128)(2,1)}, bf16[256,3072]{1,0:T(8,128)(2,1)}, u32[]{:S(2)}, u32[]{:S(2)}) %collective-permute-start.1) | collective-permute-done | bytes 1572896 | tf_op jit(solution)/shard_map/ppermute | solution.py:23
  120.2 2.0 %multiply_reduce_fusion = (f32[3072]{0:T(1024)S(1)}, bf16[256,3072]{1,0:T(8,128)(2,1)S(1)}) fusion(bf16[256,3072]{1,0:T(8,128)(2,1)} %collective-permute-done.1, bf16[256,3072]{1,0:T(8,128)(2,1)} %broadcast_select_fusion, pred[]{:T(512)S(6)} %eq.11), kind=kLoop, calls=%fused_computation.12 | loop fusion | flops 3142656 | bytes 4730881 | tf_op jit(solution)/shard_map/reduce_sum | solution.py:81
  122.3 0.0 copy-start
  122.3 1.1 copy-done
  123.4 0.0 copy-done.1
  123.4 1.4 fusion.8
  124.9 0.0 copy-done.2
  124.9 0.6 collective-permute-start.2
  125.5 3.4 %collective-permute-done.2 = f32[256,32]{0,1:T(8,128)S(1)} collective-permute-done((f32[256,32]{0,1:T(8,128)S(1)}, f32[256,32]{0,1:T(8,128)S(1)}, u32[]{:S(2)}, u32[]{:S(2)}) %collective-permute-start.2) | collective-permute-done | bytes 32800 | tf_op jit(solution)/shard_map/ppermute | solution.py:23
  128.9 1.1 collective-permute-start.3
  130.2 0.0 collective-permute-done.5
  130.2 1.1 add.82
  131.3 1.5 collective-permute-start.6
  132.8 0.0 collective-permute-done.3
  132.9 2.1 %collective-permute-start.4 = (f32[256,32]{0,1:T(8,128)S(1)}, f32[256,32]{0,1:T(8,128)S(1)}, u32[]{:S(2)}, u32[]{:S(2)}) collective-permute-start(f32[256,32]{0,1:T(8,128)S(1)} %add.76), channel_id=1, source_target_pairs={{0,16},{4,20},{8,24},{12,28},{16,0},{20,4},{24,8},{28,12},{1,17},{... | collective-permute-start | bytes 98312 | tf_op jit(solution)/shard_map/ppermute | solution.py:23
  134.9 29.7 %fusion.18 = f32[3072,6144]{1,0:T(8,128)} fusion(bf16[256,3072]{1,0:T(8,128)(2,1)} %copy-done, bf16[256,6144]{1,0:T(8,128)(2,1)S(1)} %get-tuple-element.7), kind=kOutput, calls=%fused_computation.34 | convolution fusion | flops 9663676416 | bytes 80216064 | tf_op jit(solution)/shard_map/dot_general | solution.py:71
  164.6 0.0 collective-permute-done.4
  164.6 2.3 %convolution_subtract_fusion.1 = f32[3072,32]{0,1:T(8,128)S(1)} fusion(f32[3072,32]{0,1:T(8,128)} %param.7, bf16[256,3072]{1,0:T(8,128)(2,1)} %copy-done, f32[]{:T(128)} %bitcast.1, f32[256,32]{0,1:T(8,128)S(1)} %add.76, f32[256,32]{0,1:T(8,128)S(1)} %collective-permute-done.4), kind=kOutput, calls=%fused_computation.6 | convolution fusion | flops 302104576 | bytes 2424836 | tf_op jit(solution)/shard_map/dot_general | solution.py:52
  166.9 0.0 collective-permute-done.6
  167.0 1.3 fusion.7
  168.3 3.1 %fusion.5 = f32[3072,32]{0,1:T(8,128)} fusion(f32[3072,32]{0,1:T(8,128)S(1)} %convolution_subtract_fusion.1, bf16[256,3072]{1,0:T(8,128)(2,1)} %copy-done, f32[3072,32]{0,1:T(8,128)} %param.7, f32[]{:T(128)S(6)} %div.110, f32[]{:T(128)S(6)} %mul.65, f32[3072]{0:T(1024)S(1)} %get-tuple-element.5, f32[]{:T(128)S(6)} %div.103, f32[]{:T(128)S(6)} %mul.59, ...), kind=kOutput, calls=%fused_computation.10 | convolution fusion | flops 303202304 | bytes 2875412 | tf_op jit(solution)/shard_map/dot_general | solution.py:52
  (4 shorter events, 0.0 us)
Async XLA Ops:
  7.2 66.2 %all-gather.2.cloned.1.call-start = ((), (), s32[]{:S(2)}) async-start(), calls=%async_computation | async-start | bytes 3538944 | tf_op jit(solution)/shard_map/all_gather | solution.py:65
  77.7 3.8 %collective-permute-start = (bf16[256,3072]{1,0:T(8,128)(2,1)}, bf16[256,3072]{1,0:T(8,128)(2,1)}, u32[]{:S(2)}, u32[]{:S(2)}) collective-permute-start(bf16[256,3072]{1,0:T(8,128)(2,1)} %constant_dynamic-slice_fusion), channel_id=1, source_target_pairs={{0,1},{1,0},{2,3},{3,2},{4,5},{5,4},{6,7},{7,6},{8,9},{9,8},{10,11... | collective-permute-start | bytes 4718600 | tf_op jit(solution)/shard_map/ppermute | solution.py:23
  83.2 37.1 %collective-permute-start.1 = (bf16[256,3072]{1,0:T(8,128)(2,1)}, bf16[256,3072]{1,0:T(8,128)(2,1)}, u32[]{:S(2)}, u32[]{:S(2)}) collective-permute-start(bf16[256,3072]{1,0:T(8,128)(2,1)} %broadcast_select_fusion), channel_id=1, source_target_pairs={{0,2},{1,3},{2,0},{3,1},{4,6},{5,7},{6,4},{7,5},{8,10},{9,11},{10,... | collective-permute-start | bytes 4718600 | tf_op jit(solution)/shard_map/ppermute | solution.py:23
  89.3 35.5 %copy-start.2 = (f32[256,256]{1,0:T(8,128)}, f32[256,256]{1,0:T(8,128)S(1)}, u32[]{:S(2)}) copy-start(f32[256,256]{1,0:T(8,128)S(1)} %fusion) | copy-start | bytes 786436
  89.3 34.1 %copy-start.1 = (f32[3072,32]{0,1:T(8,128)S(1)}, f32[3072,32]{0,1:T(8,128)}, u32[]{:S(2)}) copy-start(f32[3072,32]{0,1:T(8,128)} %param.7) | copy-start | bytes 1179652
  89.4 40.9 %collective-permute-start.5 = (f32[256,256]{1,0:T(8,128)S(1)}, f32[256,256]{1,0:T(8,128)}, u32[]{:S(2)}, u32[]{:S(2)}) collective-permute-start(f32[256,256]{1,0:T(8,128)S(1)} %fusion), channel_id=1, source_target_pairs={{0,1},{1,0},{2,3},{3,2},{4,5},{5,4},{6,7},{7,6},{8,9},{9,8},{10,11... | collective-permute-start | bytes 786440 | tf_op jit(solution)/shard_map/ppermute | solution.py:23
  122.3 1.2 copy-start
  124.9 4.0 %collective-permute-start.2 = (f32[256,32]{0,1:T(8,128)S(1)}, f32[256,32]{0,1:T(8,128)S(1)}, u32[]{:S(2)}, u32[]{:S(2)}) collective-permute-start(f32[256,32]{0,1:T(8,128)S(1)} %fusion.8), channel_id=1, source_target_pairs={{0,4},{4,0},{8,12},{12,8},{16,20},{20,16},{24,28},{28,24},{1,5},{5... | collective-permute-start | bytes 98312 | tf_op jit(solution)/shard_map/ppermute | solution.py:23
  128.9 4.0 %collective-permute-start.3 = (f32[256,32]{0,1:T(8,128)S(1)}, f32[256,32]{0,1:T(8,128)S(1)}, u32[]{:S(2)}, u32[]{:S(2)}) collective-permute-start(f32[256,32]{0,1:T(8,128)S(1)} %add.75), channel_id=1, source_target_pairs={{0,8},{4,12},{8,0},{12,4},{16,24},{20,28},{24,16},{28,20},{1,9},{5... | collective-permute-start | bytes 98312 | tf_op jit(solution)/shard_map/ppermute | solution.py:23
  131.3 35.6 %collective-permute-start.6 = (f32[256,256]{1,0:T(8,128)S(1)}, f32[256,256]{1,0:T(8,128)}, u32[]{:S(2)}, u32[]{:S(2)}) collective-permute-start(f32[256,256]{1,0:T(8,128)S(1)} %add.82), channel_id=1, source_target_pairs={{0,2},{1,3},{2,0},{3,1},{4,6},{5,7},{6,4},{7,5},{8,10},{9,11},{10,... | collective-permute-start | bytes 786440 | tf_op jit(solution)/shard_map/ppermute | solution.py:23
  132.9 31.7 %collective-permute-start.4 = (f32[256,32]{0,1:T(8,128)S(1)}, f32[256,32]{0,1:T(8,128)S(1)}, u32[]{:S(2)}, u32[]{:S(2)}) collective-permute-start(f32[256,32]{0,1:T(8,128)S(1)} %add.76), channel_id=1, source_target_pairs={{0,16},{4,20},{8,24},{12,28},{16,0},{20,4},{24,8},{28,12},{1,17},{... | collective-permute-start | bytes 98312 | tf_op jit(solution)/shard_map/ppermute | solution.py:23
Sparse Core Ops, SparseCore 0:
  10.2 63.1 all-gather.1

commit v2 on v1

--- a/solution.py
+++ b/solution.py
@@ -34,17 +34,27 @@
     return block
 
 
-def tree_broadcast(block, axis, owner):
-    count = lax.axis_size(axis)
-    offset = lax.axis_index(axis) ^ owner
-    if not is_power_of_two(count):
+def tree_broadcast(block, fold_ratio):
+    row_count = lax.axis_size("row")
+    col_count = lax.axis_size("col")
+    owner = lax.axis_index("row") // fold_ratio
+    offset = lax.axis_index("col") ^ owner
+    if not is_power_of_two(col_count):
         block = jnp.where(offset == 0, block, jnp.zeros_like(block))
-        return lax.psum(block, axis)
-    bit = 1
-    while bit < count:
-        arrived = swap(block, axis, count, bit)
-        block = jnp.where(offset // bit == 1, arrived, block)
-        bit *= 2
+        return lax.psum(block, "col")
+    bits = [1 << k for k in range(1, col_count.bit_length() - 1)] + [1][: col_count > 1]
+    done = 0
+    for bit in bits:
+        pairs = []
+        for row in range(row_count):
+            base = row * col_count
+            row_owner = row // fold_ratio
+            for held in range(col_count):
+                if (held ^ row_owner) & ~done == 0:
+                    pairs.append((base + held, base + (held ^ bit)))
+        arrived = lax.ppermute(block, ("row", "col"), pairs)
+        done |= bit
+        block = jnp.where((offset & ~done == 0) & (offset & bit != 0), arrived, block)
     return block
 
 
@@ -62,12 +72,29 @@
     panel_width = design.shape[1]
     row_width = panel_width // fold_ratio
     filter_matrix = whitening(filter_taps)
-    whole_panel = lax.all_gather(design, "row", axis=0, tiled=True)
-    white = jnp.dot(filter_matrix, whole_panel, preferred_element_type=jnp.float32).astype(
-        jnp.bfloat16
-    )
-    own_slice = lax.dynamic_slice_in_dim(white, row_index % fold_ratio * row_width, row_width, 1)
-    panel = tree_broadcast(own_slice, "col", row_index // fold_ratio)
+
+    epoch_block = design.shape[0]
+    epochs = epoch_block * row_count
+    part_width = row_width // 2
+    slices = design.reshape(epoch_block, fold_ratio, row_width)
+    owned = row_index % fold_ratio
+    gathered = []
+    for part_index in range(2):
+        part = slices[:, :, part_index * part_width : (part_index + 1) * part_width]
+        part = part.reshape(epoch_block, fold_ratio * part_width)
+        gathered.append(lax.all_gather(part, "row", axis=0, tiled=True))
+    parts, panel_parts = [], []
+    for part_index in range(2):
+        whole = gathered[part_index]
+        if panel_parts:
+            whole, panel_parts[-1] = lax.optimization_barrier((whole, panel_parts[-1]))
+        part = jnp.dot(filter_matrix, whole, preferred_element_type=jnp.float32)
+        part = part.astype(jnp.bfloat16).reshape(epochs, fold_ratio, part_width)
+        parts.append(part)
+        own_slice = lax.dynamic_index_in_dim(part, owned, 1, keepdims=False)
+        panel_parts.append(tree_broadcast(own_slice, fold_ratio))
+    white = jnp.stack(parts, axis=2).reshape(epochs, panel_width)
+    panel = jnp.concatenate(panel_parts, axis=1)
     normal_tile = lax.dot_general(
         panel, white, (((0,), (0,)), ((), ())), preferred_element_type=jnp.float32
     )

time: 179 us -> 192 us (1.073)
  local copies, waits for them, and re-layouts: 4.49 us -> 30.3 us
  waiting for transfers between devices: 102 us -> 81.1 us
  starting transfers between devices: 7.01 us -> 15.6 us
    ppermute x7 -> x5, waiting for transfers between devices: 37.9 us -> 3.37 us  [swap(): return lax.ppermute(block, axis, [(i, i ^ bit) for i in range(count)])]
    ppermute x0 -> x4, waiting for transfers between devices: none -> 17.5 us  [tree_broadcast(): arrived = lax.ppermute(block, ('row', 'col'), pairs)]
    ppermute x0 -> x4, starting transfers between devices: none -> 11.5 us  [tree_broadcast(): arrived = lax.ppermute(block, ('row', 'col'), pairs)]
    another operation x0 -> x4, local copies, waits for them, and re-layouts: none -> 10 us  [body(): white = jnp.stack(parts, axis=2).reshape(epochs, panel_width)]
    reshape x0 -> x3, local copies, waits for them, and re-layouts: none -> 8.34 us  [the longest x2 7.05 us: body(): part = part.astype(jnp.bfloat16).reshape(epochs, fold_ratio, part_width)]
    dynamic_slice x1 -> x2, local copies, waits for them, and re-layouts: 1.29 us -> 6.05 us  [body(): own_slice = lax.dynamic_index_in_dim(part, owned, 1, keepdims=False)]
    unnamed x8 -> x25, local copies, waits for them, and re-layouts: 1.33 us -> 5.21 us
    all_gather x1 -> x2, waiting for transfers between devices: 63.4 us -> 60.2 us  [body(): gathered.append(lax.all_gather(part, 'row', axis=0, tiled=True))]
  transfers between devices with their start and end apart: 8 -> 11, of which waited for: 4 -> 5; matrix products, arithmetic and copies ran while one was open for 24% -> 30% of each run, Pallas kernels for 0% -> 0%
where the time goes in v2:
time: 192 us; the launch traced here: 191 us
  waiting for transfers between devices  81.1 us (42%)
  matrix products  42.9 us (22%)
  local copies, waits for them, and re-layouts  30.3 us (16%)
  between operations  15.9 us (8%)
  starting transfers between devices  15.6 us (8%)
  other arithmetic  5.36 us (3%)
    all_gather x2, waiting for transfers between devices, body(): gathered.append(lax.all_gather(part, 'row', axis=0, tiled=True))  60.2 us
    dot_general x1, matrix products, body(): lax.dot_general(panel, white, (((0,), (0,)), ((), ())), preferred_element...  30.1 us
    ppermute x4, waiting for transfers between devices, tree_broadcast(): arrived = lax.ppermute(block, ('row', 'col'), pairs)  17.5 us
    ppermute x4, starting transfers between devices, tree_broadcast(): arrived = lax.ppermute(block, ('row', 'col'), pairs)  11.5 us
    another operation x4, local copies, waits for them, and re-layouts, body(): white = jnp.stack(parts, axis=2).reshape(epochs, panel_width)  10 us
    reshape x2, local copies, waits for them, and re-layouts, body(): part = part.astype(jnp.bfloat16).reshape(epochs, fold_ratio, part_width)  7.05 us
    dynamic_slice x2, local copies, waits for them, and re-layouts, body(): own_slice = lax.dynamic_index_in_dim(part, owned, 1, keepdims=False)  6.05 us
    dot_general x2, matrix products, body(): part = jnp.dot(filter_matrix, whole, preferred_element_type=jnp.float32)  5.25 us
  transfers between devices with their start and end apart: 11, of which 5 were waited for; matrix products, arithmetic and copies ran while one was open for 30% of the time, Pallas kernels for 0%

profile of v2, /device:TPU:0, one launch (start us, length us, event | category | flops | bytes accessed | tf_op | source)
XLA Modules:
  0.0 191.3 jit_solution(7840296608959321044)
XLA Ops:
  7.2 0.0 copy-start.6
  7.2 0.0 all-gather.5.cloned.1.call-start
  7.2 1.3 reshape.47
  8.5 0.3 fusion.21
  8.8 0.7 copy.19
  9.5 0.0 all-gather.5.cloned.1.call-update
  9.5 0.0 all-gather.3.cloned.1.call-start
  9.6 0.7 copy.17
  10.3 0.0 all-gather.3.cloned.1.call-update
  10.3 0.0 copy-done.6
  10.3 0.1 broadcast_bitcast_fusion
  10.4 0.1 copy.18
  10.5 0.4 reshape.49
  10.9 0.0 copy-start.5
  10.9 46.7 %all-gather.5.cloned.1.call-done = bf16[256,3072]{1,0:T(8,128)(2,1)} async-done(((bf16[32,3072]{1,0:T(8,128)(2,1)}), bf16[256,3072]{1,0:T(8,128)(2,1)}) %all-gather.5.cloned.1.call-update) | async-done | bytes 1572880 | tf_op jit(solution)/shard_map/all_gather | solution.py:85
  57.7 2.0 %convolution_convert_fusion.1 = bf16[256,3072]{1,0:T(8,128)(2,1)S(1)} fusion(bf16[256,3072]{1,0:T(8,128)(2,1)} %all-gather.5.cloned.1.call-done, f32[256,511]{1,0:T(8,128)S(1)} %reshape.49), kind=kOutput, calls=%fused_computation.5 | convolution fusion | flops 403701760 | bytes 3407872 | tf_op jit(solution)/shard_map/dot_general | solution.py:91
  59.7 0.0 copy-done.5
  59.7 2.1 %reshape.51 = bf16[256,2,1536]{2,1,0:T(2,128)(2,1)} reshape(bf16[256,3072]{1,0:T(8,128)(2,1)S(1)} %convolution_convert_fusion.1) | data formatting | bytes 3145728 | tf_op jit(solution)/shard_map/reshape | solution.py:92
  61.8 3.0 %constant_dynamic-slice_fusion.1 = bf16[256,1,1536]{2,1,0:T(2,128)(2,1)S(1)} fusion(bf16[256,2,1536]{2,1,0:T(2,128)(2,1)} %reshape.51, s32[]{:T(128)S(6)} %select_n.43), kind=kLoop, calls=%fused_computation.43 | loop fusion | bytes 1572868 | tf_op jit(solution)/shard_map/jit(dynamic_index_in_dim)/dynamic_slice | solution.py:94
  64.8 1.0 copy.29
  65.8 4.2 %collective-permute-start = (bf16[256,1536]{1,0:T(8,128)(2,1)}, bf16[256,1536]{1,0:T(8,128)(2,1)}, u32[]{:S(2)}, u32[]{:S(2)}) collective-permute-start(bf16[256,1536]{1,0:T(8,128)(2,1)} %bitcast.35), channel_id=1, source_target_pairs={{0,2},{4,6},{9,11},{13,15},{18,16},{22,20},{27,25},{31,29}} | collective-permute-start | bytes 2359304 | tf_op jit(solution)/shard_map/ppermute | solution.py:55
  70.0 8.9 %collective-permute-done = bf16[256,1536]{1,0:T(8,128)(2,1)} collective-permute-done((bf16[256,1536]{1,0:T(8,128)(2,1)}, bf16[256,1536]{1,0:T(8,128)(2,1)}, u32[]{:S(2)}, u32[]{:S(2)}) %collective-permute-start) | collective-permute-done | bytes 786464 | tf_op jit(solution)/shard_map/ppermute | solution.py:55
  78.9 1.0 broadcast_select_fusion.1
  80.0 2.2 %collective-permute-start.1 = (bf16[256,1536]{1,0:T(8,128)(2,1)}, bf16[256,1536]{1,0:T(8,128)(2,1)}, u32[]{:S(2)}, u32[]{:S(2)}) collective-permute-start(bf16[256,1536]{1,0:T(8,128)(2,1)} %broadcast_select_fusion.1), channel_id=1, source_target_pairs={{0,1},{2,3},{4,5},{6,7},{9,8},{11,10},{13,12},{15,14},{16,17},{18,... | collective-permute-start | bytes 2359304 | tf_op jit(solution)/shard_map/ppermute | solution.py:55
  83.4 2.1 %stack_reshape.6 = bf16[256,2,1,1536]{3,1,0,2:T(2,128)(2,1)} reshape(bf16[256,3072]{1,0:T(8,128)(2,1)S(1)} %convolution_convert_fusion.1) | data formatting | bytes 3145728 | tf_op jit(solution)/shard_map/stack;reshape | solution.py:96
  85.5 1.6 copy_dynamic-update-slice_fusion.1
  87.1 0.0 collective-permute-done.1
  87.1 2.1 %broadcast_select_fusion.3 = bf16[256,1536]{1,0:T(8,128)(2,1)} fusion(bf16[256,1536]{1,0:T(8,128)(2,1)} %collective-permute-done.1, bf16[256,1536]{1,0:T(8,128)(2,1)} %broadcast_select_fusion.1, pred[]{:T(512)S(6)} %and.40), kind=kLoop, calls=%fused_computation.25 | loop fusion | flops 393216 | bytes 2359297 | tf_op jit(solution)/shard_map/jit(_where)/select_n | solution.py:57
  89.2 13.5 %all-gather.3.cloned.1.call-done = bf16[256,3072]{1,0:T(8,128)(2,1)} async-done(((bf16[32,3072]{1,0:T(8,128)(2,1)}), bf16[256,3072]{1,0:T(8,128)(2,1)}) %all-gather.3.cloned.1.call-update) | async-done | bytes 1572880 | tf_op jit(solution)/shard_map/all_gather | solution.py:85
  102.7 3.2 %convolution_convert_fusion = bf16[256,3072]{1,0:T(8,128)(2,1)} fusion(bf16[256,3072]{1,0:T(8,128)(2,1)} %all-gather.3.cloned.1.call-done, f32[256,511]{1,0:T(8,128)} %copy-done.5), kind=kOutput, calls=%fused_computation.4 | convolution fusion | flops 403701760 | bytes 3407872 | tf_op jit(solution)/shard_map/dot_general | solution.py:91
  105.9 5.0 %stack_reshape.7 = bf16[256,2,1,1536]{3,1,0,2:T(2,128)(2,1)} reshape(bf16[256,3072]{1,0:T(8,128)(2,1)} %convolution_convert_fusion) | data formatting | bytes 3145728 | tf_op jit(solution)/shard_map/stack;reshape | solution.py:96
  110.9 5.0 %reshape.52 = bf16[256,2,1536]{2,1,0:T(2,128)(2,1)} reshape(bf16[256,3072]{1,0:T(8,128)(2,1)} %convolution_convert_fusion) | data formatting | bytes 3145728 | tf_op jit(solution)/shard_map/reshape | solution.py:92
  115.9 3.0 %constant_dynamic-slice_fusion = bf16[256,1,1536]{2,1,0:T(2,128)(2,1)S(1)} fusion(bf16[256,2,1536]{2,1,0:T(2,128)(2,1)} %reshape.52, s32[]{:T(128)S(6)} %select_n.43), kind=kLoop, calls=%fused_computation.42 | loop fusion | bytes 1572868 | tf_op jit(solution)/shard_map/jit(dynamic_index_in_dim)/dynamic_slice | solution.py:94
  119.0 0.1 copy.28
  119.1 3.6 %collective-permute-start.2 = (bf16[256,1536]{1,0:T(8,128)(2,1)S(1)}, bf16[256,1536]{1,0:T(8,128)(2,1)S(1)}, u32[]{:S(2)}, u32[]{:S(2)}) collective-permute-start(bf16[256,1536]{1,0:T(8,128)(2,1)S(1)} %bitcast.43), channel_id=1, source_target_pairs={{0,2},{4,6},{9,11},{13,15},{18,16},{22,20},{27,25},{31,29}} | collective-permute-start | bytes 2359304 | tf_op jit(solution)/shard_map/ppermute | solution.py:55
  122.7 0.0 copy-done.4
  122.7 0.2 copy_dynamic-update-slice_fusion
  122.8 0.7 fusion.1
  123.5 8.6 %collective-permute-done.2 = bf16[256,1536]{1,0:T(8,128)(2,1)S(1)} collective-permute-done((bf16[256,1536]{1,0:T(8,128)(2,1)S(1)}, bf16[256,1536]{1,0:T(8,128)(2,1)S(1)}, u32[]{:S(2)}, u32[]{:S(2)}) %collective-permute-start.2) | collective-permute-done | bytes 786464 | tf_op jit(solution)/shard_map/ppermute | solution.py:55
  132.1 0.1 broadcast_select_fusion
  132.2 1.6 collective-permute-start.3
  133.8 3.3 %fusion.7 = f32[256,256]{1,0:T(8,128)S(1)} fusion(bf16[256,2,2,1536]{3,0,2,1:T(8,128)(2,1)S(1)} %copy_dynamic-update-slice_fusion, f32[2,2,1536]{2,1,0:T(2,128)S(1)} %broadcast_add_fusion), kind=kOutput, calls=%fused_computation.17 | convolution fusion | flops 4834983936 | bytes 3432448 | tf_op jit(solution)/shard_map/dot_general | solution.py:103
  137.1 0.0 copy-start.7
  137.1 0.1 collective-permute-start.7
  137.2 0.0 collective-permute-done.3
  137.2 0.1 broadcast_select_fusion.2
  137.3 0.9 copy-done
  138.2 0.3 multiply_reduce_fusion
  138.6 1.4 fusion.9
  140.0 0.6 collective-permute-start.4
  140.6 3.4 %collective-permute-done.4 = f32[256,32]{0,1:T(8,128)S(1)} collective-permute-done((f32[256,32]{0,1:T(8,128)S(1)}, f32[256,32]{0,1:T(8,128)S(1)}, u32[]{:S(2)}, u32[]{:S(2)}) %collective-permute-start.4) | collective-permute-done | bytes 32800 | tf_op jit(solution)/shard_map/ppermute | solution.py:23
  144.0 0.0 collective-permute-start.5
  144.3 2.8 %copy.13 = bf16[256,2,2,1536]{0,3,2,1:T(8,128)(2,1)} copy(bf16[256,2,2,1536]{3,0,2,1:T(8,128)(2,1)S(1)} %copy_dynamic-update-slice_fusion) | data formatting | bytes 6291456 | tf_op jit(solution)/shard_map/stack | solution.py:96
  147.1 0.0 collective-permute-done.7
  147.1 1.0 add.82
  148.1 2.5 %collective-permute-start.8 = (f32[256,256]{1,0:T(8,128)S(1)}, f32[256,256]{1,0:T(8,128)S(1)}, u32[]{:S(2)}, u32[]{:S(2)}) collective-permute-start(f32[256,256]{1,0:T(8,128)S(1)} %add.82), channel_id=1, source_target_pairs={{0,2},{1,3},{2,0},{3,1},{4,6},{5,7},{6,4},{7,5},{8,10},{9,11},{10,... | collective-permute-start | bytes 786440 | tf_op jit(solution)/shard_map/ppermute | solution.py:23
  150.6 0.0 collective-permute-done.5
  150.6 0.8 collective-permute-start.6
  151.4 30.1 %fusion.20 = f32[3072,6144]{1,0:T(8,128)} fusion(bf16[256,6144]{0,1:T(8,128)(2,1)} %bitcast.37, bf16[256,1536]{1,0:T(8,128)(2,1)} %copy-done.2, bf16[256,1536]{1,0:T(8,128)(2,1)} %broadcast_select_fusion.3), kind=kOutput, calls=%fused_computation.44 | convolution fusion | flops 9666822144 | bytes 80216064 | tf_op jit(solution)/shard_map/dot_general | solution.py:98
  181.5 0.0 collective-permute-done.6
  181.5 0.9 convolution_subtract_fusion.1
  182.4 0.0 collective-permute-done.8
  182.4 0.4 fusion.8
  182.8 1.6 fusion.5
  (16 shorter events, 0.1 us)
Async XLA Ops:
  7.2 3.2 %copy-start.6 = (f32[256]{0:T(256)S(1)}, f32[256]{0:T(256)}, u32[]{:S(2)}) copy-start(f32[256]{0:T(256)} %param.6) | copy-start | bytes 3076
  7.2 50.5 %all-gather.5.cloned.1.call-start = ((), (), s32[]{:S(2)}) async-start(), calls=%async_computation.1 | async-start | bytes 1769472 | tf_op jit(solution)/shard_map/all_gather | solution.py:85
  9.5 93.2 %all-gather.3.cloned.1.call-start = ((), (), s32[]{:S(2)}) async-start(), calls=%async_computation | async-start | bytes 1769472 | tf_op jit(solution)/shard_map/all_gather | solution.py:85
  10.9 48.8 %copy-start.5 = (f32[256,511]{1,0:T(8,128)}, f32[256,511]{1,0:T(8,128)S(1)}, u32[]{:S(2)}) copy-start(f32[256,511]{1,0:T(8,128)S(1)} %reshape.49) | copy-start | bytes 1569796
  65.8 13.2 %collective-permute-start = (bf16[256,1536]{1,0:T(8,128)(2,1)}, bf16[256,1536]{1,0:T(8,128)(2,1)}, u32[]{:S(2)}, u32[]{:S(2)}) collective-permute-start(bf16[256,1536]{1,0:T(8,128)(2,1)} %bitcast.35), channel_id=1, source_target_pairs={{0,2},{4,6},{9,11},{13,15},{18,16},{22,20},{27,25},{31,29}} | collective-permute-start | bytes 2359304 | tf_op jit(solution)/shard_map/ppermute | solution.py:55
  80.0 7.1 %collective-permute-start.1 = (bf16[256,1536]{1,0:T(8,128)(2,1)}, bf16[256,1536]{1,0:T(8,128)(2,1)}, u32[]{:S(2)}, u32[]{:S(2)}) collective-permute-start(bf16[256,1536]{1,0:T(8,128)(2,1)} %broadcast_select_fusion.1), channel_id=1, source_target_pairs={{0,1},{2,3},{4,5},{6,7},{9,8},{11,10},{13,12},{15,14},{16,17},{18,... | collective-permute-start | bytes 2359304 | tf_op jit(solution)/shard_map/ppermute | solution.py:55
  119.0 3.7 %copy-start.4 = (bf16[256,2,1,1536]{3,1,0,2:T(2,128)(2,1)S(1)}, bf16[256,2,1,1536]{3,1,0,2:T(2,128)(2,1)}, u32[]{:S(2)}) copy-start(bf16[256,2,1,1536]{3,1,0,2:T(2,128)(2,1)} %stack_reshape.7) | copy-start | bytes 4718596
  119.1 13.0 %collective-permute-start.2 = (bf16[256,1536]{1,0:T(8,128)(2,1)S(1)}, bf16[256,1536]{1,0:T(8,128)(2,1)S(1)}, u32[]{:S(2)}, u32[]{:S(2)}) collective-permute-start(bf16[256,1536]{1,0:T(8,128)(2,1)S(1)} %bitcast.43), channel_id=1, source_target_pairs={{0,2},{4,6},{9,11},{13,15},{18,16},{22,20},{27,25},{31,29}} | collective-permute-start | bytes 2359304 | tf_op jit(solution)/shard_map/ppermute | solution.py:55
  132.2 5.0 %collective-permute-start.3 = (bf16[256,1536]{1,0:T(8,128)(2,1)S(1)}, bf16[256,1536]{1,0:T(8,128)(2,1)S(1)}, u32[]{:S(2)}, u32[]{:S(2)}) collective-permute-start(bf16[256,1536]{1,0:T(8,128)(2,1)S(1)} %broadcast_select_fusion), channel_id=1, source_target_pairs={{0,1},{2,3},{4,5},{6,7},{9,8},{11,10},{13,12},{15,14},{16,17},{18,... | collective-permute-start | bytes 2359304 | tf_op jit(solution)/shard_map/ppermute | solution.py:55
  137.1 1.1 copy-start
  137.1 1.5 copy-start.7
  137.1 10.0 %collective-permute-start.7 = (f32[256,256]{1,0:T(8,128)S(1)}, f32[256,256]{1,0:T(8,128)}, u32[]{:S(2)}, u32[]{:S(2)}) collective-permute-start(f32[256,256]{1,0:T(8,128)S(1)} %fusion.7), channel_id=1, source_target_pairs={{0,1},{1,0},{2,3},{3,2},{4,5},{5,4},{6,7},{7,6},{8,9},{9,8},{10,11... | collective-permute-start | bytes 786440 | tf_op jit(solution)/shard_map/ppermute | solution.py:23
  138.2 1.8 copy-start.2
  140.0 4.0 %collective-permute-start.4 = (f32[256,32]{0,1:T(8,128)S(1)}, f32[256,32]{0,1:T(8,128)S(1)}, u32[]{:S(2)}, u32[]{:S(2)}) collective-permute-start(f32[256,32]{0,1:T(8,128)S(1)} %fusion.9), channel_id=1, source_target_pairs={{0,4},{4,0},{8,12},{12,8},{16,20},{20,16},{24,28},{28,24},{1,5},{5... | collective-permute-start | bytes 98312 | tf_op jit(solution)/shard_map/ppermute | solution.py:23
  144.0 6.6 %collective-permute-start.5 = (f32[256,32]{0,1:T(8,128)S(1)}, f32[256,32]{0,1:T(8,128)S(1)}, u32[]{:S(2)}, u32[]{:S(2)}) collective-permute-start(f32[256,32]{0,1:T(8,128)S(1)} %add.75), channel_id=1, source_target_pairs={{0,8},{4,12},{8,0},{12,4},{16,24},{20,28},{24,16},{28,20},{1,9},{5... | collective-permute-start | bytes 98312 | tf_op jit(solution)/shard_map/ppermute | solution.py:23
  148.1 34.3 %collective-permute-start.8 = (f32[256,256]{1,0:T(8,128)S(1)}, f32[256,256]{1,0:T(8,128)S(1)}, u32[]{:S(2)}, u32[]{:S(2)}) collective-permute-start(f32[256,256]{1,0:T(8,128)S(1)} %add.82), channel_id=1, source_target_pairs={{0,2},{1,3},{2,0},{3,1},{4,6},{5,7},{6,4},{7,5},{8,10},{9,11},{10,... | collective-permute-start | bytes 786440 | tf_op jit(solution)/shard_map/ppermute | solution.py:23
  150.6 30.9 %collective-permute-start.6 = (f32[256,32]{0,1:T(8,128)S(1)}, f32[256,32]{0,1:T(8,128)S(1)}, u32[]{:S(2)}, u32[]{:S(2)}) collective-permute-start(f32[256,32]{0,1:T(8,128)S(1)} %add.76), channel_id=1, source_target_pairs={{0,16},{4,20},{8,24},{12,28},{16,0},{20,4},{24,8},{28,12},{1,17},{... | collective-permute-start | bytes 98312 | tf_op jit(solution)/shard_map/ppermute | solution.py:23
  151.4 30.1 %copy-start.1 = (bf16[256,1536]{1,0:T(8,128)(2,1)S(1)}, bf16[256,1536]{1,0:T(8,128)(2,1)}, u32[]{:S(2)}) copy-start(bf16[256,1536]{1,0:T(8,128)(2,1)} %broadcast_select_fusion.3) | copy-start | bytes 2359300
  151.4 30.1 %copy-start.3 = (bf16[256,1536]{1,0:T(8,128)(2,1)S(1)}, bf16[256,1536]{1,0:T(8,128)(2,1)}, u32[]{:S(2)}) copy-start(bf16[256,1536]{1,0:T(8,128)(2,1)} %copy-done.2) | copy-start | bytes 2359300
  151.4 30.1 %copy-start.8 = (f32[3072,32]{0,1:T(8,128)S(1)}, f32[3072,32]{0,1:T(8,128)}, u32[]{:S(2)}) copy-start(f32[3072,32]{0,1:T(8,128)} %param.7) | copy-start | bytes 1179652
Sparse Core Ops, SparseCore 0:
  10.8 46.8 all-gather.4
  59.9 42.7 all-gather.2

commit v3 on v2

--- a/solution.py
+++ b/solution.py
@@ -31,6 +31,17 @@
     while bit < count:
         block = block + swap(block, axis, count, bit)
         bit *= 2
+    return block
+
+
+def shift_sum(block, axis):
+    count = lax.axis_size(axis)
+    arrived = [
+        lax.ppermute(block, axis, [(i, (i + shift) % count) for i in range(count)])
+        for shift in range(1, count)
+    ]
+    for other in arrived:
+        block = block + other
     return block
 
 
@@ -72,29 +83,12 @@
     panel_width = design.shape[1]
     row_width = panel_width // fold_ratio
     filter_matrix = whitening(filter_taps)
-
-    epoch_block = design.shape[0]
-    epochs = epoch_block * row_count
-    part_width = row_width // 2
-    slices = design.reshape(epoch_block, fold_ratio, row_width)
-    owned = row_index % fold_ratio
-    gathered = []
-    for part_index in range(2):
-        part = slices[:, :, part_index * part_width : (part_index + 1) * part_width]
-        part = part.reshape(epoch_block, fold_ratio * part_width)
-        gathered.append(lax.all_gather(part, "row", axis=0, tiled=True))
-    parts, panel_parts = [], []
-    for part_index in range(2):
-        whole = gathered[part_index]
-        if panel_parts:
-            whole, panel_parts[-1] = lax.optimization_barrier((whole, panel_parts[-1]))
-        part = jnp.dot(filter_matrix, whole, preferred_element_type=jnp.float32)
-        part = part.astype(jnp.bfloat16).reshape(epochs, fold_ratio, part_width)
-        parts.append(part)
-        own_slice = lax.dynamic_index_in_dim(part, owned, 1, keepdims=False)
-        panel_parts.append(tree_broadcast(own_slice, fold_ratio))
-    white = jnp.stack(parts, axis=2).reshape(epochs, panel_width)
-    panel = jnp.concatenate(panel_parts, axis=1)
+    whole_panel = lax.all_gather(design, "row", axis=0, tiled=True)
+    white = jnp.dot(filter_matrix, whole_panel, preferred_element_type=jnp.float32).astype(
+        jnp.bfloat16
+    )
+    own_slice = lax.dynamic_slice_in_dim(white, row_index % fold_ratio * row_width, row_width, 1)
+    panel = tree_broadcast(own_slice, fold_ratio)
     normal_tile = lax.dot_general(
         panel, white, (((0,), (0,)), ((), ())), preferred_element_type=jnp.float32
     )
@@ -113,7 +107,7 @@
     residual = probes
     scaled = residual / jacobi
     direction = scaled / center_value
-    scaled_image = tree_sum(jnp.dot(panel_wide, scaled, precision=lax.Precision.HIGHEST), "row")
+    scaled_image = shift_sum(jnp.dot(panel_wide, scaled, precision=lax.Precision.HIGHEST), "row")
     image = scaled_image / center_value
     solution = jnp.zeros_like(residual)
     for sweep_index in range(SWEEPS):

time: 192 us -> 172 us (0.90)
  local copies, waits for them, and re-layouts: 30.3 us -> 4.51 us
  starting transfers between devices: 15.6 us -> 19.6 us
  waiting for transfers between devices: 81.1 us -> 84.4 us
    ppermute x0 -> x7, starting transfers between devices: none -> 12.4 us  [shift_sum(): lax.ppermute(block, axis, [(i, (i + shift) % count) for i in range(count)])]
    another operation x4 -> x0, local copies, waits for them, and re-layouts: 10 us -> none  [body(): white = jnp.stack(parts, axis=2).reshape(epochs, panel_width)]
    reshape x3 -> x0, local copies, waits for them, and re-layouts: 8.34 us -> none  [the longest x2 7.05 us: body(): part = part.astype(jnp.bfloat16).reshape(epochs, fold_ratio, part_width)]
    dynamic_slice x2 -> x1, local copies, waits for them, and re-layouts: 6.05 us -> 1.29 us  [body(): lax.dynamic_slice_in_dim(white, row_index % fold_ratio * row_width, row_w...]
    ppermute x4 -> x2, starting transfers between devices: 11.5 us -> 7 us  [tree_broadcast(): arrived = lax.ppermute(block, ('row', 'col'), pairs)]
    unnamed x25 -> x16, local copies, waits for them, and re-layouts: 5.21 us -> 1.36 us
    ppermute x5 -> x2, starting transfers between devices: 3.99 us -> 0.14 us  [swap(): return lax.ppermute(block, axis, [(i, i ^ bit) for i in range(count)])]
    all_gather x2 -> x1, waiting for transfers between devices: 60.2 us -> 63.4 us  [body(): whole_panel = lax.all_gather(design, 'row', axis=0, tiled=True)]
  transfers between devices with their start and end apart: 11 -> 12, of which waited for: 5 -> 3; matrix products, arithmetic and copies ran while one was open for 30% -> 25% of each run, Pallas kernels for 0% -> 0%
where the time goes in v3:
time: 172 us
  waiting for transfers between devices  84.4 us (49%)
  matrix products  41.8 us (24%)
  starting transfers between devices  19.6 us (11%)
  between operations  15.8 us (9%)
  other arithmetic  5.89 us (3%)
  local copies, waits for them, and re-layouts  4.51 us (3%)
    all_gather x1, waiting for transfers between devices, body(): whole_panel = lax.all_gather(design, 'row', axis=0, tiled=True)  63.4 us
    dot_general x1, matrix products, body(): lax.dot_general(panel, white, (((0,), (0,)), ((), ())), preferred_element...  29.7 us
    ppermute x2, waiting for transfers between devices, tree_broadcast(): arrived = lax.ppermute(block, ('row', 'col'), pairs)  17.1 us
    ppermute x7, starting transfers between devices, shift_sum(): lax.ppermute(block, axis, [(i, (i + shift) % count) for i in range(count)])  12.4 us
    ppermute x2, starting transfers between devices, tree_broadcast(): arrived = lax.ppermute(block, ('row', 'col'), pairs)  7 us
    dot_general x2, matrix products, contract_epochs(): lax.dot_general(left, right, (((0,), (0,)), ((), ())), precision=lax.Prec...  3.98 us
  transfers between devices with their start and end apart: 12, of which 3 were waited for; matrix products, arithmetic and copies ran while one was open for 25% of the time, Pallas kernels for 0%

profile of v3, /device:TPU:0, one launch (start us, length us, event | category | flops | bytes accessed | tf_op | source)
XLA Modules:
  0.0 172.0 jit_solution(2562290980935797204)
XLA Ops:
  7.2 0.0 all-gather.2.cloned.1.call-start
  7.2 0.7 all-gather.2.cloned.1.call-update
  7.9 0.7 concatenate.3
  8.6 0.1 broadcast_bitcast_fusion
  8.7 0.1 copy.7
  8.8 1.2 reshape.20
  10.0 63.4 %all-gather.2.cloned.1.call-done = bf16[256,6144]{1,0:T(8,128)(2,1)} async-done(((bf16[32,6144]{1,0:T(8,128)(2,1)}), bf16[256,6144]{1,0:T(8,128)(2,1)}) %all-gather.2.cloned.1.call-update) | async-done | bytes 3145744 | tf_op jit(solution)/shard_map/all_gather | solution.py:86
  73.4 3.0 %fusion.1 = (f32[6144]{0:T(1024)S(1)}, bf16[256,6144]{1,0:T(8,128)(2,1)S(1)}) fusion(bf16[256,6144]{1,0:T(8,128)(2,1)} %all-gather.2.cloned.1.call-done, f32[256,511]{1,0:T(8,128)} %reshape.20), kind=kOutput, calls=%fused_computation.4 | convolution fusion | flops 811853824 | bytes 6578176 | tf_op jit(solution)/shard_map/dot_general | solution.py:87
  76.4 1.3 constant_dynamic-slice_fusion
  77.7 4.5 %collective-permute-start = (bf16[256,3072]{1,0:T(8,128)(2,1)}, bf16[256,3072]{1,0:T(8,128)(2,1)}, u32[]{:S(2)}, u32[]{:S(2)}) collective-permute-start(bf16[256,3072]{1,0:T(8,128)(2,1)} %constant_dynamic-slice_fusion), channel_id=1, source_target_pairs={{0,2},{4,6},{9,11},{13,15},{18,16},{22,20},{27,25},{31,29}} | collective-permute-start | bytes 4718600 | tf_op jit(solution)/shard_map/ppermute | solution.py:66
  82.2 17.1 %collective-permute-done = bf16[256,3072]{1,0:T(8,128)(2,1)} collective-permute-done((bf16[256,3072]{1,0:T(8,128)(2,1)}, bf16[256,3072]{1,0:T(8,128)(2,1)}, u32[]{:S(2)}, u32[]{:S(2)}) %collective-permute-start) | collective-permute-done | bytes 1572896 | tf_op jit(solution)/shard_map/ppermute | solution.py:66
  99.3 1.7 %broadcast_select_fusion = bf16[256,3072]{1,0:T(8,128)(2,1)} fusion(bf16[256,3072]{1,0:T(8,128)(2,1)} %collective-permute-done, pred[]{:T(512)S(6)} %and.36, bf16[256,6144]{1,0:T(8,128)(2,1)S(1)} %get-tuple-element.7, s32[]{:T(128)S(6)} %select_n.32), kind=kLoop, calls=%fused_computation.13 | loop fusion | flops 786432 | bytes 4718597 | tf_op jit(solution)/shard_map/jit(_where)/select_n | solution.py:68
  101.0 2.5 %collective-permute-start.1 = (bf16[256,3072]{1,0:T(8,128)(2,1)}, bf16[256,3072]{1,0:T(8,128)(2,1)}, u32[]{:S(2)}, u32[]{:S(2)}) collective-permute-start(bf16[256,3072]{1,0:T(8,128)(2,1)} %broadcast_select_fusion), channel_id=1, source_target_pairs={{0,1},{2,3},{4,5},{6,7},{9,8},{11,10},{13,12},{15,14},{16,17},{18,... | collective-permute-start | bytes 4718600 | tf_op jit(solution)/shard_map/ppermute | solution.py:66
  104.8 3.4 %fusion = f32[256,256]{1,0:T(8,128)S(1)} fusion(bf16[256,6144]{1,0:T(8,128)(2,1)S(1)} %get-tuple-element.7, f32[6144]{0:T(1024)S(1)} %broadcast_add_fusion), kind=kOutput, calls=%fused_computation.2 | convolution fusion | flops 4834983936 | bytes 3432448 | tf_op jit(solution)/shard_map/dot_general | solution.py:97
  108.2 0.0 copy-start.4
  108.2 0.0 copy-start.2
  108.2 0.1 collective-permute-start.9
  108.3 0.0 collective-permute-done.1
  108.3 2.1 %multiply_reduce_fusion = (f32[3072]{0:T(1024)S(1)}, bf16[256,3072]{1,0:T(8,128)(2,1)S(1)}) fusion(bf16[256,3072]{1,0:T(8,128)(2,1)} %collective-permute-done.1, bf16[256,3072]{1,0:T(8,128)(2,1)} %broadcast_select_fusion, pred[]{:T(512)S(6)} %and.33), kind=kLoop, calls=%fused_computation.12 | loop fusion | flops 3142656 | bytes 4730881 | tf_op jit(solution)/shard_map/reduce_sum | solution.py:102
  110.4 0.0 copy-start
  110.4 0.0 copy-start.5
  110.5 1.1 copy-done
  111.6 0.0 copy-done.5
  111.6 0.0 copy-done.2
  111.6 1.4 fusion.8
  113.0 0.0 copy-done.4
  113.1 3.0 %collective-permute-start.8 = (f32[256,32]{0,1:T(8,128)S(1)}, f32[256,32]{0,1:T(8,128)S(1)}, u32[]{:S(2)}, u32[]{:S(2)}) collective-permute-start(f32[256,32]{0,1:T(8,128)S(1)} %fusion.8), channel_id=1, source_target_pairs={{0,28},{4,0},{8,4},{12,8},{16,12},{20,16},{24,20},{28,24},{1,29},{... | collective-permute-start | bytes 98312 | tf_op jit(solution)/shard_map/ppermute | solution.py:40
  116.1 2.9 %collective-permute-start.7 = (f32[256,32]{0,1:T(8,128)S(1)}, f32[256,32]{0,1:T(8,128)S(1)}, u32[]{:S(2)}, u32[]{:S(2)}) collective-permute-start(f32[256,32]{0,1:T(8,128)S(1)} %fusion.8), channel_id=1, source_target_pairs={{0,24},{4,28},{8,0},{12,4},{16,8},{20,12},{24,16},{28,20},{1,25},{... | collective-permute-start | bytes 98312 | tf_op jit(solution)/shard_map/ppermute | solution.py:40
  119.2 0.0 collective-permute-done.9
  119.2 1.1 add.96
  120.3 0.1 collective-permute-start.6
  120.4 1.5 collective-permute-start.5
  121.9 1.4 collective-permute-start.4
  123.3 0.0 collective-permute-done.8
  123.3 1.5 collective-permute-start.3
  124.8 0.0 collective-permute-done.7
  124.8 2.0 %collective-permute-start.2 = (f32[256,32]{0,1:T(8,128)S(1)}, f32[256,32]{0,1:T(8,128)}, u32[]{:S(2)}, u32[]{:S(2)}) collective-permute-start(f32[256,32]{0,1:T(8,128)S(1)} %fusion.8), channel_id=1, source_target_pairs={{0,4},{4,8},{8,12},{12,16},{16,20},{20,24},{24,28},{28,0},{1,5},{5... | collective-permute-start | bytes 98312 | tf_op jit(solution)/shard_map/ppermute | solution.py:40
  126.8 29.7 %fusion.18 = f32[3072,6144]{1,0:T(8,128)} fusion(bf16[256,3072]{1,0:T(8,128)(2,1)} %copy-done, bf16[256,6144]{1,0:T(8,128)(2,1)S(1)} %get-tuple-element.7), kind=kOutput, calls=%fused_computation.35 | convolution fusion | flops 9663676416 | bytes 80216064 | tf_op jit(solution)/shard_map/dot_general | solution.py:92
  156.4 0.0 copy-start.1
  156.4 0.0 copy-start.3
  156.4 0.0 copy-start.6
  156.4 0.0 collective-permute-done.6
  156.4 0.1 collective-permute-start.10
  156.5 0.0 collective-permute-done.5
  156.5 0.0 collective-permute-done.4
  156.5 0.0 collective-permute-done.3
  156.5 0.0 collective-permute-done.2
  156.6 0.9 add_add_fusion
  157.5 2.3 %convolution_subtract_fusion.1 = f32[3072,32]{0,1:T(8,128)S(1)} fusion(f32[3072,32]{0,1:T(8,128)} %param.7, bf16[256,3072]{1,0:T(8,128)(2,1)} %copy-done, f32[256,32]{0,1:T(8,128)S(1)} %add_add_fusion, f32[]{:T(128)} %bitcast.1), kind=kOutput, calls=%fused_computation.6 | convolution fusion | flops 302096384 | bytes 2392068 | tf_op jit(solution)/shard_map/dot_general | solution.py:73
  159.8 3.3 %collective-permute-done.10 = f32[256,256]{1,0:T(8,128)S(1)} collective-permute-done((f32[256,256]{1,0:T(8,128)S(1)}, f32[256,256]{1,0:T(8,128)S(1)}, u32[]{:S(2)}, u32[]{:S(2)}) %collective-permute-start.10) | collective-permute-done | bytes 262176 | tf_op jit(solution)/shard_map/ppermute | solution.py:23
  163.1 0.4 fusion.7
  163.5 0.0 copy-done.1
  163.5 0.0 copy-done.3
  163.5 0.0 copy-done.6
  163.5 1.6 fusion.5
  (2 shorter events, 0.0 us)
Async XLA Ops:
  7.2 66.2 %all-gather.2.cloned.1.call-start = ((), (), s32[]{:S(2)}) async-start(), calls=%async_computation | async-start | bytes 3538944 | tf_op jit(solution)/shard_map/all_gather | solution.py:86
  77.7 21.6 %collective-permute-start = (bf16[256,3072]{1,0:T(8,128)(2,1)}, bf16[256,3072]{1,0:T(8,128)(2,1)}, u32[]{:S(2)}, u32[]{:S(2)}) collective-permute-start(bf16[256,3072]{1,0:T(8,128)(2,1)} %constant_dynamic-slice_fusion), channel_id=1, source_target_pairs={{0,2},{4,6},{9,11},{13,15},{18,16},{22,20},{27,25},{31,29}} | collective-permute-start | bytes 4718600 | tf_op jit(solution)/shard_map/ppermute | solution.py:66
  101.0 7.3 %collective-permute-start.1 = (bf16[256,3072]{1,0:T(8,128)(2,1)}, bf16[256,3072]{1,0:T(8,128)(2,1)}, u32[]{:S(2)}, u32[]{:S(2)}) collective-permute-start(bf16[256,3072]{1,0:T(8,128)(2,1)} %broadcast_select_fusion), channel_id=1, source_target_pairs={{0,1},{2,3},{4,5},{6,7},{9,8},{11,10},{13,12},{15,14},{16,17},{18,... | collective-permute-start | bytes 4718600 | tf_op jit(solution)/shard_map/ppermute | solution.py:66
  108.2 4.9 %copy-start.4 = (f32[256,256]{1,0:T(8,128)}, f32[256,256]{1,0:T(8,128)S(1)}, u32[]{:S(2)}) copy-start(f32[256,256]{1,0:T(8,128)S(1)} %fusion) | copy-start | bytes 786436
  108.2 3.4 %copy-start.2 = (f32[3072,32]{0,1:T(8,128)S(1)}, f32[3072,32]{0,1:T(8,128)}, u32[]{:S(2)}) copy-start(f32[3072,32]{0,1:T(8,128)} %param.7) | copy-start | bytes 1179652
  108.2 11.0 %collective-permute-start.9 = (f32[256,256]{1,0:T(8,128)S(1)}, f32[256,256]{1,0:T(8,128)}, u32[]{:S(2)}, u32[]{:S(2)}) collective-permute-start(f32[256,256]{1,0:T(8,128)S(1)} %fusion), channel_id=1, source_target_pairs={{0,1},{1,0},{2,3},{3,2},{4,5},{5,4},{6,7},{7,6},{8,9},{9,8},{10,11... | collective-permute-start | bytes 786440 | tf_op jit(solution)/shard_map/ppermute | solution.py:23
  110.4 1.2 copy-start
  110.4 1.2 copy-start.5
  113.1 10.2 %collective-permute-start.8 = (f32[256,32]{0,1:T(8,128)S(1)}, f32[256,32]{0,1:T(8,128)S(1)}, u32[]{:S(2)}, u32[]{:S(2)}) collective-permute-start(f32[256,32]{0,1:T(8,128)S(1)} %fusion.8), channel_id=1, source_target_pairs={{0,28},{4,0},{8,4},{12,8},{16,12},{20,16},{24,20},{28,24},{1,29},{... | collective-permute-start | bytes 98312 | tf_op jit(solution)/shard_map/ppermute | solution.py:40
  116.1 8.7 %collective-permute-start.7 = (f32[256,32]{0,1:T(8,128)S(1)}, f32[256,32]{0,1:T(8,128)S(1)}, u32[]{:S(2)}, u32[]{:S(2)}) collective-permute-start(f32[256,32]{0,1:T(8,128)S(1)} %fusion.8), channel_id=1, source_target_pairs={{0,24},{4,28},{8,0},{12,4},{16,8},{20,12},{24,16},{28,20},{1,25},{... | collective-permute-start | bytes 98312 | tf_op jit(solution)/shard_map/ppermute | solution.py:40
  120.3 36.1 %collective-permute-start.6 = (f32[256,32]{0,1:T(8,128)S(1)}, f32[256,32]{0,1:T(8,128)S(1)}, u32[]{:S(2)}, u32[]{:S(2)}) collective-permute-start(f32[256,32]{0,1:T(8,128)S(1)} %fusion.8), channel_id=1, source_target_pairs={{0,20},{4,24},{8,28},{12,0},{16,4},{20,8},{24,12},{28,16},{1,21},{... | collective-permute-start | bytes 98312 | tf_op jit(solution)/shard_map/ppermute | solution.py:40
  120.4 36.2 %collective-permute-start.5 = (f32[256,32]{0,1:T(8,128)S(1)}, f32[256,32]{0,1:T(8,128)}, u32[]{:S(2)}, u32[]{:S(2)}) collective-permute-start(f32[256,32]{0,1:T(8,128)S(1)} %fusion.8), channel_id=1, source_target_pairs={{0,16},{4,20},{8,24},{12,28},{16,0},{20,4},{24,8},{28,12},{1,17},{... | collective-permute-start | bytes 98312 | tf_op jit(solution)/shard_map/ppermute | solution.py:40
  121.9 34.7 %collective-permute-start.4 = (f32[256,32]{0,1:T(8,128)S(1)}, f32[256,32]{0,1:T(8,128)}, u32[]{:S(2)}, u32[]{:S(2)}) collective-permute-start(f32[256,32]{0,1:T(8,128)S(1)} %fusion.8), channel_id=1, source_target_pairs={{0,12},{4,16},{8,20},{12,24},{16,28},{20,0},{24,4},{28,8},{1,13},{... | collective-permute-start | bytes 98312 | tf_op jit(solution)/shard_map/ppermute | solution.py:40
  123.3 33.3 %collective-permute-start.3 = (f32[256,32]{0,1:T(8,128)S(1)}, f32[256,32]{0,1:T(8,128)}, u32[]{:S(2)}, u32[]{:S(2)}) collective-permute-start(f32[256,32]{0,1:T(8,128)S(1)} %fusion.8), channel_id=1, source_target_pairs={{0,8},{4,12},{8,16},{12,20},{16,24},{20,28},{24,0},{28,4},{1,9},{5... | collective-permute-start | bytes 98312 | tf_op jit(solution)/shard_map/ppermute | solution.py:40
  124.8 31.7 %collective-permute-start.2 = (f32[256,32]{0,1:T(8,128)S(1)}, f32[256,32]{0,1:T(8,128)}, u32[]{:S(2)}, u32[]{:S(2)}) collective-permute-start(f32[256,32]{0,1:T(8,128)S(1)} %fusion.8), channel_id=1, source_target_pairs={{0,4},{4,8},{8,12},{12,16},{16,20},{20,24},{24,28},{28,0},{1,5},{5... | collective-permute-start | bytes 98312 | tf_op jit(solution)/shard_map/ppermute | solution.py:40
  156.4 7.0 %copy-start.1 = (bf16[256,3072]{1,0:T(8,128)(2,1)S(1)}, bf16[256,3072]{1,0:T(8,128)(2,1)}, u32[]{:S(2)}) copy-start(bf16[256,3072]{1,0:T(8,128)(2,1)} %copy-done) | copy-start | bytes 4718596
  156.4 7.1 %copy-start.3 = (f32[3072,32]{0,1:T(8,128)S(1)}, f32[3072,32]{0,1:T(8,128)}, u32[]{:S(2)}) copy-start(f32[3072,32]{0,1:T(8,128)} %param.7) | copy-start | bytes 1179652
  156.4 7.1 %copy-start.6 = (f32[3072]{0:T(1024)S(1)}, f32[3072]{0:T(1024)}, u32[]{:S(2)}) copy-start(f32[3072]{0:T(1024)} %copy-done.5) | copy-start | bytes 36868
  156.4 6.7 %collective-permute-start.10 = (f32[256,256]{1,0:T(8,128)S(1)}, f32[256,256]{1,0:T(8,128)S(1)}, u32[]{:S(2)}, u32[]{:S(2)}) collective-permute-start(f32[256,256]{1,0:T(8,128)S(1)} %add.96), channel_id=1, source_target_pairs={{0,2},{1,3},{2,0},{3,1},{4,6},{5,7},{6,4},{7,5},{8,10},{9,11},{10,... | collective-permute-start | bytes 786440 | tf_op jit(solution)/shard_map/ppermute | solution.py:23
Sparse Core Ops, SparseCore 0:
  10.2 63.1 all-gather.1

commit v4 on v3

--- a/solution.py
+++ b/solution.py
@@ -45,14 +45,14 @@
     return block
 
 
-def tree_broadcast(block, fold_ratio):
+def tree_broadcast(block, fold_ratio, companion):
     row_count = lax.axis_size("row")
     col_count = lax.axis_size("col")
     owner = lax.axis_index("row") // fold_ratio
     offset = lax.axis_index("col") ^ owner
     if not is_power_of_two(col_count):
         block = jnp.where(offset == 0, block, jnp.zeros_like(block))
-        return lax.psum(block, "col")
+        return lax.psum(block, "col"), companion()
     bits = [1 << k for k in range(1, col_count.bit_length() - 1)] + [1][: col_count > 1]
     done = 0
     for bit in bits:
@@ -66,7 +66,9 @@
         arrived = lax.ppermute(block, ("row", "col"), pairs)
         done |= bit
         block = jnp.where((offset & ~done == 0) & (offset & bit != 0), arrived, block)
-    return block
+        block, companion = lax.optimization_barrier((block, companion()))
+        companion = lambda held=companion: held
+    return block, companion()
 
 
 def contract_epochs(left, right):
@@ -88,17 +90,20 @@
         jnp.bfloat16
     )
     own_slice = lax.dynamic_slice_in_dim(white, row_index % fold_ratio * row_width, row_width, 1)
-    panel = tree_broadcast(own_slice, fold_ratio)
+
+    def couple():
+        white_wide = white.astype(jnp.float32)
+        panel_jacobi = jnp.sum(jnp.square(white_wide), axis=0) + 1e-06
+        coupling = jnp.dot(
+            white_wide / panel_jacobi[None, :], white_wide.T, precision=lax.Precision.HIGHEST
+        )
+        return tree_sum(coupling, "col")
+
+    panel, coupling = tree_broadcast(own_slice, fold_ratio, couple)
+    panel_wide = panel.astype(jnp.float32)
     normal_tile = lax.dot_general(
         panel, white, (((0,), (0,)), ((), ())), preferred_element_type=jnp.float32
     )
-    white_wide = white.astype(jnp.float32)
-    panel_jacobi = jnp.sum(jnp.square(white_wide), axis=0) + 1e-06
-    coupling = jnp.dot(
-        white_wide / panel_jacobi[None, :], white_wide.T, precision=lax.Precision.HIGHEST
-    )
-    coupling = tree_sum(coupling, "col")
-    panel_wide = panel.astype(jnp.float32)
     jacobi = (jnp.sum(jnp.square(panel_wide), axis=0) + 1e-06)[:, None]
     center_value = (lower_bound[0] + upper_bound[0]) / 2.0
     half_width = (upper_bound[0] - lower_bound[0]) / 2.0

time: 172 us -> 174 us (1.012)
    ppermute x2, waiting for transfers between devices: 17.1 us -> 0.88 us  [tree_broadcast(): arrived = lax.ppermute(block, ('row', 'col'), pairs)]
    ppermute x2, waiting for transfers between devices: 3.27 us -> 19 us  [swap(): return lax.ppermute(block, axis, [(i, i ^ bit) for i in range(count)])]
    reduce_sum x1, other arithmetic: 2.13 us -> 0.33 us  [body(): jacobi = (jnp.sum(jnp.square(panel_wide), axis=0) + 1e-06)[:, None]]
  transfers between devices with their start and end apart: 12 -> 12, of which waited for: 3 -> 4; matrix products, arithmetic and copies ran while one was open for 25% -> 21% of each run, Pallas kernels for 0% -> 0%
where the time goes in v4:
time: 174 us; the launch traced here: 173 us
  waiting for transfers between devices  83.9 us (48%)
  matrix products  43.3 us (25%)
  starting transfers between devices  19.6 us (11%)
  between operations  15.8 us (9%)
  other arithmetic  6.2 us (4%)
  local copies, waits for them, and re-layouts  4.18 us (2%)
    all_gather x1, waiting for transfers between devices, body(): whole_panel = lax.all_gather(design, 'row', axis=0, tiled=True)  63.4 us
    dot_general x1, matrix products, body(): lax.dot_general(panel, white, (((0,), (0,)), ((), ())), preferred_element...  29.7 us
    ppermute x2, waiting for transfers between devices, swap(): return lax.ppermute(block, axis, [(i, i ^ bit) for i in range(count)])  19 us
    ppermute x7, starting transfers between devices, shift_sum(): lax.ppermute(block, axis, [(i, (i + shift) % count) for i in range(count)])  12.5 us
    ppermute x2, starting transfers between devices, tree_broadcast(): arrived = lax.ppermute(block, ('row', 'col'), pairs)  7 us
    dot_general x2, matrix products, contract_epochs(): lax.dot_general(left, right, (((0,), (0,)), ((), ())), precision=lax.Prec...  5.52 us
  transfers between devices with their start and end apart: 12, of which 4 were waited for; matrix products, arithmetic and copies ran while one was open for 21% of the time, Pallas kernels for 0%

profile of v4, /device:TPU:0, one launch (start us, length us, event | category | flops | bytes accessed | tf_op | source)
XLA Modules:
  0.0 173.1 jit_solution(8631186746344671447)
XLA Ops:
  7.2 0.0 all-gather.2.cloned.1.call-start
  7.2 0.7 all-gather.2.cloned.1.call-update
  7.9 0.7 concatenate.3
  8.6 0.1 broadcast_bitcast_fusion
  8.7 0.1 copy.7
  8.8 1.2 reshape.20
  10.0 63.4 %all-gather.2.cloned.1.call-done = bf16[256,6144]{1,0:T(8,128)(2,1)} async-done(((bf16[32,6144]{1,0:T(8,128)(2,1)}), bf16[256,6144]{1,0:T(8,128)(2,1)}) %all-gather.2.cloned.1.call-update) | async-done | bytes 3145744 | tf_op jit(solution)/shard_map/all_gather | solution.py:88
  73.4 3.0 %fusion.1 = (f32[6144]{0:T(1024)S(1)}, bf16[256,6144]{1,0:T(8,128)(2,1)S(1)}) fusion(bf16[256,6144]{1,0:T(8,128)(2,1)} %all-gather.2.cloned.1.call-done, f32[256,511]{1,0:T(8,128)} %reshape.20), kind=kOutput, calls=%fused_computation.4 | convolution fusion | flops 811853824 | bytes 6578176 | tf_op jit(solution)/shard_map/dot_general | solution.py:89
  76.4 1.3 constant_dynamic-slice_fusion
  77.7 4.5 %collective-permute-start = (bf16[256,3072]{1,0:T(8,128)(2,1)}, bf16[256,3072]{1,0:T(8,128)(2,1)}, u32[]{:S(2)}, u32[]{:S(2)}) collective-permute-start(bf16[256,3072]{1,0:T(8,128)(2,1)} %constant_dynamic-slice_fusion), channel_id=1, source_target_pairs={{0,2},{4,6},{9,11},{13,15},{18,16},{22,20},{27,25},{31,29}} | collective-permute-start | bytes 4718600 | tf_op jit(solution)/shard_map/ppermute | solution.py:66
  82.2 3.4 %fusion = f32[256,256]{1,0:T(8,128)S(1)} fusion(bf16[256,6144]{1,0:T(8,128)(2,1)S(1)} %get-tuple-element.13, f32[6144]{0:T(1024)S(1)} %broadcast_add_fusion), kind=kOutput, calls=%fused_computation.2 | convolution fusion | flops 4834983936 | bytes 3432448 | tf_op jit(solution)/shard_map/dot_general | solution.py:97
  85.6 0.1 collective-permute-start.1
  85.7 1.5 collective-permute-done.1
  87.2 0.1 collective-permute-start.2
  87.3 17.4 %collective-permute-done.2 = f32[256,256]{1,0:T(8,128)} collective-permute-done((f32[256,256]{1,0:T(8,128)S(1)}, f32[256,256]{1,0:T(8,128)}, u32[]{:S(2)}, u32[]{:S(2)}) %collective-permute-start.2) | collective-permute-done | bytes 262176 | tf_op jit(solution)/shard_map/ppermute | solution.py:23
  104.8 1.7 add.85
  106.5 0.0 collective-permute-done
  106.5 1.7 %broadcast_select_fusion = bf16[256,3072]{1,0:T(8,128)(2,1)} fusion(bf16[256,3072]{1,0:T(8,128)(2,1)} %collective-permute-done, pred[]{:T(512)S(6)} %and.36, bf16[256,6144]{1,0:T(8,128)(2,1)S(1)} %get-tuple-element.13, s32[]{:T(128)S(6)} %select_n.32), kind=kLoop, calls=%fused_computation.13 | loop fusion | flops 786432 | bytes 4718597 | tf_op jit(solution)/shard_map/jit(_where)/select_n | solution.py:68
  108.2 2.5 %collective-permute-start.3 = (bf16[256,3072]{1,0:T(8,128)(2,1)}, bf16[256,3072]{1,0:T(8,128)(2,1)}, u32[]{:S(2)}, u32[]{:S(2)}) collective-permute-start(bf16[256,3072]{1,0:T(8,128)(2,1)} %broadcast_select_fusion), channel_id=1, source_target_pairs={{0,1},{2,3},{4,5},{6,7},{9,8},{11,10},{13,12},{15,14},{16,17},{18,... | collective-permute-start | bytes 4718600 | tf_op jit(solution)/shard_map/ppermute | solution.py:66
  112.0 0.0 copy-start.2
  112.0 0.9 collective-permute-done.3
  112.9 1.6 broadcast_select_fusion.1
  114.4 0.0 copy-start
  114.5 0.3 multiply_reduce_fusion
  114.8 0.0 copy-start.3
  114.8 0.8 copy-done
  115.6 0.0 copy-done.3
  115.6 0.0 copy-done.2
  115.6 1.4 fusion.8
  117.1 3.1 %collective-permute-start.10 = (f32[256,32]{0,1:T(8,128)S(1)}, f32[256,32]{0,1:T(8,128)S(1)}, u32[]{:S(2)}, u32[]{:S(2)}) collective-permute-start(f32[256,32]{0,1:T(8,128)S(1)} %fusion.8), channel_id=1, source_target_pairs={{0,28},{4,0},{8,4},{12,8},{16,12},{20,16},{24,20},{28,24},{1,29},{... | collective-permute-start | bytes 98312 | tf_op jit(solution)/shard_map/ppermute | solution.py:40
  120.2 2.9 %collective-permute-start.9 = (f32[256,32]{0,1:T(8,128)S(1)}, f32[256,32]{0,1:T(8,128)S(1)}, u32[]{:S(2)}, u32[]{:S(2)}) collective-permute-start(f32[256,32]{0,1:T(8,128)S(1)} %fusion.8), channel_id=1, source_target_pairs={{0,24},{4,28},{8,0},{12,4},{16,8},{20,12},{24,16},{28,20},{1,25},{... | collective-permute-start | bytes 98312 | tf_op jit(solution)/shard_map/ppermute | solution.py:40
  123.3 0.0 copy-start.1
  123.3 0.1 collective-permute-start.8
  123.4 1.5 collective-permute-start.7
  124.9 1.4 collective-permute-start.6
  126.3 0.0 collective-permute-done.10
  126.3 1.5 collective-permute-start.5
  127.9 0.0 collective-permute-done.9
  127.9 2.0 %collective-permute-start.4 = (f32[256,32]{0,1:T(8,128)S(1)}, f32[256,32]{0,1:T(8,128)}, u32[]{:S(2)}, u32[]{:S(2)}) collective-permute-start(f32[256,32]{0,1:T(8,128)S(1)} %fusion.8), channel_id=1, source_target_pairs={{0,4},{4,8},{8,12},{12,16},{16,20},{20,24},{24,28},{28,0},{1,5},{5... | collective-permute-start | bytes 98312 | tf_op jit(solution)/shard_map/ppermute | solution.py:40
  129.8 29.7 %fusion.17 = f32[3072,6144]{1,0:T(8,128)} fusion(bf16[256,3072]{1,0:T(8,128)(2,1)} %copy-done, bf16[256,6144]{1,0:T(8,128)(2,1)S(1)} %get-tuple-element.13), kind=kOutput, calls=%fused_computation.34 | convolution fusion | flops 9663676416 | bytes 80216064 | tf_op jit(solution)/shard_map/dot_general | solution.py:104
  159.5 0.0 collective-permute-done.8
  159.5 0.0 collective-permute-done.7
  159.5 0.0 collective-permute-done.6
  159.5 0.0 collective-permute-done.5
  159.5 0.0 collective-permute-done.4
  159.5 0.8 add_add_fusion
  160.3 2.3 %convolution_subtract_fusion.1 = f32[3072,32]{0,1:T(8,128)S(1)} fusion(f32[3072,32]{0,1:T(8,128)} %param.7, bf16[256,3072]{1,0:T(8,128)(2,1)} %copy-done, f32[256,32]{0,1:T(8,128)S(1)} %add_add_fusion, f32[]{:T(128)} %bitcast.1), kind=kOutput, calls=%fused_computation.6 | convolution fusion | flops 302096384 | bytes 2392068 | tf_op jit(solution)/shard_map/dot_general | solution.py:75
  162.7 0.0 copy-done.1
  162.7 0.3 fusion.7
  163.1 3.2 %fusion.5 = f32[3072,32]{0,1:T(8,128)} fusion(f32[3072,32]{0,1:T(8,128)S(1)} %convolution_subtract_fusion.1, bf16[256,3072]{1,0:T(8,128)(2,1)} %copy-done, f32[3072,32]{0,1:T(8,128)} %param.7, f32[]{:T(128)S(6)} %div.101, f32[]{:T(128)S(6)} %mul.65, f32[3072]{0:T(1024)} %copy-done.3, f32[]{:T(128)S(6)} %div.94, f32[]{:T(128)S(6)} %mul.59, ...), kind=kOutput, calls=%fused_computation.10 | convolution fusion | flops 303194112 | bytes 2842644 | tf_op jit(solution)/shard_map/dot_general | solution.py:75
  (3 shorter events, 0.0 us)
Async XLA Ops:
  7.2 66.2 %all-gather.2.cloned.1.call-start = ((), (), s32[]{:S(2)}) async-start(), calls=%async_computation | async-start | bytes 3538944 | tf_op jit(solution)/shard_map/all_gather | solution.py:88
  77.7 28.8 %collective-permute-start = (bf16[256,3072]{1,0:T(8,128)(2,1)}, bf16[256,3072]{1,0:T(8,128)(2,1)}, u32[]{:S(2)}, u32[]{:S(2)}) collective-permute-start(bf16[256,3072]{1,0:T(8,128)(2,1)} %constant_dynamic-slice_fusion), channel_id=1, source_target_pairs={{0,2},{4,6},{9,11},{13,15},{18,16},{22,20},{27,25},{31,29}} | collective-permute-start | bytes 4718600 | tf_op jit(solution)/shard_map/ppermute | solution.py:66
  85.6 1.6 collective-permute-start.1
  87.2 17.5 %collective-permute-start.2 = (f32[256,256]{1,0:T(8,128)S(1)}, f32[256,256]{1,0:T(8,128)}, u32[]{:S(2)}, u32[]{:S(2)}) collective-permute-start(f32[256,256]{1,0:T(8,128)S(1)} %add.84), channel_id=1, source_target_pairs={{0,2},{1,3},{2,0},{3,1},{4,6},{5,7},{6,4},{7,5},{8,10},{9,11},{10,... | collective-permute-start | bytes 786440 | tf_op jit(solution)/shard_map/ppermute | solution.py:23
  108.2 4.6 %collective-permute-start.3 = (bf16[256,3072]{1,0:T(8,128)(2,1)}, bf16[256,3072]{1,0:T(8,128)(2,1)}, u32[]{:S(2)}, u32[]{:S(2)}) collective-permute-start(bf16[256,3072]{1,0:T(8,128)(2,1)} %broadcast_select_fusion), channel_id=1, source_target_pairs={{0,1},{2,3},{4,5},{6,7},{9,8},{11,10},{13,12},{15,14},{16,17},{18,... | collective-permute-start | bytes 4718600 | tf_op jit(solution)/shard_map/ppermute | solution.py:66
  112.0 3.7 %copy-start.2 = (f32[3072,32]{0,1:T(8,128)S(1)}, f32[3072,32]{0,1:T(8,128)}, u32[]{:S(2)}) copy-start(f32[3072,32]{0,1:T(8,128)} %param.7) | copy-start | bytes 1179652
  114.4 1.2 copy-start
  114.8 0.8 copy-start.3
  117.1 9.2 %collective-permute-start.10 = (f32[256,32]{0,1:T(8,128)S(1)}, f32[256,32]{0,1:T(8,128)S(1)}, u32[]{:S(2)}, u32[]{:S(2)}) collective-permute-start(f32[256,32]{0,1:T(8,128)S(1)} %fusion.8), channel_id=1, source_target_pairs={{0,28},{4,0},{8,4},{12,8},{16,12},{20,16},{24,20},{28,24},{1,29},{... | collective-permute-start | bytes 98312 | tf_op jit(solution)/shard_map/ppermute | solution.py:40
  120.2 7.6 %collective-permute-start.9 = (f32[256,32]{0,1:T(8,128)S(1)}, f32[256,32]{0,1:T(8,128)S(1)}, u32[]{:S(2)}, u32[]{:S(2)}) collective-permute-start(f32[256,32]{0,1:T(8,128)S(1)} %fusion.8), channel_id=1, source_target_pairs={{0,24},{4,28},{8,0},{12,4},{16,8},{20,12},{24,16},{28,20},{1,25},{... | collective-permute-start | bytes 98312 | tf_op jit(solution)/shard_map/ppermute | solution.py:40
  123.3 39.4 %copy-start.1 = (f32[256,256]{1,0:T(8,128)S(1)}, f32[256,256]{1,0:T(8,128)}, u32[]{:S(2)}) copy-start(f32[256,256]{1,0:T(8,128)} %add.85) | copy-start | bytes 786436
  123.3 36.1 %collective-permute-start.8 = (f32[256,32]{0,1:T(8,128)S(1)}, f32[256,32]{0,1:T(8,128)S(1)}, u32[]{:S(2)}, u32[]{:S(2)}) collective-permute-start(f32[256,32]{0,1:T(8,128)S(1)} %fusion.8), channel_id=1, source_target_pairs={{0,20},{4,24},{8,28},{12,0},{16,4},{20,8},{24,12},{28,16},{1,21},{... | collective-permute-start | bytes 98312 | tf_op jit(solution)/shard_map/ppermute | solution.py:40
  123.4 36.1 %collective-permute-start.7 = (f32[256,32]{0,1:T(8,128)S(1)}, f32[256,32]{0,1:T(8,128)}, u32[]{:S(2)}, u32[]{:S(2)}) collective-permute-start(f32[256,32]{0,1:T(8,128)S(1)} %fusion.8), channel_id=1, source_target_pairs={{0,16},{4,20},{8,24},{12,28},{16,0},{20,4},{24,8},{28,12},{1,17},{... | collective-permute-start | bytes 98312 | tf_op jit(solution)/shard_map/ppermute | solution.py:40
  124.9 34.6 %collective-permute-start.6 = (f32[256,32]{0,1:T(8,128)S(1)}, f32[256,32]{0,1:T(8,128)}, u32[]{:S(2)}, u32[]{:S(2)}) collective-permute-start(f32[256,32]{0,1:T(8,128)S(1)} %fusion.8), channel_id=1, source_target_pairs={{0,12},{4,16},{8,20},{12,24},{16,28},{20,0},{24,4},{28,8},{1,13},{... | collective-permute-start | bytes 98312 | tf_op jit(solution)/shard_map/ppermute | solution.py:40
  126.3 33.2 %collective-permute-start.5 = (f32[256,32]{0,1:T(8,128)S(1)}, f32[256,32]{0,1:T(8,128)}, u32[]{:S(2)}, u32[]{:S(2)}) collective-permute-start(f32[256,32]{0,1:T(8,128)S(1)} %fusion.8), channel_id=1, source_target_pairs={{0,8},{4,12},{8,16},{12,20},{16,24},{20,28},{24,0},{28,4},{1,9},{5... | collective-permute-start | bytes 98312 | tf_op jit(solution)/shard_map/ppermute | solution.py:40
  127.9 31.6 %collective-permute-start.4 = (f32[256,32]{0,1:T(8,128)S(1)}, f32[256,32]{0,1:T(8,128)}, u32[]{:S(2)}, u32[]{:S(2)}) collective-permute-start(f32[256,32]{0,1:T(8,128)S(1)} %fusion.8), channel_id=1, source_target_pairs={{0,4},{4,8},{8,12},{12,16},{16,20},{20,24},{24,28},{28,0},{1,5},{5... | collective-permute-start | bytes 98312 | tf_op jit(solution)/shard_map/ppermute | solution.py:40
Sparse Core Ops, SparseCore 0:
  10.2 63.1 all-gather.1

commit v5 on v4

--- a/solution.py
+++ b/solution.py
@@ -1,6 +1,8 @@
 import jax
 import jax.numpy as jnp
 from jax import lax
+from jax.experimental import pallas as pl
+from jax.experimental.pallas import tpu as pltpu
 from jax.sharding import PartitionSpec as P
 
 SWEEPS = 2
@@ -45,7 +47,7 @@
     return block
 
 
-def tree_broadcast(block, fold_ratio, companion):
+def tree_broadcast(block, fold_ratio, companion, on_first=None):
     row_count = lax.axis_size("row")
     col_count = lax.axis_size("col")
     owner = lax.axis_index("row") // fold_ratio
@@ -68,7 +70,50 @@
         block = jnp.where((offset & ~done == 0) & (offset & bit != 0), arrived, block)
         block, companion = lax.optimization_barrier((block, companion()))
         companion = lambda held=companion: held
+        if on_first is not None:
+            block = on_first(block)
+            on_first = None
     return block, companion()
+
+
+def product_kernel(left_ref, right_ref, out_ref):
+    out_ref[...] = jnp.dot(left_ref[...], right_ref[...], preferred_element_type=jnp.float32)
+
+
+def normal_rows(left, right, total_rows, first_row, previous):
+    rows, epochs = left.shape
+    width = right.shape[1]
+    tile_rows = 512 if rows % 512 == 0 else rows
+    tile_cols = 2048 if width % 2048 == 0 else width
+    row_offset = first_row // tile_rows
+    in_specs = [
+        pl.BlockSpec((tile_rows, epochs), lambda j, i: (i, 0)),
+        pl.BlockSpec((epochs, tile_cols), lambda j, i: (0, j)),
+    ]
+    operands = [left, right]
+    aliases = {}
+    if previous is not None:
+        in_specs.append(pl.BlockSpec(memory_space=pl.ANY))
+        operands.append(previous)
+        aliases = {2: 0}
+
+    def kernel(left_ref, right_ref, *rest):
+        product_kernel(left_ref, right_ref, rest[-1])
+
+    return pl.pallas_call(
+        kernel,
+        grid=(width // tile_cols, rows // tile_rows),
+        in_specs=in_specs,
+        out_specs=pl.BlockSpec((tile_rows, tile_cols), lambda j, i: (i + row_offset, j)),
+        out_shape=jax.ShapeDtypeStruct((total_rows, width), jnp.float32),
+        input_output_aliases=aliases,
+        compiler_params=pltpu.CompilerParams(vmem_limit_bytes=48 * 1024 * 1024),
+        cost_estimate=pl.CostEstimate(
+            flops=2 * rows * epochs * width,
+            transcendentals=0,
+            bytes_accessed=rows * width * 4 + epochs * width * 2 + rows * epochs * 2,
+        ),
+    )(*operands)
 
 
 def contract_epochs(left, right):
@@ -99,11 +144,24 @@
         )
         return tree_sum(coupling, "col")
 
-    panel, coupling = tree_broadcast(own_slice, fold_ratio, couple)
+    half_rows = row_width // 2
+    held = {}
+
+    def release_second(block):
+        held["second"], block = lax.optimization_barrier((own_slice[:, half_rows:], block))
+        return block
+
+    panel_first, coupling = tree_broadcast(
+        own_slice[:, :half_rows], fold_ratio, couple, release_second
+    )
+    panel_second, normal_tile = tree_broadcast(
+        held["second"],
+        fold_ratio,
+        lambda: normal_rows(panel_first.T, white, row_width, 0, None),
+    )
+    normal_tile = normal_rows(panel_second.T, white, row_width, half_rows, normal_tile)
+    panel = jnp.concatenate([panel_first, panel_second], axis=1)
     panel_wide = panel.astype(jnp.float32)
-    normal_tile = lax.dot_general(
-        panel, white, (((0,), (0,)), ((), ())), preferred_element_type=jnp.float32
-    )
     jacobi = (jnp.sum(jnp.square(panel_wide), axis=0) + 1e-06)[:, None]
     center_value = (lower_bound[0] + upper_bound[0]) / 2.0
     half_width = (upper_bound[0] - lower_bound[0]) / 2.0

time: 174 us -> 173 us (level)
  matrix products: 43.3 us -> 10.7 us
  Pallas kernels: 0 us -> 27.6 us
  waiting for transfers between devices: 83.9 us -> 75.3 us
  local copies, waits for them, and re-layouts: 4.18 us -> 12.1 us
  starting transfers between devices: 19.6 us -> 23.3 us
    dot_general x1 -> x0, matrix products: 29.7 us -> none  [body(): lax.dot_general(panel, white, (((0,), (0,)), ((), ())), preferred_element...]
    pallas_call x0 -> x2, Pallas kernels: none -> 27.6 us  [normal_rows(): pl.pallas_call(kernel, grid=(width // tile_cols, rows // tile_rows), in_s...]
    ppermute x2, waiting for transfers between devices: 19 us -> 10.8 us  [swap(): return lax.ppermute(block, axis, [(i, i ^ bit) for i in range(count)])]
    ppermute x2 -> x4, starting transfers between devices: 7 us -> 13.2 us  [tree_broadcast(): arrived = lax.ppermute(block, ('row', 'col'), pairs)]
    transpose x0 -> x2, local copies, waits for them, and re-layouts: none -> 4.63 us  [the longest x1 2.35 us: body(): normal_tile = normal_rows(panel_second.T, white, row_width, half_rows, no...]
    unnamed x10 -> x27, local copies, waits for them, and re-layouts: 1.02 us -> 4.25 us
    dot_general x2, matrix products: 5.52 us -> 2.51 us  [contract_epochs(): lax.dot_general(left, right, (((0,), (0,)), ((), ())), precision=lax.Prec...]
    ppermute x7, starting transfers between devices: 12.5 us -> 9.95 us  [shift_sum(): lax.ppermute(block, axis, [(i, (i + shift) % count) for i in range(count)])]
  transfers between devices with their start and end apart: 12 -> 14, of which waited for: 4 -> 4; matrix products, arithmetic and copies ran while one was open for 21% -> 8% of each run, Pallas kernels for 0% -> 16%
where the time goes in v5:
time: 173 us; the launch traced here: 172 us
  waiting for transfers between devices  75.3 us (44%)
  Pallas kernels  27.6 us (16%)
  starting transfers between devices  23.3 us (13%)
  between operations  15.9 us (9%)
  local copies, waits for them, and re-layouts  12.1 us (7%)
  matrix products  10.7 us (6%)
  other arithmetic  7.29 us (4%)
    all_gather x1, waiting for transfers between devices, body(): whole_panel = lax.all_gather(design, 'row', axis=0, tiled=True)  63.4 us
    pallas_call x2, Pallas kernels, normal_rows(): pl.pallas_call(kernel, grid=(width // tile_cols, rows // tile_rows), in_s...  27.6 us
    ppermute x4, starting transfers between devices, tree_broadcast(): arrived = lax.ppermute(block, ('row', 'col'), pairs)  13.2 us
    ppermute x2, waiting for transfers between devices, swap(): return lax.ppermute(block, axis, [(i, i ^ bit) for i in range(count)])  10.8 us
    ppermute x7, starting transfers between devices, shift_sum(): lax.ppermute(block, axis, [(i, (i + shift) % count) for i in range(count)])  9.95 us
    select_n x4, other arithmetic, tree_broadcast(): jnp.where((offset & ~done == 0) & (offset & bit != 0), arrived, block)  4.44 us
    unnamed x27, local copies, waits for them, and re-layouts  4.25 us
  transfers between devices with their start and end apart: 14, of which 4 were waited for; matrix products, arithmetic and copies ran while one was open for 8% of the time, Pallas kernels for 16%

profile of v5, /device:TPU:0, one launch (start us, length us, event | category | flops | bytes accessed | tf_op | source)
XLA Modules:
  0.0 172.1 jit_solution(16196136024311553586)
XLA Ops:
  7.2 0.0 all-gather.2.cloned.1.call-start
  7.2 0.7 all-gather.2.cloned.1.call-update
  7.9 0.7 concatenate.6
  8.6 0.1 broadcast_bitcast_fusion
  8.7 0.1 copy.10
  8.8 1.2 reshape.20
  10.0 63.4 %all-gather.2.cloned.1.call-done = bf16[256,6144]{1,0:T(8,128)(2,1)} async-done(((bf16[32,6144]{1,0:T(8,128)(2,1)}), bf16[256,6144]{1,0:T(8,128)(2,1)}) %all-gather.2.cloned.1.call-update) | async-done | bytes 3145744 | tf_op jit(solution)/shard_map/all_gather | solution.py:133
  73.4 3.0 %fusion.1 = (f32[6144]{0:T(1024)S(1)}, bf16[256,6144]{1,0:T(8,128)(2,1)S(1)}) fusion(bf16[256,6144]{1,0:T(8,128)(2,1)} %all-gather.2.cloned.1.call-done, f32[256,511]{1,0:T(8,128)} %reshape.20), kind=kOutput, calls=%fused_computation.4 | convolution fusion | flops 811853824 | bytes 6578176 | tf_op jit(solution)/shard_map/dot_general | solution.py:134
  76.4 1.2 constant_dynamic-slice_fusion.1
  77.6 4.3 %collective-permute-start = (bf16[256,1536]{1,0:T(8,128)(2,1)}, bf16[256,1536]{1,0:T(8,128)(2,1)}, u32[]{:S(2)}, u32[]{:S(2)}) collective-permute-start(bf16[256,1536]{1,0:T(8,128)(2,1)} %get-tuple-element.22), channel_id=1, source_target_pairs={{0,2},{4,6},{9,11},{13,15},{18,16},{22,20},{27,25},{31,29}} | collective-permute-start | bytes 2359304 | tf_op jit(solution)/shard_map/ppermute | solution.py:68
  81.9 3.4 %fusion = f32[256,256]{1,0:T(8,128)S(1)} fusion(bf16[256,6144]{1,0:T(8,128)(2,1)S(1)} %get-tuple-element.27.right_ref, f32[6144]{0:T(1024)S(1)} %broadcast_add_fusion), kind=kOutput, calls=%fused_computation.2 | convolution fusion | flops 4834983936 | bytes 3432448 | tf_op jit(solution)/shard_map/dot_general | solution.py:142
  85.3 0.1 collective-permute-start.1
  85.4 1.5 collective-permute-done.1
  87.0 0.1 collective-permute-start.2
  87.1 9.3 %collective-permute-done.2 = f32[256,256]{1,0:T(8,128)} collective-permute-done((f32[256,256]{1,0:T(8,128)S(1)}, f32[256,256]{1,0:T(8,128)}, u32[]{:S(2)}, u32[]{:S(2)}) %collective-permute-start.2) | collective-permute-done | bytes 262176 | tf_op jit(solution)/shard_map/ppermute | solution.py:25
  96.3 1.7 add.85
  98.0 0.0 collective-permute-done
  98.0 2.1 %broadcast_select_fusion.1 = bf16[256,1536]{1,0:T(8,128)(2,1)} fusion(bf16[256,1536]{1,0:T(8,128)(2,1)} %collective-permute-done, bf16[256,1536]{1,0:T(8,128)(2,1)} %get-tuple-element.22, pred[]{:T(512)S(6)} %and.43), kind=kLoop, calls=%fused_computation.16 | loop fusion | flops 393216 | bytes 2359297 | tf_op jit(solution)/shard_map/jit(_where)/select_n | solution.py:70
  100.1 2.2 %collective-permute-start.4 = (bf16[256,1536]{1,0:T(8,128)(2,1)}, bf16[256,1536]{1,0:T(8,128)(2,1)}, u32[]{:S(2)}, u32[]{:S(2)}) collective-permute-start(bf16[256,1536]{1,0:T(8,128)(2,1)} %broadcast_select_fusion.1), channel_id=1, source_target_pairs={{0,1},{2,3},{4,5},{6,7},{9,8},{11,10},{13,12},{15,14},{16,17},{18,... | collective-permute-start | bytes 2359304 | tf_op jit(solution)/shard_map/ppermute | solution.py:68
  102.3 5.4 %collective-permute-start.3 = (bf16[256,1536]{1,0:T(8,128)(2,1)}, bf16[256,1536]{1,0:T(8,128)(2,1)}, u32[]{:S(2)}, u32[]{:S(2)}) collective-permute-start(bf16[256,1536]{1,0:T(8,128)(2,1)} %get-tuple-element.13), channel_id=1, source_target_pairs={{0,2},{4,6},{9,11},{13,15},{18,16},{22,20},{27,25},{31,29}} | collective-permute-start | bytes 2359304 | tf_op jit(solution)/shard_map/ppermute | solution.py:68
  107.7 0.0 collective-permute-done.4
  107.7 2.1 %broadcast_select_fusion.3 = bf16[256,1536]{1,0:T(8,128)(2,1)} fusion(bf16[256,1536]{1,0:T(8,128)(2,1)} %collective-permute-done.4, bf16[256,1536]{1,0:T(8,128)(2,1)} %broadcast_select_fusion.1, pred[]{:T(512)S(6)} %and.40), kind=kLoop, calls=%fused_computation.18 | loop fusion | flops 393216 | bytes 2359297 | tf_op jit(solution)/shard_map/jit(_where)/select_n | solution.py:70
  109.8 2.3 %copy.8.left_ref = bf16[1536,256]{1,0:T(8,128)(2,1)} copy(bf16[1536,256]{0,1:T(8,128)(2,1)} %bitcast.24) | data formatting | bytes 1572864 | tf_op jit(solution)/shard_map/transpose | solution.py:160
  112.1 1.1 copy-done.1
  113.2 13.8 %shard_map.68.rest_0_ = f32[3072,6144]{1,0:T(8,128)} custom-call(bf16[1536,256]{1,0:T(8,128)(2,1)S(1)} %copy-done.1, bf16[256,6144]{1,0:T(8,128)(2,1)S(1)} %get-tuple-element.27.right_ref), custom_call_target="tpu_custom_call" | custom-call | flops 4831838208 | bytes 41680896 | tf_op jit(solution)/shard_map/pallas_call | solution.py:103
  127.0 0.0 collective-permute-done.3
  127.0 0.0 copy-done.6
  127.0 0.1 broadcast_select_fusion
  127.1 1.3 collective-permute-start.5
  129.8 0.0 copy-done.5
  129.8 0.1 constant_dynamic-update-slice_fusion.1
  129.9 0.0 copy-start.8
  129.9 0.4 collective-permute-done.5
  130.3 0.1 broadcast_select_fusion.2
  130.4 0.0 copy-start.4
  130.4 0.9 copy-done.4
  131.3 0.1 constant_dynamic-update-slice_fusion
  131.4 0.0 copy-start.2
  131.4 0.3 multiply_reduce_fusion
  131.8 0.0 copy-start.10
  131.8 0.8 copy-done.2
  132.6 0.0 copy-done.8
  132.6 1.4 fusion.8
  134.0 0.2 collective-permute-start.10
  134.2 0.7 collective-permute-start.11
  135.2 1.8 %collective-permute-start.12 = (f32[256,32]{0,1:T(8,128)S(1)}, f32[256,32]{0,1:T(8,128)S(1)}, u32[]{:S(2)}, u32[]{:S(2)}) collective-permute-start(f32[256,32]{0,1:T(8,128)S(1)} %fusion.8), channel_id=1, source_target_pairs={{0,28},{4,0},{8,4},{12,8},{16,12},{20,16},{24,20},{28,24},{1,29},{... | collective-permute-start | bytes 98312 | tf_op jit(solution)/shard_map/ppermute | solution.py:42
  136.9 0.6 collective-permute-start.6
  137.6 1.4 collective-permute-start.7
  139.0 2.3 %copy.9.left_ref = bf16[1536,256]{1,0:T(8,128)(2,1)} copy(bf16[1536,256]{0,1:T(8,128)(2,1)} %bitcast.23) | data formatting | bytes 1572864 | tf_op jit(solution)/shard_map/transpose | solution.py:162
  141.3 0.0 collective-permute-done.10
  141.3 3.3 %collective-permute-start.8 = (f32[256,32]{0,1:T(8,128)S(1)}, f32[256,32]{0,1:T(8,128)S(1)}, u32[]{:S(2)}, u32[]{:S(2)}) collective-permute-start(f32[256,32]{0,1:T(8,128)S(1)} %fusion.8), channel_id=1, source_target_pairs={{0,12},{4,16},{8,20},{12,24},{16,28},{20,0},{24,4},{28,8},{1,13},{... | collective-permute-start | bytes 98312 | tf_op jit(solution)/shard_map/ppermute | solution.py:42
  144.6 0.0 collective-permute-done.11
  144.6 2.0 %collective-permute-start.9 = (f32[256,32]{0,1:T(8,128)S(1)}, f32[256,32]{0,1:T(8,128)S(1)}, u32[]{:S(2)}, u32[]{:S(2)}) collective-permute-start(f32[256,32]{0,1:T(8,128)S(1)} %fusion.8), channel_id=1, source_target_pairs={{0,16},{4,20},{8,24},{12,28},{16,0},{20,4},{24,8},{28,12},{1,17},{... | collective-permute-start | bytes 98312 | tf_op jit(solution)/shard_map/ppermute | solution.py:42
  146.6 1.1 copy-done
  147.7 13.8 %shard_map.69 = f32[3072,6144]{1,0:T(8,128)} custom-call(bf16[1536,256]{1,0:T(8,128)(2,1)S(1)} %copy-done, bf16[256,6144]{1,0:T(8,128)(2,1)S(1)} %get-tuple-element.27.right_ref, f32[3072,6144]{1,0:T(8,128)} %shard_map.68.rest_0_), custom_call_target="tpu_custom_call", output_to_operand_aliasing={{}: (2, {})} | custom-call | flops 4831838208 | bytes 41680896 | tf_op jit(solution)/shard_map/pallas_call | solution.py:103
  161.5 0.0 collective-permute-done.12
  161.5 0.0 collective-permute-done.6
  161.5 0.0 collective-permute-done.7
  161.5 0.0 collective-permute-done.8
  161.6 0.0 collective-permute-done.9
  161.6 0.8 add_add_fusion
  162.4 0.9 convolution_subtract_fusion.1
  163.3 0.3 fusion.7
  163.6 1.6 fusion.5
  (16 shorter events, 0.1 us)
Async XLA Ops:
  7.2 66.2 %all-gather.2.cloned.1.call-start = ((), (), s32[]{:S(2)}) async-start(), calls=%async_computation | async-start | bytes 3538944 | tf_op jit(solution)/shard_map/all_gather | solution.py:133
  77.6 20.4 %collective-permute-start = (bf16[256,1536]{1,0:T(8,128)(2,1)}, bf16[256,1536]{1,0:T(8,128)(2,1)}, u32[]{:S(2)}, u32[]{:S(2)}) collective-permute-start(bf16[256,1536]{1,0:T(8,128)(2,1)} %get-tuple-element.22), channel_id=1, source_target_pairs={{0,2},{4,6},{9,11},{13,15},{18,16},{22,20},{27,25},{31,29}} | collective-permute-start | bytes 2359304 | tf_op jit(solution)/shard_map/ppermute | solution.py:68
  85.3 1.6 collective-permute-start.1
  87.0 9.4 %collective-permute-start.2 = (f32[256,256]{1,0:T(8,128)S(1)}, f32[256,256]{1,0:T(8,128)}, u32[]{:S(2)}, u32[]{:S(2)}) collective-permute-start(f32[256,256]{1,0:T(8,128)S(1)} %add.84), channel_id=1, source_target_pairs={{0,2},{1,3},{2,0},{3,1},{4,6},{5,7},{6,4},{7,5},{8,10},{9,11},{10,... | collective-permute-start | bytes 786440 | tf_op jit(solution)/shard_map/ppermute | solution.py:25
  100.1 7.6 %collective-permute-start.4 = (bf16[256,1536]{1,0:T(8,128)(2,1)}, bf16[256,1536]{1,0:T(8,128)(2,1)}, u32[]{:S(2)}, u32[]{:S(2)}) collective-permute-start(bf16[256,1536]{1,0:T(8,128)(2,1)} %broadcast_select_fusion.1), channel_id=1, source_target_pairs={{0,1},{2,3},{4,5},{6,7},{9,8},{11,10},{13,12},{15,14},{16,17},{18,... | collective-permute-start | bytes 2359304 | tf_op jit(solution)/shard_map/ppermute | solution.py:68
  102.3 24.7 %collective-permute-start.3 = (bf16[256,1536]{1,0:T(8,128)(2,1)}, bf16[256,1536]{1,0:T(8,128)(2,1)}, u32[]{:S(2)}, u32[]{:S(2)}) collective-permute-start(bf16[256,1536]{1,0:T(8,128)(2,1)} %get-tuple-element.13), channel_id=1, source_target_pairs={{0,2},{4,6},{9,11},{13,15},{18,16},{22,20},{27,25},{31,29}} | collective-permute-start | bytes 2359304 | tf_op jit(solution)/shard_map/ppermute | solution.py:68
  112.1 1.1 copy-start.1
  113.2 13.8 %copy-start.6 = (bf16[256,1536]{1,0:T(8,128)(2,1)S(1)}, bf16[256,1536]{1,0:T(8,128)(2,1)}, u32[]{:S(2)}) copy-start(bf16[256,1536]{1,0:T(8,128)(2,1)} %get-tuple-element.13) | copy-start | bytes 2359300
  113.2 16.5 %copy-start.5 = (bf16[256,1536]{1,0:T(8,128)(2,1)S(1)}, bf16[256,1536]{1,0:T(8,128)(2,1)}, u32[]{:S(2)}) copy-start(bf16[256,1536]{1,0:T(8,128)(2,1)} %broadcast_select_fusion.3) | copy-start | bytes 2359300
  127.1 3.2 %collective-permute-start.5 = (bf16[256,1536]{1,0:T(8,128)(2,1)S(1)}, bf16[256,1536]{1,0:T(8,128)(2,1)S(1)}, u32[]{:S(2)}, u32[]{:S(2)}) collective-permute-start(bf16[256,1536]{1,0:T(8,128)(2,1)S(1)} %broadcast_select_fusion), channel_id=1, source_target_pairs={{0,1},{2,3},{4,5},{6,7},{9,8},{11,10},{13,12},{15,14},{16,17},{18,... | collective-permute-start | bytes 2359304 | tf_op jit(solution)/shard_map/ppermute | solution.py:68
  129.9 2.7 %copy-start.8 = (f32[3072,32]{0,1:T(8,128)S(1)}, f32[3072,32]{0,1:T(8,128)}, u32[]{:S(2)}) copy-start(f32[3072,32]{0,1:T(8,128)} %param.7) | copy-start | bytes 1179652
  130.4 0.9 copy-start.4
  131.4 1.2 copy-start.2
  131.8 0.8 copy-start.10
  134.0 7.3 %collective-permute-start.10 = (f32[256,32]{0,1:T(8,128)S(1)}, f32[256,32]{0,1:T(8,128)S(1)}, u32[]{:S(2)}, u32[]{:S(2)}) collective-permute-start(f32[256,32]{0,1:T(8,128)S(1)} %fusion.8), channel_id=1, source_target_pairs={{0,20},{4,24},{8,28},{12,0},{16,4},{20,8},{24,12},{28,16},{1,21},{... | collective-permute-start | bytes 98312 | tf_op jit(solution)/shard_map/ppermute | solution.py:42
  134.2 10.4 %collective-permute-start.11 = (f32[256,32]{0,1:T(8,128)S(1)}, f32[256,32]{0,1:T(8,128)S(1)}, u32[]{:S(2)}, u32[]{:S(2)}) collective-permute-start(f32[256,32]{0,1:T(8,128)S(1)} %fusion.8), channel_id=1, source_target_pairs={{0,24},{4,28},{8,0},{12,4},{16,8},{20,12},{24,16},{28,20},{1,25},{... | collective-permute-start | bytes 98312 | tf_op jit(solution)/shard_map/ppermute | solution.py:42
  135.2 26.4 %collective-permute-start.12 = (f32[256,32]{0,1:T(8,128)S(1)}, f32[256,32]{0,1:T(8,128)S(1)}, u32[]{:S(2)}, u32[]{:S(2)}) collective-permute-start(f32[256,32]{0,1:T(8,128)S(1)} %fusion.8), channel_id=1, source_target_pairs={{0,28},{4,0},{8,4},{12,8},{16,12},{20,16},{24,20},{28,24},{1,29},{... | collective-permute-start | bytes 98312 | tf_op jit(solution)/shard_map/ppermute | solution.py:42
  136.9 24.6 %collective-permute-start.6 = (f32[256,32]{0,1:T(8,128)S(1)}, f32[256,32]{0,1:T(8,128)}, u32[]{:S(2)}, u32[]{:S(2)}) collective-permute-start(f32[256,32]{0,1:T(8,128)S(1)} %fusion.8), channel_id=1, source_target_pairs={{0,4},{4,8},{8,12},{12,16},{16,20},{20,24},{24,28},{28,0},{1,5},{5... | collective-permute-start | bytes 98312 | tf_op jit(solution)/shard_map/ppermute | solution.py:42
  137.6 24.0 %collective-permute-start.7 = (f32[256,32]{0,1:T(8,128)S(1)}, f32[256,32]{0,1:T(8,128)}, u32[]{:S(2)}, u32[]{:S(2)}) collective-permute-start(f32[256,32]{0,1:T(8,128)S(1)} %fusion.8), channel_id=1, source_target_pairs={{0,8},{4,12},{8,16},{12,20},{16,24},{20,28},{24,0},{28,4},{1,9},{5... | collective-permute-start | bytes 98312 | tf_op jit(solution)/shard_map/ppermute | solution.py:42
  139.0 24.3 %copy-start.7 = (f32[256,256]{1,0:T(8,128)S(1)}, f32[256,256]{1,0:T(8,128)}, u32[]{:S(2)}) copy-start(f32[256,256]{1,0:T(8,128)} %add.85) | copy-start | bytes 786436
  141.3 20.2 %collective-permute-start.8 = (f32[256,32]{0,1:T(8,128)S(1)}, f32[256,32]{0,1:T(8,128)S(1)}, u32[]{:S(2)}, u32[]{:S(2)}) collective-permute-start(f32[256,32]{0,1:T(8,128)S(1)} %fusion.8), channel_id=1, source_target_pairs={{0,12},{4,16},{8,20},{12,24},{16,28},{20,0},{24,4},{28,8},{1,13},{... | collective-permute-start | bytes 98312 | tf_op jit(solution)/shard_map/ppermute | solution.py:42
  144.6 16.9 %collective-permute-start.9 = (f32[256,32]{0,1:T(8,128)S(1)}, f32[256,32]{0,1:T(8,128)S(1)}, u32[]{:S(2)}, u32[]{:S(2)}) collective-permute-start(f32[256,32]{0,1:T(8,128)S(1)} %fusion.8), channel_id=1, source_target_pairs={{0,16},{4,20},{8,24},{12,28},{16,0},{20,4},{24,8},{28,12},{1,17},{... | collective-permute-start | bytes 98312 | tf_op jit(solution)/shard_map/ppermute | solution.py:42
  146.6 1.1 copy-start
  147.7 14.6 %copy-start.3 = (bf16[256,3072]{1,0:T(8,128)(2,1)S(1)}, bf16[256,3072]{1,0:T(8,128)(2,1)}, u32[]{:S(2)}) copy-start(bf16[256,3072]{1,0:T(8,128)(2,1)} %copy-done.2) | copy-start | bytes 4718596
  147.7 14.6 %copy-start.9 = (f32[3072,32]{0,1:T(8,128)S(1)}, f32[3072,32]{0,1:T(8,128)}, u32[]{:S(2)}) copy-start(f32[3072,32]{0,1:T(8,128)} %param.7) | copy-start | bytes 1179652
  147.7 15.9 %copy-start.11 = (f32[3072]{0:T(1024)S(1)}, f32[3072]{0:T(1024)}, u32[]{:S(2)}) copy-start(f32[3072]{0:T(1024)} %copy-done.10) | copy-start | bytes 36868
Sparse Core Ops, SparseCore 0:
  10.2 63.1 all-gather.1

commit v6 on v5

--- a/solution.py
+++ b/solution.py
@@ -77,17 +77,19 @@
 
 
 def product_kernel(left_ref, right_ref, out_ref):
-    out_ref[...] = jnp.dot(left_ref[...], right_ref[...], preferred_element_type=jnp.float32)
+    out_ref[...] = lax.dot_general(
+        left_ref[...], right_ref[...], (((0,), (0,)), ((), ())), preferred_element_type=jnp.float32
+    )
 
 
 def normal_rows(left, right, total_rows, first_row, previous):
-    rows, epochs = left.shape
+    epochs, rows = left.shape
     width = right.shape[1]
     tile_rows = 512 if rows % 512 == 0 else rows
     tile_cols = 2048 if width % 2048 == 0 else width
     row_offset = first_row // tile_rows
     in_specs = [
-        pl.BlockSpec((tile_rows, epochs), lambda j, i: (i, 0)),
+        pl.BlockSpec((epochs, tile_rows), lambda j, i: (0, i)),
         pl.BlockSpec((epochs, tile_cols), lambda j, i: (0, j)),
     ]
     operands = [left, right]
@@ -118,7 +120,7 @@
 
 def contract_epochs(left, right):
     return lax.dot_general(
-        left, right, (((0,), (0,)), ((), ())), precision=lax.Precision.HIGHEST
+        left, right, (((0,), (0,)), ((), ())), precision=lax.Precision.HIGH
     )
 
 
@@ -140,7 +142,7 @@
         white_wide = white.astype(jnp.float32)
         panel_jacobi = jnp.sum(jnp.square(white_wide), axis=0) + 1e-06
         coupling = jnp.dot(
-            white_wide / panel_jacobi[None, :], white_wide.T, precision=lax.Precision.HIGHEST
+            white_wide / panel_jacobi[None, :], white_wide.T, precision=lax.Precision.HIGH
         )
         return tree_sum(coupling, "col")
 
@@ -157,9 +159,9 @@
     panel_second, normal_tile = tree_broadcast(
         held["second"],
         fold_ratio,
-        lambda: normal_rows(panel_first.T, white, row_width, 0, None),
-    )
-    normal_tile = normal_rows(panel_second.T, white, row_width, half_rows, normal_tile)
+        lambda: normal_rows(panel_first, white, row_width, 0, None),
+    )
+    normal_tile = normal_rows(panel_second, white, row_width, half_rows, normal_tile)
     panel = jnp.concatenate([panel_first, panel_second], axis=1)
     panel_wide = panel.astype(jnp.float32)
     jacobi = (jnp.sum(jnp.square(panel_wide), axis=0) + 1e-06)[:, None]
@@ -170,7 +172,7 @@
     residual = probes
     scaled = residual / jacobi
     direction = scaled / center_value
-    scaled_image = shift_sum(jnp.dot(panel_wide, scaled, precision=lax.Precision.HIGHEST), "row")
+    scaled_image = shift_sum(jnp.dot(panel_wide, scaled, precision=lax.Precision.HIGH), "row")
     image = scaled_image / center_value
     solution = jnp.zeros_like(residual)
     for sweep_index in range(SWEEPS):
@@ -182,7 +184,7 @@
         )
         if sweep_index + 1 < SWEEPS:
             scaled_image = scaled_image - jnp.dot(
-                coupling, image, precision=lax.Precision.HIGHEST
+                coupling, image, precision=lax.Precision.HIGH
             )
             image = weight_next * weight_now * image + 2.0 * weight_next / half_width * scaled_image
         weight_now = weight_next

time: 173 us -> 166 us (0.960)
  local copies, waits for them, and re-layouts: 12.1 us -> 6.33 us
  matrix products: 10.7 us -> 8.74 us
    transpose x2 -> x0, local copies, waits for them, and re-layouts: 4.63 us -> none  [the longest x1 2.35 us: body(): normal_tile = normal_rows(panel_second.T, white, row_width, half_rows, no...]
    unnamed x27 -> x21, local copies, waits for them, and re-layouts: 4.25 us -> 3.12 us
  transfers between devices with their start and end apart: 14 -> 14, of which waited for: 4 -> 4; matrix products, arithmetic and copies ran while one was open for 8% -> 4% of each run, Pallas kernels for 16% -> 17%
where the time goes in v6:
time: 166 us; the launch traced here: 165 us
  waiting for transfers between devices  76.9 us (46%)
  Pallas kernels  28 us (17%)
  starting transfers between devices  23.1 us (14%)
  between operations  15.8 us (10%)
  matrix products  8.74 us (5%)
  other arithmetic  6.39 us (4%)
  local copies, waits for them, and re-layouts  6.33 us (4%)
    all_gather x1, waiting for transfers between devices, body(): whole_panel = lax.all_gather(design, 'row', axis=0, tiled=True)  63.4 us
    pallas_call x2, Pallas kernels, normal_rows(): pl.pallas_call(kernel, grid=(width // tile_cols, rows // tile_rows), in_s...  28 us
    ppermute x4, starting transfers between devices, tree_broadcast(): arrived = lax.ppermute(block, ('row', 'col'), pairs)  12.3 us
    ppermute x2, waiting for transfers between devices, swap(): return lax.ppermute(block, axis, [(i, i ^ bit) for i in range(count)])  12.3 us
    ppermute x7, starting transfers between devices, shift_sum(): lax.ppermute(block, axis, [(i, (i + shift) % count) for i in range(count)])  10.6 us
    select_n x4, other arithmetic, tree_broadcast(): jnp.where((offset & ~done == 0) & (offset & bit != 0), arrived, block)  3.52 us
  transfers between devices with their start and end apart: 14, of which 4 were waited for; matrix products, arithmetic and copies ran while one was open for 4% of the time, Pallas kernels for 17%

profile of v6, /device:TPU:0, one launch (start us, length us, event | category | flops | bytes accessed | tf_op | source)
XLA Modules:
  0.0 165.3 jit_solution(6076600170849329409)
XLA Ops:
  7.2 0.0 all-gather.2.cloned.1.call-start
  7.2 0.7 all-gather.2.cloned.1.call-update
  7.9 0.7 concatenate.6
  8.6 0.1 broadcast_bitcast_fusion
  8.7 0.1 copy.8
  8.8 1.2 reshape.20
  10.0 63.4 %all-gather.2.cloned.1.call-done = bf16[256,6144]{1,0:T(8,128)(2,1)} async-done(((bf16[32,6144]{1,0:T(8,128)(2,1)}), bf16[256,6144]{1,0:T(8,128)(2,1)}) %all-gather.2.cloned.1.call-update) | async-done | bytes 3145744 | tf_op jit(solution)/shard_map/all_gather | solution.py:135
  73.4 3.0 %fusion.1 = (f32[6144]{0:T(1024)S(1)}, bf16[256,6144]{1,0:T(8,128)(2,1)S(1)}) fusion(bf16[256,6144]{1,0:T(8,128)(2,1)} %all-gather.2.cloned.1.call-done, f32[256,511]{1,0:T(8,128)} %reshape.20), kind=kOutput, calls=%fused_computation.4 | convolution fusion | flops 811853824 | bytes 6578176 | tf_op jit(solution)/shard_map/dot_general | solution.py:136
  76.4 1.3 constant_dynamic-slice_fusion.1
  77.7 4.3 %collective-permute-start = (bf16[256,1536]{1,0:T(8,128)(2,1)}, bf16[256,1536]{1,0:T(8,128)(2,1)}, u32[]{:S(2)}, u32[]{:S(2)}) collective-permute-start(bf16[256,1536]{1,0:T(8,128)(2,1)} %get-tuple-element.22), channel_id=1, source_target_pairs={{0,2},{4,6},{9,11},{13,15},{18,16},{22,20},{27,25},{31,29}} | collective-permute-start | bytes 2359304 | tf_op jit(solution)/shard_map/ppermute | solution.py:68
  81.9 1.8 %fusion = f32[256,256]{1,0:T(8,128)S(1)} fusion(bf16[256,6144]{1,0:T(8,128)(2,1)S(1)} %get-tuple-element.27.right_ref, f32[6144]{0:T(1024)S(1)} %broadcast_add_fusion), kind=kOutput, calls=%fused_computation.2 | convolution fusion | flops 2419064832 | bytes 3432448 | tf_op jit(solution)/shard_map/dot_general | solution.py:144
  83.8 0.1 collective-permute-start.1
  83.9 1.5 collective-permute-done.1
  85.4 0.1 collective-permute-start.2
  85.5 10.8 %collective-permute-done.2 = f32[256,256]{1,0:T(8,128)} collective-permute-done((f32[256,256]{1,0:T(8,128)S(1)}, f32[256,256]{1,0:T(8,128)}, u32[]{:S(2)}, u32[]{:S(2)}) %collective-permute-start.2) | collective-permute-done | bytes 262176 | tf_op jit(solution)/shard_map/ppermute | solution.py:25
  96.3 1.7 %add.85 = f32[256,256]{1,0:T(8,128)} add(f32[256,256]{1,0:T(8,128)S(1)} %add.84, f32[256,256]{1,0:T(8,128)} %collective-permute-done.2) | non-fusion elementwise | flops 65536 | bytes 786432 | tf_op jit(solution)/shard_map/add | solution.py:34
  98.0 0.0 collective-permute-done
  98.0 2.1 %broadcast_select_fusion.1 = bf16[256,1536]{1,0:T(8,128)(2,1)} fusion(bf16[256,1536]{1,0:T(8,128)(2,1)} %collective-permute-done, bf16[256,1536]{1,0:T(8,128)(2,1)} %get-tuple-element.22, pred[]{:T(512)S(6)} %and.43), kind=kLoop, calls=%fused_computation.16 | loop fusion | flops 393216 | bytes 2359297 | tf_op jit(solution)/shard_map/jit(_where)/select_n | solution.py:70
  100.1 2.2 %collective-permute-start.4 = (bf16[256,1536]{1,0:T(8,128)(2,1)}, bf16[256,1536]{1,0:T(8,128)(2,1)}, u32[]{:S(2)}, u32[]{:S(2)}) collective-permute-start(bf16[256,1536]{1,0:T(8,128)(2,1)} %broadcast_select_fusion.1), channel_id=1, source_target_pairs={{0,1},{2,3},{4,5},{6,7},{9,8},{11,10},{13,12},{15,14},{16,17},{18,... | collective-permute-start | bytes 2359304 | tf_op jit(solution)/shard_map/ppermute | solution.py:68
  102.3 4.5 %collective-permute-start.3 = (bf16[256,1536]{1,0:T(8,128)(2,1)}, bf16[256,1536]{1,0:T(8,128)(2,1)S(1)}, u32[]{:S(2)}, u32[]{:S(2)}) collective-permute-start(bf16[256,1536]{1,0:T(8,128)(2,1)} %get-tuple-element.13), channel_id=1, source_target_pairs={{0,2},{4,6},{9,11},{13,15},{18,16},{22,20},{27,25},{31,29}} | collective-permute-start | bytes 2359304 | tf_op jit(solution)/shard_map/ppermute | solution.py:68
  106.9 0.0 collective-permute-done.4
  106.9 1.2 broadcast_select_fusion.3.left_ref
  108.1 0.0 copy-start.4
  108.1 14.0 %shard_map.68.rest_0_ = f32[3072,6144]{1,0:T(8,128)} custom-call(bf16[256,1536]{1,0:T(8,128)(2,1)S(1)} %broadcast_select_fusion.3.left_ref, bf16[256,6144]{1,0:T(8,128)(2,1)S(1)} %get-tuple-element.27.right_ref), custom_call_target="tpu_custom_call" | custom-call | flops 4831838208 | bytes 41680896 | tf_op jit(solution)/shard_map/pallas_call | solution.py:105
  122.1 0.0 collective-permute-done.3
  122.1 0.0 copy-done.4
  122.1 0.1 broadcast_select_fusion
  122.2 1.3 collective-permute-start.5
  124.9 0.1 constant_dynamic-update-slice_fusion.1
  125.0 0.0 copy-start.6
  125.0 0.4 collective-permute-done.5
  125.4 0.1 broadcast_select_fusion.2.left_ref
  125.5 0.1 constant_dynamic-update-slice_fusion
  125.6 0.0 copy-start
  125.6 0.9 copy-done
  126.5 0.3 multiply_reduce_fusion
  126.9 0.0 copy-start.7
  126.9 0.8 copy-done.2
  127.7 0.0 copy-done.6
  127.7 1.6 fusion.8
  129.3 0.0 copy-done.7
  129.3 0.8 collective-permute-start.10
  130.1 0.0 collective-permute-start.11
  130.4 2.4 %collective-permute-start.12 = (f32[256,32]{0,1:T(8,128)}, f32[256,32]{0,1:T(8,128)S(1)}, u32[]{:S(2)}, u32[]{:S(2)}) collective-permute-start(f32[256,32]{0,1:T(8,128)} %fusion.8), channel_id=1, source_target_pairs={{0,28},{4,0},{8,4},{12,8},{16,12},{20,16},{24,20},{28,24},{1,29},{... | collective-permute-start | bytes 98312 | tf_op jit(solution)/shard_map/ppermute | solution.py:42
  132.8 0.6 collective-permute-start.6
  133.4 1.4 collective-permute-start.7
  134.8 0.0 collective-permute-done.10
  134.8 2.7 %collective-permute-start.8 = (f32[256,32]{0,1:T(8,128)}, f32[256,32]{0,1:T(8,128)S(1)}, u32[]{:S(2)}, u32[]{:S(2)}) collective-permute-start(f32[256,32]{0,1:T(8,128)} %fusion.8), channel_id=1, source_target_pairs={{0,12},{4,16},{8,20},{12,24},{16,28},{20,0},{24,4},{28,8},{1,13},{... | collective-permute-start | bytes 98312 | tf_op jit(solution)/shard_map/ppermute | solution.py:42
  137.5 0.0 collective-permute-done.11
  137.5 2.6 %collective-permute-start.9 = (f32[256,32]{0,1:T(8,128)}, f32[256,32]{0,1:T(8,128)S(1)}, u32[]{:S(2)}, u32[]{:S(2)}) collective-permute-start(f32[256,32]{0,1:T(8,128)} %fusion.8), channel_id=1, source_target_pairs={{0,16},{4,20},{8,24},{12,28},{16,0},{20,4},{24,8},{28,12},{1,17},{... | collective-permute-start | bytes 98312 | tf_op jit(solution)/shard_map/ppermute | solution.py:42
  140.1 1.1 copy-done.1
  141.3 14.0 %shard_map.69 = f32[3072,6144]{1,0:T(8,128)} custom-call(bf16[256,1536]{1,0:T(8,128)(2,1)S(1)} %copy-done.1, bf16[256,6144]{1,0:T(8,128)(2,1)S(1)} %get-tuple-element.27.right_ref, f32[3072,6144]{1,0:T(8,128)} %shard_map.68.rest_0_), custom_call_target="tpu_custom_call", output_to_operand_aliasing={{}: (2, {})} | custom-call | flops 4831838208 | bytes 41680896 | tf_op jit(solution)/shard_map/pallas_call | solution.py:105
  155.3 0.0 collective-permute-done.12
  155.3 0.0 collective-permute-done.6
  155.3 0.0 collective-permute-done.7
  155.3 0.0 collective-permute-done.8
  155.3 0.0 collective-permute-done.9
  155.3 0.8 add_add_fusion
  156.1 0.0 copy-done.3
  156.1 0.6 convolution_subtract_fusion.1
  156.7 0.0 copy-done.5
  156.8 0.3 fusion.7
  157.0 0.0 copy-done.8
  157.0 1.4 fusion.5
  (8 shorter events, 0.1 us)
Async XLA Ops:
  7.2 66.2 %all-gather.2.cloned.1.call-start = ((), (), s32[]{:S(2)}) async-start(), calls=%async_computation | async-start | bytes 3538944 | tf_op jit(solution)/shard_map/all_gather | solution.py:135
  77.7 20.4 %collective-permute-start = (bf16[256,1536]{1,0:T(8,128)(2,1)}, bf16[256,1536]{1,0:T(8,128)(2,1)}, u32[]{:S(2)}, u32[]{:S(2)}) collective-permute-start(bf16[256,1536]{1,0:T(8,128)(2,1)} %get-tuple-element.22), channel_id=1, source_target_pairs={{0,2},{4,6},{9,11},{13,15},{18,16},{22,20},{27,25},{31,29}} | collective-permute-start | bytes 2359304 | tf_op jit(solution)/shard_map/ppermute | solution.py:68
  83.8 1.6 collective-permute-start.1
  85.4 10.9 %collective-permute-start.2 = (f32[256,256]{1,0:T(8,128)S(1)}, f32[256,256]{1,0:T(8,128)}, u32[]{:S(2)}, u32[]{:S(2)}) collective-permute-start(f32[256,256]{1,0:T(8,128)S(1)} %add.84), channel_id=1, source_target_pairs={{0,2},{1,3},{2,0},{3,1},{4,6},{5,7},{6,4},{7,5},{8,10},{9,11},{10,... | collective-permute-start | bytes 786440 | tf_op jit(solution)/shard_map/ppermute | solution.py:25
  100.1 6.7 %collective-permute-start.4 = (bf16[256,1536]{1,0:T(8,128)(2,1)}, bf16[256,1536]{1,0:T(8,128)(2,1)}, u32[]{:S(2)}, u32[]{:S(2)}) collective-permute-start(bf16[256,1536]{1,0:T(8,128)(2,1)} %broadcast_select_fusion.1), channel_id=1, source_target_pairs={{0,1},{2,3},{4,5},{6,7},{9,8},{11,10},{13,12},{15,14},{16,17},{18,... | collective-permute-start | bytes 2359304 | tf_op jit(solution)/shard_map/ppermute | solution.py:68
  102.3 19.8 %collective-permute-start.3 = (bf16[256,1536]{1,0:T(8,128)(2,1)}, bf16[256,1536]{1,0:T(8,128)(2,1)S(1)}, u32[]{:S(2)}, u32[]{:S(2)}) collective-permute-start(bf16[256,1536]{1,0:T(8,128)(2,1)} %get-tuple-element.13), channel_id=1, source_target_pairs={{0,2},{4,6},{9,11},{13,15},{18,16},{22,20},{27,25},{31,29}} | collective-permute-start | bytes 2359304 | tf_op jit(solution)/shard_map/ppermute | solution.py:68
  108.1 14.0 %copy-start.4 = (bf16[256,1536]{1,0:T(8,128)(2,1)S(1)}, bf16[256,1536]{1,0:T(8,128)(2,1)}, u32[]{:S(2)}) copy-start(bf16[256,1536]{1,0:T(8,128)(2,1)} %get-tuple-element.13) | copy-start | bytes 2359300
  122.2 3.2 %collective-permute-start.5 = (bf16[256,1536]{1,0:T(8,128)(2,1)S(1)}, bf16[256,1536]{1,0:T(8,128)(2,1)S(1)}, u32[]{:S(2)}, u32[]{:S(2)}) collective-permute-start(bf16[256,1536]{1,0:T(8,128)(2,1)S(1)} %broadcast_select_fusion), channel_id=1, source_target_pairs={{0,1},{2,3},{4,5},{6,7},{9,8},{11,10},{13,12},{15,14},{16,17},{18,... | collective-permute-start | bytes 2359304 | tf_op jit(solution)/shard_map/ppermute | solution.py:68
  125.0 2.7 %copy-start.6 = (f32[3072,32]{0,1:T(8,128)S(1)}, f32[3072,32]{0,1:T(8,128)}, u32[]{:S(2)}) copy-start(f32[3072,32]{0,1:T(8,128)} %param.7) | copy-start | bytes 1179652
  125.6 0.9 copy-start
  126.5 1.2 copy-start.2
  126.9 2.5 %copy-start.7 = (f32[3072]{0:T(1024)}, f32[3072]{0:T(1024)S(1)}, u32[]{:S(2)}) copy-start(f32[3072]{0:T(1024)S(1)} %get-tuple-element.25) | copy-start | bytes 36868
  129.3 5.5 %collective-permute-start.10 = (f32[256,32]{0,1:T(8,128)}, f32[256,32]{0,1:T(8,128)}, u32[]{:S(2)}, u32[]{:S(2)}) collective-permute-start(f32[256,32]{0,1:T(8,128)} %fusion.8), channel_id=1, source_target_pairs={{0,20},{4,24},{8,28},{12,0},{16,4},{20,8},{24,12},{28,16},{1,21},{... | collective-permute-start | bytes 98312 | tf_op jit(solution)/shard_map/ppermute | solution.py:42
  130.1 7.4 %collective-permute-start.11 = (f32[256,32]{0,1:T(8,128)}, f32[256,32]{0,1:T(8,128)}, u32[]{:S(2)}, u32[]{:S(2)}) collective-permute-start(f32[256,32]{0,1:T(8,128)} %fusion.8), channel_id=1, source_target_pairs={{0,24},{4,28},{8,0},{12,4},{16,8},{20,12},{24,16},{28,20},{1,25},{... | collective-permute-start | bytes 98312 | tf_op jit(solution)/shard_map/ppermute | solution.py:42
  130.4 24.9 %collective-permute-start.12 = (f32[256,32]{0,1:T(8,128)}, f32[256,32]{0,1:T(8,128)S(1)}, u32[]{:S(2)}, u32[]{:S(2)}) collective-permute-start(f32[256,32]{0,1:T(8,128)} %fusion.8), channel_id=1, source_target_pairs={{0,28},{4,0},{8,4},{12,8},{16,12},{20,16},{24,20},{28,24},{1,29},{... | collective-permute-start | bytes 98312 | tf_op jit(solution)/shard_map/ppermute | solution.py:42
  132.8 22.5 %collective-permute-start.6 = (f32[256,32]{0,1:T(8,128)}, f32[256,32]{0,1:T(8,128)S(1)}, u32[]{:S(2)}, u32[]{:S(2)}) collective-permute-start(f32[256,32]{0,1:T(8,128)} %fusion.8), channel_id=1, source_target_pairs={{0,4},{4,8},{8,12},{12,16},{16,20},{20,24},{24,28},{28,0},{1,5},{5... | collective-permute-start | bytes 98312 | tf_op jit(solution)/shard_map/ppermute | solution.py:42
  133.4 21.8 %collective-permute-start.7 = (f32[256,32]{0,1:T(8,128)}, f32[256,32]{0,1:T(8,128)S(1)}, u32[]{:S(2)}, u32[]{:S(2)}) collective-permute-start(f32[256,32]{0,1:T(8,128)} %fusion.8), channel_id=1, source_target_pairs={{0,8},{4,12},{8,16},{12,20},{16,24},{20,28},{24,0},{28,4},{1,9},{5... | collective-permute-start | bytes 98312 | tf_op jit(solution)/shard_map/ppermute | solution.py:42
  134.8 20.4 %collective-permute-start.8 = (f32[256,32]{0,1:T(8,128)}, f32[256,32]{0,1:T(8,128)S(1)}, u32[]{:S(2)}, u32[]{:S(2)}) collective-permute-start(f32[256,32]{0,1:T(8,128)} %fusion.8), channel_id=1, source_target_pairs={{0,12},{4,16},{8,20},{12,24},{16,28},{20,0},{24,4},{28,8},{1,13},{... | collective-permute-start | bytes 98312 | tf_op jit(solution)/shard_map/ppermute | solution.py:42
  137.5 17.8 %collective-permute-start.9 = (f32[256,32]{0,1:T(8,128)}, f32[256,32]{0,1:T(8,128)S(1)}, u32[]{:S(2)}, u32[]{:S(2)}) collective-permute-start(f32[256,32]{0,1:T(8,128)} %fusion.8), channel_id=1, source_target_pairs={{0,16},{4,20},{8,24},{12,28},{16,0},{20,4},{24,8},{28,12},{1,17},{... | collective-permute-start | bytes 98312 | tf_op jit(solution)/shard_map/ppermute | solution.py:42
  140.1 1.1 copy-start.1
  141.3 14.8 %copy-start.3 = (bf16[256,3072]{1,0:T(8,128)(2,1)S(1)}, bf16[256,3072]{1,0:T(8,128)(2,1)}, u32[]{:S(2)}) copy-start(bf16[256,3072]{1,0:T(8,128)(2,1)} %copy-done.2) | copy-start | bytes 4718596
  141.3 15.5 %copy-start.5 = (f32[256,256]{1,0:T(8,128)S(1)}, f32[256,256]{1,0:T(8,128)}, u32[]{:S(2)}) copy-start(f32[256,256]{1,0:T(8,128)} %add.85) | copy-start | bytes 786436
  141.3 15.8 %copy-start.8 = (f32[3072]{0:T(1024)S(1)}, f32[3072]{0:T(1024)}, u32[]{:S(2)}) copy-start(f32[3072]{0:T(1024)} %copy-done.7) | copy-start | bytes 36868
Sparse Core Ops, SparseCore 0:
  10.2 63.1 all-gather.1

commit v7 on v6

--- a/solution.py
+++ b/solution.py
@@ -172,7 +172,7 @@
     residual = probes
     scaled = residual / jacobi
     direction = scaled / center_value
-    scaled_image = shift_sum(jnp.dot(panel_wide, scaled, precision=lax.Precision.HIGH), "row")
+    scaled_image = tree_sum(jnp.dot(panel_wide, scaled, precision=lax.Precision.HIGH), "row")
     image = scaled_image / center_value
     solution = jnp.zeros_like(residual)
     for sweep_index in range(SWEEPS):

time: 166 us -> 164 us (0.988)
  starting transfers between devices: 23.1 us -> 14 us
  waiting for transfers between devices: 76.9 us -> 84.2 us
    ppermute x7 -> x0, starting transfers between devices: 10.6 us -> none  [shift_sum(): lax.ppermute(block, axis, [(i, (i + shift) % count) for i in range(count)])]
    ppermute x2 -> x5, waiting for transfers between devices: 12.3 us -> 19.7 us  [swap(): return lax.ppermute(block, axis, [(i, i ^ bit) for i in range(count)])]
  transfers between devices with their start and end apart: 14 -> 10, of which waited for: 4 -> 6; matrix products, arithmetic and copies ran while one was open for 4% -> 4% of each run, Pallas kernels for 17% -> 17%
where the time goes in v7:
time: 164 us; the launch traced here: 163 us
  waiting for transfers between devices  84.2 us (51%)
  Pallas kernels  28 us (17%)
  between operations  15.8 us (10%)
  starting transfers between devices  14 us (9%)
  matrix products  8.12 us (5%)
  other arithmetic  6.97 us (4%)
  local copies, waits for them, and re-layouts  6.34 us (4%)
    all_gather x1, waiting for transfers between devices, body(): whole_panel = lax.all_gather(design, 'row', axis=0, tiled=True)  63.4 us
    pallas_call x2, Pallas kernels, normal_rows(): pl.pallas_call(kernel, grid=(width // tile_cols, rows // tile_rows), in_s...  28 us
    ppermute x5, waiting for transfers between devices, swap(): return lax.ppermute(block, axis, [(i, i ^ bit) for i in range(count)])  19.7 us
    ppermute x4, starting transfers between devices, tree_broadcast(): arrived = lax.ppermute(block, ('row', 'col'), pairs)  12.3 us
    select_n x4, other arithmetic, tree_broadcast(): jnp.where((offset & ~done == 0) & (offset & bit != 0), arrived, block)  3.52 us
  transfers between devices with their start and end apart: 10, of which 6 were waited for; matrix products, arithmetic and copies ran while one was open for 4% of the time, Pallas kernels for 17%

profile of v7, /device:TPU:0, one launch (start us, length us, event | category | flops | bytes accessed | tf_op | source)
XLA Modules:
  0.0 163.4 jit_solution(444402951559208936)
XLA Ops:
  7.2 0.0 all-gather.2.cloned.1.call-start
  7.2 0.7 all-gather.2.cloned.1.call-update
  7.9 0.7 concatenate.6
  8.6 0.1 broadcast_bitcast_fusion
  8.7 0.1 copy.8
  8.8 1.2 reshape.20
  10.0 63.4 %all-gather.2.cloned.1.call-done = bf16[256,6144]{1,0:T(8,128)(2,1)} async-done(((bf16[32,6144]{1,0:T(8,128)(2,1)}), bf16[256,6144]{1,0:T(8,128)(2,1)}) %all-gather.2.cloned.1.call-update) | async-done | bytes 3145744 | tf_op jit(solution)/shard_map/all_gather | solution.py:135
  73.4 3.0 %fusion.1 = (f32[6144]{0:T(1024)S(1)}, bf16[256,6144]{1,0:T(8,128)(2,1)S(1)}) fusion(bf16[256,6144]{1,0:T(8,128)(2,1)} %all-gather.2.cloned.1.call-done, f32[256,511]{1,0:T(8,128)} %reshape.20), kind=kOutput, calls=%fused_computation.4 | convolution fusion | flops 811853824 | bytes 6578176 | tf_op jit(solution)/shard_map/dot_general | solution.py:136
  76.4 1.3 constant_dynamic-slice_fusion.1
  77.7 4.3 %collective-permute-start = (bf16[256,1536]{1,0:T(8,128)(2,1)}, bf16[256,1536]{1,0:T(8,128)(2,1)}, u32[]{:S(2)}, u32[]{:S(2)}) collective-permute-start(bf16[256,1536]{1,0:T(8,128)(2,1)} %get-tuple-element.22), channel_id=1, source_target_pairs={{0,2},{4,6},{9,11},{13,15},{18,16},{22,20},{27,25},{31,29}} | collective-permute-start | bytes 2359304 | tf_op jit(solution)/shard_map/ppermute | solution.py:68
  81.9 1.8 %fusion = f32[256,256]{1,0:T(8,128)S(1)} fusion(bf16[256,6144]{1,0:T(8,128)(2,1)S(1)} %get-tuple-element.27.right_ref, f32[6144]{0:T(1024)S(1)} %broadcast_add_fusion), kind=kOutput, calls=%fused_computation.2 | convolution fusion | flops 2419064832 | bytes 3432448 | tf_op jit(solution)/shard_map/dot_general | solution.py:144
  83.8 0.1 collective-permute-start.1
  83.9 1.5 collective-permute-done.1
  85.4 0.1 collective-permute-start.2
  85.5 10.8 %collective-permute-done.2 = f32[256,256]{1,0:T(8,128)} collective-permute-done((f32[256,256]{1,0:T(8,128)S(1)}, f32[256,256]{1,0:T(8,128)}, u32[]{:S(2)}, u32[]{:S(2)}) %collective-permute-start.2) | collective-permute-done | bytes 262176 | tf_op jit(solution)/shard_map/ppermute | solution.py:25
  96.3 1.7 %add.73 = f32[256,256]{1,0:T(8,128)} add(f32[256,256]{1,0:T(8,128)S(1)} %add.72, f32[256,256]{1,0:T(8,128)} %collective-permute-done.2) | non-fusion elementwise | flops 65536 | bytes 786432 | tf_op jit(solution)/shard_map/add | solution.py:34
  98.0 0.0 collective-permute-done
  98.0 2.1 %broadcast_select_fusion.1 = bf16[256,1536]{1,0:T(8,128)(2,1)} fusion(bf16[256,1536]{1,0:T(8,128)(2,1)} %collective-permute-done, bf16[256,1536]{1,0:T(8,128)(2,1)} %get-tuple-element.22, pred[]{:T(512)S(6)} %and.43), kind=kLoop, calls=%fused_computation.16 | loop fusion | flops 393216 | bytes 2359297 | tf_op jit(solution)/shard_map/jit(_where)/select_n | solution.py:70
  100.1 2.2 %collective-permute-start.4 = (bf16[256,1536]{1,0:T(8,128)(2,1)}, bf16[256,1536]{1,0:T(8,128)(2,1)}, u32[]{:S(2)}, u32[]{:S(2)}) collective-permute-start(bf16[256,1536]{1,0:T(8,128)(2,1)} %broadcast_select_fusion.1), channel_id=1, source_target_pairs={{0,1},{2,3},{4,5},{6,7},{9,8},{11,10},{13,12},{15,14},{16,17},{18,... | collective-permute-start | bytes 2359304 | tf_op jit(solution)/shard_map/ppermute | solution.py:68
  102.3 4.5 %collective-permute-start.3 = (bf16[256,1536]{1,0:T(8,128)(2,1)}, bf16[256,1536]{1,0:T(8,128)(2,1)S(1)}, u32[]{:S(2)}, u32[]{:S(2)}) collective-permute-start(bf16[256,1536]{1,0:T(8,128)(2,1)} %get-tuple-element.13), channel_id=1, source_target_pairs={{0,2},{4,6},{9,11},{13,15},{18,16},{22,20},{27,25},{31,29}} | collective-permute-start | bytes 2359304 | tf_op jit(solution)/shard_map/ppermute | solution.py:68
  106.9 0.0 collective-permute-done.4
  106.9 1.2 broadcast_select_fusion.3.left_ref
  108.1 0.0 copy-start.4
  108.1 14.0 %shard_map.68.rest_0_ = f32[3072,6144]{1,0:T(8,128)} custom-call(bf16[256,1536]{1,0:T(8,128)(2,1)S(1)} %broadcast_select_fusion.3.left_ref, bf16[256,6144]{1,0:T(8,128)(2,1)S(1)} %get-tuple-element.27.right_ref), custom_call_target="tpu_custom_call" | custom-call | flops 4831838208 | bytes 41680896 | tf_op jit(solution)/shard_map/pallas_call | solution.py:105
  122.1 0.0 collective-permute-done.3
  122.1 0.0 copy-done.4
  122.1 0.1 broadcast_select_fusion
  122.2 1.3 collective-permute-start.5
  124.9 0.1 constant_dynamic-update-slice_fusion.1
  125.0 0.0 copy-start.6
  125.0 0.4 collective-permute-done.5
  125.4 0.1 broadcast_select_fusion.2.left_ref
  125.5 0.1 constant_dynamic-update-slice_fusion
  125.6 0.0 copy-start
  125.6 0.9 copy-done
  126.5 0.0 copy-start.2
  126.5 0.3 multiply_reduce_fusion
  126.9 0.0 copy-start.7
  126.9 0.8 copy-done.2
  127.7 0.0 copy-done.6
  127.7 1.0 fusion.8
  128.7 0.6 collective-permute-start.6
  129.3 3.4 %collective-permute-done.6 = f32[256,32]{0,1:T(8,128)S(1)} collective-permute-done((f32[256,32]{0,1:T(8,128)S(1)}, f32[256,32]{0,1:T(8,128)S(1)}, u32[]{:S(2)}, u32[]{:S(2)}) %collective-permute-start.6) | collective-permute-done | bytes 32800 | tf_op jit(solution)/shard_map/ppermute | solution.py:25
  132.7 0.6 add.77
  133.3 0.0 copy-done.7
  133.3 0.0 collective-permute-start.7
  133.6 4.0 %collective-permute-done.7 = f32[256,32]{0,1:T(8,128)} collective-permute-done((f32[256,32]{0,1:T(8,128)}, f32[256,32]{0,1:T(8,128)}, u32[]{:S(2)}, u32[]{:S(2)}) %collective-permute-start.7) | collective-permute-done | bytes 32800 | tf_op jit(solution)/shard_map/ppermute | solution.py:25
  137.5 0.8 add.78
  138.3 0.8 collective-permute-start.8
  139.1 0.0 copy-start.1
  139.1 1.1 copy-done.1
  140.3 0.0 copy-start.3
  140.3 0.0 copy-start.5
  140.3 0.0 copy-start.8
  140.3 14.0 %shard_map.69 = f32[3072,6144]{1,0:T(8,128)} custom-call(bf16[256,1536]{1,0:T(8,128)(2,1)S(1)} %copy-done.1, bf16[256,6144]{1,0:T(8,128)(2,1)S(1)} %get-tuple-element.27.right_ref, f32[3072,6144]{1,0:T(8,128)} %shard_map.68.rest_0_), custom_call_target="tpu_custom_call", output_to_operand_aliasing={{}: (2, {})} | custom-call | flops 4831838208 | bytes 41680896 | tf_op jit(solution)/shard_map/pallas_call | solution.py:105
  154.3 0.0 collective-permute-done.8
  154.3 0.0 copy-done.3
  154.3 0.6 convolution_subtract_fusion.1
  154.9 0.0 copy-done.5
  154.9 0.3 fusion.7
  155.2 0.0 copy-done.8
  155.2 1.4 fusion.5
  (3 shorter events, 0.0 us)
Async XLA Ops:
  7.2 66.2 %all-gather.2.cloned.1.call-start = ((), (), s32[]{:S(2)}) async-start(), calls=%async_computation | async-start | bytes 3538944 | tf_op jit(solution)/shard_map/all_gather | solution.py:135
  77.7 20.4 %collective-permute-start = (bf16[256,1536]{1,0:T(8,128)(2,1)}, bf16[256,1536]{1,0:T(8,128)(2,1)}, u32[]{:S(2)}, u32[]{:S(2)}) collective-permute-start(bf16[256,1536]{1,0:T(8,128)(2,1)} %get-tuple-element.22), channel_id=1, source_target_pairs={{0,2},{4,6},{9,11},{13,15},{18,16},{22,20},{27,25},{31,29}} | collective-permute-start | bytes 2359304 | tf_op jit(solution)/shard_map/ppermute | solution.py:68
  83.8 1.6 collective-permute-start.1
  85.4 10.9 %collective-permute-start.2 = (f32[256,256]{1,0:T(8,128)S(1)}, f32[256,256]{1,0:T(8,128)}, u32[]{:S(2)}, u32[]{:S(2)}) collective-permute-start(f32[256,256]{1,0:T(8,128)S(1)} %add.72), channel_id=1, source_target_pairs={{0,2},{1,3},{2,0},{3,1},{4,6},{5,7},{6,4},{7,5},{8,10},{9,11},{10,... | collective-permute-start | bytes 786440 | tf_op jit(solution)/shard_map/ppermute | solution.py:25
  100.1 6.7 %collective-permute-start.4 = (bf16[256,1536]{1,0:T(8,128)(2,1)}, bf16[256,1536]{1,0:T(8,128)(2,1)}, u32[]{:S(2)}, u32[]{:S(2)}) collective-permute-start(bf16[256,1536]{1,0:T(8,128)(2,1)} %broadcast_select_fusion.1), channel_id=1, source_target_pairs={{0,1},{2,3},{4,5},{6,7},{9,8},{11,10},{13,12},{15,14},{16,17},{18,... | collective-permute-start | bytes 2359304 | tf_op jit(solution)/shard_map/ppermute | solution.py:68
  102.3 19.8 %collective-permute-start.3 = (bf16[256,1536]{1,0:T(8,128)(2,1)}, bf16[256,1536]{1,0:T(8,128)(2,1)S(1)}, u32[]{:S(2)}, u32[]{:S(2)}) collective-permute-start(bf16[256,1536]{1,0:T(8,128)(2,1)} %get-tuple-element.13), channel_id=1, source_target_pairs={{0,2},{4,6},{9,11},{13,15},{18,16},{22,20},{27,25},{31,29}} | collective-permute-start | bytes 2359304 | tf_op jit(solution)/shard_map/ppermute | solution.py:68
  108.1 14.0 %copy-start.4 = (bf16[256,1536]{1,0:T(8,128)(2,1)S(1)}, bf16[256,1536]{1,0:T(8,128)(2,1)}, u32[]{:S(2)}) copy-start(bf16[256,1536]{1,0:T(8,128)(2,1)} %get-tuple-element.13) | copy-start | bytes 2359300
  122.2 3.2 %collective-permute-start.5 = (bf16[256,1536]{1,0:T(8,128)(2,1)S(1)}, bf16[256,1536]{1,0:T(8,128)(2,1)S(1)}, u32[]{:S(2)}, u32[]{:S(2)}) collective-permute-start(bf16[256,1536]{1,0:T(8,128)(2,1)S(1)} %broadcast_select_fusion), channel_id=1, source_target_pairs={{0,1},{2,3},{4,5},{6,7},{9,8},{11,10},{13,12},{15,14},{16,17},{18,... | collective-permute-start | bytes 2359304 | tf_op jit(solution)/shard_map/ppermute | solution.py:68
  125.0 2.7 %copy-start.6 = (f32[3072,32]{0,1:T(8,128)S(1)}, f32[3072,32]{0,1:T(8,128)}, u32[]{:S(2)}) copy-start(f32[3072,32]{0,1:T(8,128)} %param.7) | copy-start | bytes 1179652
  125.6 0.9 copy-start
  126.5 1.2 copy-start.2
  126.9 6.5 %copy-start.7 = (f32[3072]{0:T(1024)}, f32[3072]{0:T(1024)S(1)}, u32[]{:S(2)}) copy-start(f32[3072]{0:T(1024)S(1)} %get-tuple-element.25) | copy-start | bytes 36868
  128.7 4.0 %collective-permute-start.6 = (f32[256,32]{0,1:T(8,128)S(1)}, f32[256,32]{0,1:T(8,128)S(1)}, u32[]{:S(2)}, u32[]{:S(2)}) collective-permute-start(f32[256,32]{0,1:T(8,128)S(1)} %fusion.8), channel_id=1, source_target_pairs={{0,4},{4,0},{8,12},{12,8},{16,20},{20,16},{24,28},{28,24},{1,5},{5... | collective-permute-start | bytes 98312 | tf_op jit(solution)/shard_map/ppermute | solution.py:25
  133.3 4.2 %collective-permute-start.7 = (f32[256,32]{0,1:T(8,128)}, f32[256,32]{0,1:T(8,128)}, u32[]{:S(2)}, u32[]{:S(2)}) collective-permute-start(f32[256,32]{0,1:T(8,128)} %add.77), channel_id=1, source_target_pairs={{0,8},{4,12},{8,0},{12,4},{16,24},{20,28},{24,16},{28,20},{1,9},{5... | collective-permute-start | bytes 98312 | tf_op jit(solution)/shard_map/ppermute | solution.py:25
  138.3 16.0 %collective-permute-start.8 = (f32[256,32]{0,1:T(8,128)S(1)}, f32[256,32]{0,1:T(8,128)S(1)}, u32[]{:S(2)}, u32[]{:S(2)}) collective-permute-start(f32[256,32]{0,1:T(8,128)S(1)} %add.78), channel_id=1, source_target_pairs={{0,16},{4,20},{8,24},{12,28},{16,0},{20,4},{24,8},{28,12},{1,17},{... | collective-permute-start | bytes 98312 | tf_op jit(solution)/shard_map/ppermute | solution.py:25
  139.1 1.1 copy-start.1
  140.3 14.0 %copy-start.3 = (bf16[256,3072]{1,0:T(8,128)(2,1)S(1)}, bf16[256,3072]{1,0:T(8,128)(2,1)}, u32[]{:S(2)}) copy-start(bf16[256,3072]{1,0:T(8,128)(2,1)} %copy-done.2) | copy-start | bytes 4718596
  140.3 14.6 %copy-start.5 = (f32[256,256]{1,0:T(8,128)S(1)}, f32[256,256]{1,0:T(8,128)}, u32[]{:S(2)}) copy-start(f32[256,256]{1,0:T(8,128)} %add.73) | copy-start | bytes 786436
  140.3 14.9 %copy-start.8 = (f32[3072]{0:T(1024)S(1)}, f32[3072]{0:T(1024)}, u32[]{:S(2)}) copy-start(f32[3072]{0:T(1024)} %copy-done.7) | copy-start | bytes 36868
Sparse Core Ops, SparseCore 0:
  10.2 63.1 all-gather.1

commit v8 on v7

--- a/solution.py
+++ b/solution.py
@@ -153,13 +153,13 @@
         held["second"], block = lax.optimization_barrier((own_slice[:, half_rows:], block))
         return block
 
-    panel_first, coupling = tree_broadcast(
-        own_slice[:, :half_rows], fold_ratio, couple, release_second
-    )
-    panel_second, normal_tile = tree_broadcast(
+    panel_first, _ = tree_broadcast(
+        own_slice[:, :half_rows], fold_ratio, lambda: (), release_second
+    )
+    panel_second, (normal_tile, coupling) = tree_broadcast(
         held["second"],
         fold_ratio,
-        lambda: normal_rows(panel_first, white, row_width, 0, None),
+        lambda: (normal_rows(panel_first, white, row_width, 0, None), couple()),
     )
     normal_tile = normal_rows(panel_second, white, row_width, half_rows, normal_tile)
     panel = jnp.concatenate([panel_first, panel_second], axis=1)

time: 164 us -> 166 us (1.012)
  waiting for transfers between devices: 84.2 us -> 88.8 us
  local copies, waits for them, and re-layouts: 6.34 us -> 4.54 us
    ppermute x4, waiting for transfers between devices: 0.46 us -> 9.44 us  [tree_broadcast(): arrived = lax.ppermute(block, ('row', 'col'), pairs)]
    ppermute x5, waiting for transfers between devices: 19.7 us -> 15.3 us  [swap(): return lax.ppermute(block, axis, [(i, i ^ bit) for i in range(count)])]
    ppermute x5, starting transfers between devices: 1.59 us -> 3.32 us  [swap(): return lax.ppermute(block, axis, [(i, i ^ bit) for i in range(count)])]
    unnamed x21 -> x18, local copies, waits for them, and re-layouts: 3.12 us -> 1.4 us
  transfers between devices with their start and end apart: 10 -> 10, of which waited for: 6 -> 7; matrix products, arithmetic and copies ran while one was open for 4% -> 4% of each run, Pallas kernels for 17% -> 17%
where the time goes in v8:
time: 166 us
  waiting for transfers between devices  88.8 us (53%)
  Pallas kernels  28 us (17%)
  between operations  15.8 us (10%)
  starting transfers between devices  15 us (9%)
  matrix products  8.11 us (5%)
  other arithmetic  5.56 us (3%)
  local copies, waits for them, and re-layouts  4.54 us (3%)
    all_gather x1, waiting for transfers between devices, body(): whole_panel = lax.all_gather(design, 'row', axis=0, tiled=True)  63.4 us
    pallas_call x2, Pallas kernels, normal_rows(): pl.pallas_call(kernel, grid=(width // tile_cols, rows // tile_rows), in_s...  28 us
    ppermute x5, waiting for transfers between devices, swap(): return lax.ppermute(block, axis, [(i, i ^ bit) for i in range(count)])  15.3 us
    ppermute x4, starting transfers between devices, tree_broadcast(): arrived = lax.ppermute(block, ('row', 'col'), pairs)  11.6 us
    ppermute x4, waiting for transfers between devices, tree_broadcast(): arrived = lax.ppermute(block, ('row', 'col'), pairs)  9.44 us
    select_n x4, other arithmetic, tree_broadcast(): jnp.where((offset & ~done == 0) & (offset & bit != 0), arrived, block)  3.5 us
    ppermute x5, starting transfers between devices, swap(): return lax.ppermute(block, axis, [(i, i ^ bit) for i in range(count)])  3.32 us
  transfers between devices with their start and end apart: 10, of which 7 were waited for; matrix products, arithmetic and copies ran while one was open for 4% of the time, Pallas kernels for 17%

profile of v8, /device:TPU:0, one launch (start us, length us, event | category | flops | bytes accessed | tf_op | source)
XLA Modules:
  0.0 165.8 jit_solution(14934006153353504521)
XLA Ops:
  7.2 0.0 all-gather.2.cloned.1.call-start
  7.2 0.7 all-gather.2.cloned.1.call-update
  7.9 0.7 concatenate.6
  8.6 0.1 broadcast_bitcast_fusion
  8.7 0.1 copy.8
  8.8 1.2 reshape.20
  10.0 63.4 %all-gather.2.cloned.1.call-done = bf16[256,6144]{1,0:T(8,128)(2,1)} async-done(((bf16[32,6144]{1,0:T(8,128)(2,1)}), bf16[256,6144]{1,0:T(8,128)(2,1)}) %all-gather.2.cloned.1.call-update) | async-done | bytes 3145744 | tf_op jit(solution)/shard_map/all_gather | solution.py:135
  73.4 3.0 %fusion.1 = (f32[6144]{0:T(1024)S(1)}, bf16[256,6144]{1,0:T(8,128)(2,1)S(1)}) fusion(bf16[256,6144]{1,0:T(8,128)(2,1)} %all-gather.2.cloned.1.call-done, f32[256,511]{1,0:T(8,128)} %reshape.20), kind=kOutput, calls=%fused_computation.4 | convolution fusion | flops 811853824 | bytes 6578176 | tf_op jit(solution)/shard_map/dot_general | solution.py:136
  76.4 1.3 constant_dynamic-slice_fusion.1
  77.7 4.3 %collective-permute-start = (bf16[256,1536]{1,0:T(8,128)(2,1)}, bf16[256,1536]{1,0:T(8,128)(2,1)}, u32[]{:S(2)}, u32[]{:S(2)}) collective-permute-start(bf16[256,1536]{1,0:T(8,128)(2,1)} %get-tuple-element.18), channel_id=1, source_target_pairs={{0,2},{4,6},{9,11},{13,15},{18,16},{22,20},{27,25},{31,29}} | collective-permute-start | bytes 2359304 | tf_op jit(solution)/shard_map/ppermute | solution.py:68
  81.9 8.9 %collective-permute-done = bf16[256,1536]{1,0:T(8,128)(2,1)} collective-permute-done((bf16[256,1536]{1,0:T(8,128)(2,1)}, bf16[256,1536]{1,0:T(8,128)(2,1)}, u32[]{:S(2)}, u32[]{:S(2)}) %collective-permute-start) | collective-permute-done | bytes 786464 | tf_op jit(solution)/shard_map/ppermute | solution.py:68
  90.8 2.1 %broadcast_select_fusion.1 = bf16[256,1536]{1,0:T(8,128)(2,1)} fusion(bf16[256,1536]{1,0:T(8,128)(2,1)} %collective-permute-done, bf16[256,1536]{1,0:T(8,128)(2,1)} %get-tuple-element.18, pred[]{:T(512)S(6)} %and.43), kind=kLoop, calls=%fused_computation.17 | loop fusion | flops 393216 | bytes 2359297 | tf_op jit(solution)/shard_map/jit(_where)/select_n | solution.py:70
  92.9 2.2 %collective-permute-start.2 = (bf16[256,1536]{1,0:T(8,128)(2,1)}, bf16[256,1536]{1,0:T(8,128)(2,1)}, u32[]{:S(2)}, u32[]{:S(2)}) collective-permute-start(bf16[256,1536]{1,0:T(8,128)(2,1)} %broadcast_select_fusion.1), channel_id=1, source_target_pairs={{0,1},{2,3},{4,5},{6,7},{9,8},{11,10},{13,12},{15,14},{16,17},{18,... | collective-permute-start | bytes 2359304 | tf_op jit(solution)/shard_map/ppermute | solution.py:68
  95.1 1.8 %fusion = f32[256,256]{1,0:T(8,128)S(1)} fusion(bf16[256,6144]{1,0:T(8,128)(2,1)S(1)} %get-tuple-element.23.right_ref, f32[6144]{0:T(1024)S(1)} %broadcast_add_fusion), kind=kOutput, calls=%fused_computation.2 | convolution fusion | flops 2419064832 | bytes 3432448 | tf_op jit(solution)/shard_map/dot_general | solution.py:144
  97.0 0.1 collective-permute-start.3
  97.1 1.5 collective-permute-done.3
  98.6 2.5 %collective-permute-start.4 = (f32[256,256]{1,0:T(8,128)S(1)}, f32[256,256]{1,0:T(8,128)}, u32[]{:S(2)}, u32[]{:S(2)}) collective-permute-start(f32[256,256]{1,0:T(8,128)S(1)} %add.72), channel_id=1, source_target_pairs={{0,2},{1,3},{2,0},{3,1},{4,6},{5,7},{6,4},{7,5},{8,10},{9,11},{10,... | collective-permute-start | bytes 786440 | tf_op jit(solution)/shard_map/ppermute | solution.py:25
  101.2 6.7 %collective-permute-done.4 = f32[256,256]{1,0:T(8,128)} collective-permute-done((f32[256,256]{1,0:T(8,128)S(1)}, f32[256,256]{1,0:T(8,128)}, u32[]{:S(2)}, u32[]{:S(2)}) %collective-permute-start.4) | collective-permute-done | bytes 262176 | tf_op jit(solution)/shard_map/ppermute | solution.py:25
  107.9 1.7 %add.73 = f32[256,256]{1,0:T(8,128)} add(f32[256,256]{1,0:T(8,128)S(1)} %add.72, f32[256,256]{1,0:T(8,128)} %collective-permute-done.4) | non-fusion elementwise | flops 65536 | bytes 786432 | tf_op jit(solution)/shard_map/add | solution.py:34
  109.6 3.7 %collective-permute-start.1 = (bf16[256,1536]{1,0:T(8,128)(2,1)}, bf16[256,1536]{1,0:T(8,128)(2,1)S(1)}, u32[]{:S(2)}, u32[]{:S(2)}) collective-permute-start(bf16[256,1536]{1,0:T(8,128)(2,1)} %get-tuple-element.10), channel_id=1, source_target_pairs={{0,2},{4,6},{9,11},{13,15},{18,16},{22,20},{27,25},{31,29}} | collective-permute-start | bytes 2359304 | tf_op jit(solution)/shard_map/ppermute | solution.py:68
  113.2 0.0 collective-permute-done.2
  113.3 1.2 broadcast_select_fusion.3.left_ref
  114.5 0.0 copy-start
  114.5 0.0 copy-start.4
  114.5 14.0 %shard_map.68.rest_0_ = f32[3072,6144]{1,0:T(8,128)} custom-call(bf16[256,1536]{1,0:T(8,128)(2,1)S(1)} %broadcast_select_fusion.3.left_ref, bf16[256,6144]{1,0:T(8,128)(2,1)S(1)} %get-tuple-element.23.right_ref), custom_call_target="tpu_custom_call" | custom-call | flops 4831838208 | bytes 41680896 | tf_op jit(solution)/shard_map/pallas_call | solution.py:105
  128.5 0.0 copy-start.6
  128.5 0.0 collective-permute-done.1
  128.5 0.0 copy-done.4
  128.5 0.1 broadcast_select_fusion
  128.6 1.5 collective-permute-start.5
  131.4 0.5 collective-permute-done.5
  132.0 0.1 broadcast_select_fusion.2.left_ref
  132.0 0.0 copy-start.2
  132.1 0.3 multiply_reduce_fusion
  132.4 0.0 copy-done
  132.4 0.0 copy-done.6
  132.4 1.0 fusion.8
  133.4 0.0 copy-done.2
  133.4 0.6 collective-permute-start.6
  134.1 3.4 %collective-permute-done.6 = f32[256,32]{0,1:T(8,128)S(1)} collective-permute-done((f32[256,32]{0,1:T(8,128)S(1)}, f32[256,32]{0,1:T(8,128)S(1)}, u32[]{:S(2)}, u32[]{:S(2)}) %collective-permute-start.6) | collective-permute-done | bytes 32800 | tf_op jit(solution)/shard_map/ppermute | solution.py:25
  137.4 0.0 collective-permute-start.7
  137.7 3.7 %collective-permute-done.7 = f32[256,32]{0,1:T(8,128)S(1)} collective-permute-done((f32[256,32]{0,1:T(8,128)S(1)}, f32[256,32]{0,1:T(8,128)S(1)}, u32[]{:S(2)}, u32[]{:S(2)}) %collective-permute-start.7) | collective-permute-done | bytes 32800 | tf_op jit(solution)/shard_map/ppermute | solution.py:25
  141.4 0.0 copy-start.1
  141.4 0.1 collective-permute-start.8
  141.4 0.0 copy-start.3
  141.5 1.2 copy-done.3
  142.6 0.0 copy-start.7
  142.6 0.0 copy-start.5
  142.6 14.0 %shard_map.69 = f32[3072,6144]{1,0:T(8,128)} custom-call(bf16[256,1536]{1,0:T(8,128)(2,1)S(1)} %copy-done.3, bf16[256,6144]{1,0:T(8,128)(2,1)S(1)} %get-tuple-element.23.right_ref, f32[3072,6144]{1,0:T(8,128)} %shard_map.68.rest_0_), custom_call_target="tpu_custom_call", output_to_operand_aliasing={{}: (2, {})} | custom-call | flops 4831838208 | bytes 41680896 | tf_op jit(solution)/shard_map/pallas_call | solution.py:105
  156.6 0.0 collective-permute-done.8
  156.6 0.0 copy-done.1
  156.6 0.0 copy-done.7
  156.7 0.6 convolution_subtract_fusion.1
  157.3 0.0 copy-done.5
  157.3 0.3 fusion.7
  157.5 1.4 fusion.5
  (5 shorter events, 0.1 us)
Async XLA Ops:
  7.2 66.2 %all-gather.2.cloned.1.call-start = ((), (), s32[]{:S(2)}) async-start(), calls=%async_computation | async-start | bytes 3538944 | tf_op jit(solution)/shard_map/all_gather | solution.py:135
  77.7 13.2 %collective-permute-start = (bf16[256,1536]{1,0:T(8,128)(2,1)}, bf16[256,1536]{1,0:T(8,128)(2,1)}, u32[]{:S(2)}, u32[]{:S(2)}) collective-permute-start(bf16[256,1536]{1,0:T(8,128)(2,1)} %get-tuple-element.18), channel_id=1, source_target_pairs={{0,2},{4,6},{9,11},{13,15},{18,16},{22,20},{27,25},{31,29}} | collective-permute-start | bytes 2359304 | tf_op jit(solution)/shard_map/ppermute | solution.py:68
  92.9 20.3 %collective-permute-start.2 = (bf16[256,1536]{1,0:T(8,128)(2,1)}, bf16[256,1536]{1,0:T(8,128)(2,1)}, u32[]{:S(2)}, u32[]{:S(2)}) collective-permute-start(bf16[256,1536]{1,0:T(8,128)(2,1)} %broadcast_select_fusion.1), channel_id=1, source_target_pairs={{0,1},{2,3},{4,5},{6,7},{9,8},{11,10},{13,12},{15,14},{16,17},{18,... | collective-permute-start | bytes 2359304 | tf_op jit(solution)/shard_map/ppermute | solution.py:68
  97.0 1.6 collective-permute-start.3
  98.6 9.3 %collective-permute-start.4 = (f32[256,256]{1,0:T(8,128)S(1)}, f32[256,256]{1,0:T(8,128)}, u32[]{:S(2)}, u32[]{:S(2)}) collective-permute-start(f32[256,256]{1,0:T(8,128)S(1)} %add.72), channel_id=1, source_target_pairs={{0,2},{1,3},{2,0},{3,1},{4,6},{5,7},{6,4},{7,5},{8,10},{9,11},{10,... | collective-permute-start | bytes 786440 | tf_op jit(solution)/shard_map/ppermute | solution.py:25
  109.6 19.0 %collective-permute-start.1 = (bf16[256,1536]{1,0:T(8,128)(2,1)}, bf16[256,1536]{1,0:T(8,128)(2,1)S(1)}, u32[]{:S(2)}, u32[]{:S(2)}) collective-permute-start(bf16[256,1536]{1,0:T(8,128)(2,1)} %get-tuple-element.10), channel_id=1, source_target_pairs={{0,2},{4,6},{9,11},{13,15},{18,16},{22,20},{27,25},{31,29}} | collective-permute-start | bytes 2359304 | tf_op jit(solution)/shard_map/ppermute | solution.py:68
  114.5 17.9 %copy-start = (bf16[256,1536]{1,0:T(8,128)(2,1)}, bf16[256,1536]{1,0:T(8,128)(2,1)S(1)}, u32[]{:S(2)}) copy-start(bf16[256,1536]{1,0:T(8,128)(2,1)S(1)} %broadcast_select_fusion.3.left_ref) | copy-start | bytes 2359300
  114.5 14.0 %copy-start.4 = (bf16[256,1536]{1,0:T(8,128)(2,1)S(1)}, bf16[256,1536]{1,0:T(8,128)(2,1)}, u32[]{:S(2)}) copy-start(bf16[256,1536]{1,0:T(8,128)(2,1)} %get-tuple-element.10) | copy-start | bytes 2359300
  128.5 3.9 %copy-start.6 = (f32[3072,32]{0,1:T(8,128)S(1)}, f32[3072,32]{0,1:T(8,128)}, u32[]{:S(2)}) copy-start(f32[3072,32]{0,1:T(8,128)} %param.7) | copy-start | bytes 1179652
  128.6 3.3 %collective-permute-start.5 = (bf16[256,1536]{1,0:T(8,128)(2,1)S(1)}, bf16[256,1536]{1,0:T(8,128)(2,1)S(1)}, u32[]{:S(2)}, u32[]{:S(2)}) collective-permute-start(bf16[256,1536]{1,0:T(8,128)(2,1)S(1)} %broadcast_select_fusion), channel_id=1, source_target_pairs={{0,1},{2,3},{4,5},{6,7},{9,8},{11,10},{13,12},{15,14},{16,17},{18,... | collective-permute-start | bytes 2359304 | tf_op jit(solution)/shard_map/ppermute | solution.py:68
  132.0 1.4 copy-start.2
  133.4 4.0 %collective-permute-start.6 = (f32[256,32]{0,1:T(8,128)S(1)}, f32[256,32]{0,1:T(8,128)S(1)}, u32[]{:S(2)}, u32[]{:S(2)}) collective-permute-start(f32[256,32]{0,1:T(8,128)S(1)} %fusion.8), channel_id=1, source_target_pairs={{0,4},{4,0},{8,12},{12,8},{16,20},{20,16},{24,28},{28,24},{1,5},{5... | collective-permute-start | bytes 98312 | tf_op jit(solution)/shard_map/ppermute | solution.py:25
  137.4 3.9 %collective-permute-start.7 = (f32[256,32]{0,1:T(8,128)S(1)}, f32[256,32]{0,1:T(8,128)S(1)}, u32[]{:S(2)}, u32[]{:S(2)}) collective-permute-start(f32[256,32]{0,1:T(8,128)S(1)} %add.77), channel_id=1, source_target_pairs={{0,8},{4,12},{8,0},{12,4},{16,24},{20,28},{24,16},{28,20},{1,9},{5... | collective-permute-start | bytes 98312 | tf_op jit(solution)/shard_map/ppermute | solution.py:25
  141.4 15.3 %copy-start.1 = (bf16[256,1536]{1,0:T(8,128)(2,1)S(1)}, bf16[256,1536]{1,0:T(8,128)(2,1)}, u32[]{:S(2)}) copy-start(bf16[256,1536]{1,0:T(8,128)(2,1)} %copy-done) | copy-start | bytes 2359300
  141.4 15.3 %collective-permute-start.8 = (f32[256,32]{0,1:T(8,128)S(1)}, f32[256,32]{0,1:T(8,128)S(1)}, u32[]{:S(2)}, u32[]{:S(2)}) collective-permute-start(f32[256,32]{0,1:T(8,128)S(1)} %add.78), channel_id=1, source_target_pairs={{0,16},{4,20},{8,24},{12,28},{16,0},{20,4},{24,8},{28,12},{1,17},{... | collective-permute-start | bytes 98312 | tf_op jit(solution)/shard_map/ppermute | solution.py:25
  141.4 1.2 copy-start.3
  142.6 14.0 %copy-start.7 = (f32[3072,32]{0,1:T(8,128)S(1)}, f32[3072,32]{0,1:T(8,128)}, u32[]{:S(2)}) copy-start(f32[3072,32]{0,1:T(8,128)} %param.7) | copy-start | bytes 1179652
  142.6 14.6 %copy-start.5 = (f32[256,256]{1,0:T(8,128)S(1)}, f32[256,256]{1,0:T(8,128)}, u32[]{:S(2)}) copy-start(f32[256,256]{1,0:T(8,128)} %add.73) | copy-start | bytes 786436
Sparse Core Ops, SparseCore 0:
  10.2 63.1 all-gather.1

commit v9 on v8

--- a/solution.py
+++ b/solution.py
@@ -139,7 +139,7 @@
     own_slice = lax.dynamic_slice_in_dim(white, row_index % fold_ratio * row_width, row_width, 1)
 
     def couple():
-        white_wide = white.astype(jnp.float32)
+        white_wide = held["white"].astype(jnp.float32)
         panel_jacobi = jnp.sum(jnp.square(white_wide), axis=0) + 1e-06
         coupling = jnp.dot(
             white_wide / panel_jacobi[None, :], white_wide.T, precision=lax.Precision.HIGH
@@ -150,16 +150,19 @@
     held = {}
 
     def release_second(block):
-        held["second"], block = lax.optimization_barrier((own_slice[:, half_rows:], block))
+        held["second"], held["white"], block = lax.optimization_barrier(
+            (own_slice[:, half_rows:], white, block)
+        )
         return block
 
     panel_first, _ = tree_broadcast(
         own_slice[:, :half_rows], fold_ratio, lambda: (), release_second
     )
-    panel_second, (normal_tile, coupling) = tree_broadcast(
+    coupling = couple()
+    panel_second, normal_tile = tree_broadcast(
         held["second"],
         fold_ratio,
-        lambda: (normal_rows(panel_first, white, row_width, 0, None), couple()),
+        lambda: normal_rows(panel_first, white, row_width, 0, None),
     )
     normal_tile = normal_rows(panel_second, white, row_width, half_rows, normal_tile)
     panel = jnp.concatenate([panel_first, panel_second], axis=1)

time: 166 us -> 155 us (0.934)
  waiting for transfers between devices: 88.8 us -> 78.9 us
  starting transfers between devices: 15 us -> 13.2 us
    ppermute x5, waiting for transfers between devices: 15.3 us -> 5.95 us  [swap(): return lax.ppermute(block, axis, [(i, i ^ bit) for i in range(count)])]
    ppermute x5, starting transfers between devices: 3.32 us -> 0.83 us  [swap(): return lax.ppermute(block, axis, [(i, i ^ bit) for i in range(count)])]
  transfers between devices with their start and end apart: 10 -> 10, of which waited for: 7 -> 4; matrix products, arithmetic and copies ran while one was open for 4% -> 6% of each run, Pallas kernels for 17% -> 18%
where the time goes in v9:
time: 155 us; the launch traced here: 154 us
  waiting for transfers between devices  78.9 us (51%)
  Pallas kernels  28 us (18%)
  between operations  15.8 us (10%)
  starting transfers between devices  13.2 us (9%)
  matrix products  8.1 us (5%)
  other arithmetic  5.49 us (4%)
  local copies, waits for them, and re-layouts  4.98 us (3%)
    all_gather x1, waiting for transfers between devices, body(): whole_panel = lax.all_gather(design, 'row', axis=0, tiled=True)  63.4 us
    pallas_call x2, Pallas kernels, normal_rows(): pl.pallas_call(kernel, grid=(width // tile_cols, rows // tile_rows), in_s...  28 us
    ppermute x4, starting transfers between devices, tree_broadcast(): arrived = lax.ppermute(block, ('row', 'col'), pairs)  12.3 us
    ppermute x4, waiting for transfers between devices, tree_broadcast(): arrived = lax.ppermute(block, ('row', 'col'), pairs)  8.89 us
    ppermute x5, waiting for transfers between devices, swap(): return lax.ppermute(block, axis, [(i, i ^ bit) for i in range(count)])  5.95 us
    select_n x4, other arithmetic, tree_broadcast(): jnp.where((offset & ~done == 0) & (offset & bit != 0), arrived, block)  3.5 us
  transfers between devices with their start and end apart: 10, of which 4 were waited for; matrix products, arithmetic and copies ran while one was open for 6% of the time, Pallas kernels for 18%

profile of v9, /device:TPU:0, one launch (start us, length us, event | category | flops | bytes accessed | tf_op | source)
XLA Modules:
  0.0 154.5 jit_solution(9611557084153893286)
XLA Ops:
  7.2 0.0 all-gather.2.cloned.1.call-start
  7.2 0.7 all-gather.2.cloned.1.call-update
  7.9 0.7 concatenate.6
  8.6 0.1 broadcast_bitcast_fusion
  8.7 0.1 copy.8
  8.8 1.2 reshape.20
  10.0 63.4 %all-gather.2.cloned.1.call-done = bf16[256,6144]{1,0:T(8,128)(2,1)} async-done(((bf16[32,6144]{1,0:T(8,128)(2,1)}), bf16[256,6144]{1,0:T(8,128)(2,1)}) %all-gather.2.cloned.1.call-update) | async-done | bytes 3145744 | tf_op jit(solution)/shard_map/all_gather | solution.py:135
  73.4 3.0 %convolution_convert_fusion.right_ref = bf16[256,6144]{1,0:T(8,128)(2,1)S(1)} fusion(bf16[256,6144]{1,0:T(8,128)(2,1)} %all-gather.2.cloned.1.call-done, f32[256,511]{1,0:T(8,128)} %reshape.20), kind=kOutput, calls=%fused_computation.3 | convolution fusion | flops 807141376 | bytes 6553600 | tf_op jit(solution)/shard_map/dot_general | solution.py:136
  76.4 1.3 constant_dynamic-slice_fusion.1
  77.6 4.3 %collective-permute-start = (bf16[256,1536]{1,0:T(8,128)(2,1)}, bf16[256,1536]{1,0:T(8,128)(2,1)}, u32[]{:S(2)}, u32[]{:S(2)}) collective-permute-start(bf16[256,1536]{1,0:T(8,128)(2,1)} %get-tuple-element.16), channel_id=1, source_target_pairs={{0,2},{4,6},{9,11},{13,15},{18,16},{22,20},{27,25},{31,29}} | collective-permute-start | bytes 2359304 | tf_op jit(solution)/shard_map/ppermute | solution.py:68
  81.9 8.9 %collective-permute-done = bf16[256,1536]{1,0:T(8,128)(2,1)} collective-permute-done((bf16[256,1536]{1,0:T(8,128)(2,1)}, bf16[256,1536]{1,0:T(8,128)(2,1)}, u32[]{:S(2)}, u32[]{:S(2)}) %collective-permute-start) | collective-permute-done | bytes 786464 | tf_op jit(solution)/shard_map/ppermute | solution.py:68
  90.8 2.1 %broadcast_select_fusion.1 = bf16[256,1536]{1,0:T(8,128)(2,1)} fusion(bf16[256,1536]{1,0:T(8,128)(2,1)} %collective-permute-done, bf16[256,1536]{1,0:T(8,128)(2,1)} %get-tuple-element.16, pred[]{:T(512)S(6)} %and.43), kind=kLoop, calls=%fused_computation.17 | loop fusion | flops 393216 | bytes 2359297 | tf_op jit(solution)/shard_map/jit(_where)/select_n | solution.py:70
  92.9 2.2 %collective-permute-start.2 = (bf16[256,1536]{1,0:T(8,128)(2,1)}, bf16[256,1536]{1,0:T(8,128)(2,1)}, u32[]{:S(2)}, u32[]{:S(2)}) collective-permute-start(bf16[256,1536]{1,0:T(8,128)(2,1)} %broadcast_select_fusion.1), channel_id=1, source_target_pairs={{0,1},{2,3},{4,5},{6,7},{9,8},{11,10},{13,12},{15,14},{16,17},{18,... | collective-permute-start | bytes 2359304 | tf_op jit(solution)/shard_map/ppermute | solution.py:68
  96.4 4.4 %collective-permute-start.1 = (bf16[256,1536]{1,0:T(8,128)(2,1)}, bf16[256,1536]{1,0:T(8,128)(2,1)S(1)}, u32[]{:S(2)}, u32[]{:S(2)}) collective-permute-start(bf16[256,1536]{1,0:T(8,128)(2,1)} %get-tuple-element.9), channel_id=1, source_target_pairs={{0,2},{4,6},{9,11},{13,15},{18,16},{22,20},{27,25},{31,29}} | collective-permute-start | bytes 2359304 | tf_op jit(solution)/shard_map/ppermute | solution.py:68
  100.9 0.7 fusion.1
  101.6 0.0 collective-permute-done.2
  101.6 1.2 broadcast_select_fusion.3.left_ref
  102.8 0.0 copy-start
  102.8 0.0 copy-start.4
  102.8 14.0 %shard_map.68.rest_0_ = f32[3072,6144]{1,0:T(8,128)} custom-call(bf16[256,1536]{1,0:T(8,128)(2,1)S(1)} %broadcast_select_fusion.3.left_ref, bf16[256,6144]{1,0:T(8,128)(2,1)S(1)} %convolution_convert_fusion.right_ref), custom_call_target="tpu_custom_call" | custom-call | flops 4831838208 | bytes 41680896 | tf_op jit(solution)/shard_map/pallas_call | solution.py:105
  116.8 0.0 collective-permute-done.1
  116.8 0.0 copy-done.4
  116.8 0.1 broadcast_select_fusion
  116.9 1.3 collective-permute-start.3
  118.3 1.8 %fusion = f32[256,256]{1,0:T(8,128)S(1)} fusion(bf16[256,6144]{1,0:T(8,128)(2,1)S(1)} %convolution_convert_fusion.right_ref, f32[6144]{0:T(1024)S(1)} %broadcast_add_fusion), kind=kOutput, calls=%fused_computation.2 | convolution fusion | flops 2419064832 | bytes 3432448 | tf_op jit(solution)/shard_map/dot_general | solution.py:144
  120.1 0.0 copy-start.5
  120.1 0.1 collective-permute-start.7
  120.2 0.0 collective-permute-done.3
  120.2 0.1 broadcast_select_fusion.2.left_ref
  120.3 0.0 copy-start.2
  120.3 0.3 multiply_reduce_fusion
  120.7 0.0 copy-done
  120.7 0.4 copy-done.5
  121.1 1.0 fusion.8
  122.1 0.0 copy-done.2
  122.1 0.6 collective-permute-start.4
  122.8 3.4 %collective-permute-done.4 = f32[256,32]{0,1:T(8,128)S(1)} collective-permute-done((f32[256,32]{0,1:T(8,128)S(1)}, f32[256,32]{0,1:T(8,128)S(1)}, u32[]{:S(2)}, u32[]{:S(2)}) %collective-permute-start.4) | collective-permute-done | bytes 32800 | tf_op jit(solution)/shard_map/ppermute | solution.py:25
  126.1 0.0 collective-permute-start.5
  126.4 0.0 collective-permute-done.7
  126.4 1.0 add.80
  127.4 0.1 collective-permute-start.8
  127.5 2.6 %collective-permute-done.5 = f32[256,32]{0,1:T(8,128)S(1)} collective-permute-done((f32[256,32]{0,1:T(8,128)S(1)}, f32[256,32]{0,1:T(8,128)S(1)}, u32[]{:S(2)}, u32[]{:S(2)}) %collective-permute-start.5) | collective-permute-done | bytes 32800 | tf_op jit(solution)/shard_map/ppermute | solution.py:25
  130.0 0.0 copy-start.1
  130.0 0.1 collective-permute-start.6
  130.1 0.0 copy-start.3
  130.1 1.2 copy-done.3
  131.3 0.0 copy-start.6
  131.3 14.0 %shard_map.69 = f32[3072,6144]{1,0:T(8,128)} custom-call(bf16[256,1536]{1,0:T(8,128)(2,1)S(1)} %copy-done.3, bf16[256,6144]{1,0:T(8,128)(2,1)S(1)} %convolution_convert_fusion.right_ref, f32[3072,6144]{1,0:T(8,128)} %shard_map.68.rest_0_), custom_call_target="tpu_custom_call", output_to_operand_aliasing={{}: (2, {})} | custom-call | flops 4831838208 | bytes 41680896 | tf_op jit(solution)/shard_map/pallas_call | solution.py:105
  145.3 0.0 collective-permute-done.6
  145.3 0.0 copy-done.1
  145.3 0.0 copy-done.6
  145.3 0.6 convolution_subtract_fusion.1
  145.9 0.0 collective-permute-done.8
  146.0 0.3 fusion.7
  146.2 1.4 fusion.5
  (4 shorter events, 0.0 us)
Async XLA Ops:
  7.2 66.2 %all-gather.2.cloned.1.call-start = ((), (), s32[]{:S(2)}) async-start(), calls=%async_computation | async-start | bytes 3538944 | tf_op jit(solution)/shard_map/all_gather | solution.py:135
  77.6 13.2 %collective-permute-start = (bf16[256,1536]{1,0:T(8,128)(2,1)}, bf16[256,1536]{1,0:T(8,128)(2,1)}, u32[]{:S(2)}, u32[]{:S(2)}) collective-permute-start(bf16[256,1536]{1,0:T(8,128)(2,1)} %get-tuple-element.16), channel_id=1, source_target_pairs={{0,2},{4,6},{9,11},{13,15},{18,16},{22,20},{27,25},{31,29}} | collective-permute-start | bytes 2359304 | tf_op jit(solution)/shard_map/ppermute | solution.py:68
  92.9 8.6 %collective-permute-start.2 = (bf16[256,1536]{1,0:T(8,128)(2,1)}, bf16[256,1536]{1,0:T(8,128)(2,1)}, u32[]{:S(2)}, u32[]{:S(2)}) collective-permute-start(bf16[256,1536]{1,0:T(8,128)(2,1)} %broadcast_select_fusion.1), channel_id=1, source_target_pairs={{0,1},{2,3},{4,5},{6,7},{9,8},{11,10},{13,12},{15,14},{16,17},{18,... | collective-permute-start | bytes 2359304 | tf_op jit(solution)/shard_map/ppermute | solution.py:68
  96.4 20.4 %collective-permute-start.1 = (bf16[256,1536]{1,0:T(8,128)(2,1)}, bf16[256,1536]{1,0:T(8,128)(2,1)S(1)}, u32[]{:S(2)}, u32[]{:S(2)}) collective-permute-start(bf16[256,1536]{1,0:T(8,128)(2,1)} %get-tuple-element.9), channel_id=1, source_target_pairs={{0,2},{4,6},{9,11},{13,15},{18,16},{22,20},{27,25},{31,29}} | collective-permute-start | bytes 2359304 | tf_op jit(solution)/shard_map/ppermute | solution.py:68
  102.8 17.9 %copy-start = (bf16[256,1536]{1,0:T(8,128)(2,1)}, bf16[256,1536]{1,0:T(8,128)(2,1)S(1)}, u32[]{:S(2)}) copy-start(bf16[256,1536]{1,0:T(8,128)(2,1)S(1)} %broadcast_select_fusion.3.left_ref) | copy-start | bytes 2359300
  102.8 14.0 %copy-start.4 = (bf16[256,1536]{1,0:T(8,128)(2,1)S(1)}, bf16[256,1536]{1,0:T(8,128)(2,1)}, u32[]{:S(2)}) copy-start(bf16[256,1536]{1,0:T(8,128)(2,1)} %get-tuple-element.9) | copy-start | bytes 2359300
  116.9 3.3 %collective-permute-start.3 = (bf16[256,1536]{1,0:T(8,128)(2,1)S(1)}, bf16[256,1536]{1,0:T(8,128)(2,1)S(1)}, u32[]{:S(2)}, u32[]{:S(2)}) collective-permute-start(bf16[256,1536]{1,0:T(8,128)(2,1)S(1)} %broadcast_select_fusion), channel_id=1, source_target_pairs={{0,1},{2,3},{4,5},{6,7},{9,8},{11,10},{13,12},{15,14},{16,17},{18,... | collective-permute-start | bytes 2359304 | tf_op jit(solution)/shard_map/ppermute | solution.py:68
  120.1 1.0 copy-start.5
  120.1 6.3 %collective-permute-start.7 = (f32[256,256]{1,0:T(8,128)S(1)}, f32[256,256]{1,0:T(8,128)}, u32[]{:S(2)}, u32[]{:S(2)}) collective-permute-start(f32[256,256]{1,0:T(8,128)S(1)} %fusion), channel_id=1, source_target_pairs={{0,1},{1,0},{2,3},{3,2},{4,5},{5,4},{6,7},{7,6},{8,9},{9,8},{10,11... | collective-permute-start | bytes 786440 | tf_op jit(solution)/shard_map/ppermute | solution.py:25
  120.3 1.8 %copy-start.2 = (bf16[256,1536]{1,0:T(8,128)(2,1)}, bf16[256,1536]{1,0:T(8,128)(2,1)S(1)}, u32[]{:S(2)}) copy-start(bf16[256,1536]{1,0:T(8,128)(2,1)S(1)} %broadcast_select_fusion.2.left_ref) | copy-start | bytes 2359300
  122.1 4.0 %collective-permute-start.4 = (f32[256,32]{0,1:T(8,128)S(1)}, f32[256,32]{0,1:T(8,128)S(1)}, u32[]{:S(2)}, u32[]{:S(2)}) collective-permute-start(f32[256,32]{0,1:T(8,128)S(1)} %fusion.8), channel_id=1, source_target_pairs={{0,4},{4,0},{8,12},{12,8},{16,20},{20,16},{24,28},{28,24},{1,5},{5... | collective-permute-start | bytes 98312 | tf_op jit(solution)/shard_map/ppermute | solution.py:25
  126.1 3.9 %collective-permute-start.5 = (f32[256,32]{0,1:T(8,128)S(1)}, f32[256,32]{0,1:T(8,128)S(1)}, u32[]{:S(2)}, u32[]{:S(2)}) collective-permute-start(f32[256,32]{0,1:T(8,128)S(1)} %add.73), channel_id=1, source_target_pairs={{0,8},{4,12},{8,0},{12,4},{16,24},{20,28},{24,16},{28,20},{1,9},{5... | collective-permute-start | bytes 98312 | tf_op jit(solution)/shard_map/ppermute | solution.py:25
  127.4 18.6 %collective-permute-start.8 = (f32[256,256]{1,0:T(8,128)S(1)}, f32[256,256]{1,0:T(8,128)S(1)}, u32[]{:S(2)}, u32[]{:S(2)}) collective-permute-start(f32[256,256]{1,0:T(8,128)S(1)} %add.80), channel_id=1, source_target_pairs={{0,2},{1,3},{2,0},{3,1},{4,6},{5,7},{6,4},{7,5},{8,10},{9,11},{10,... | collective-permute-start | bytes 786440 | tf_op jit(solution)/shard_map/ppermute | solution.py:25
  130.0 15.3 %copy-start.1 = (bf16[256,1536]{1,0:T(8,128)(2,1)S(1)}, bf16[256,1536]{1,0:T(8,128)(2,1)}, u32[]{:S(2)}) copy-start(bf16[256,1536]{1,0:T(8,128)(2,1)} %copy-done) | copy-start | bytes 2359300
  130.0 15.3 %collective-permute-start.6 = (f32[256,32]{0,1:T(8,128)S(1)}, f32[256,32]{0,1:T(8,128)S(1)}, u32[]{:S(2)}, u32[]{:S(2)}) collective-permute-start(f32[256,32]{0,1:T(8,128)S(1)} %add.74), channel_id=1, source_target_pairs={{0,16},{4,20},{8,24},{12,28},{16,0},{20,4},{24,8},{28,12},{1,17},{... | collective-permute-start | bytes 98312 | tf_op jit(solution)/shard_map/ppermute | solution.py:25
  130.1 1.2 copy-start.3
  131.3 14.0 %copy-start.6 = (f32[3072,32]{0,1:T(8,128)S(1)}, f32[3072,32]{0,1:T(8,128)}, u32[]{:S(2)}) copy-start(f32[3072,32]{0,1:T(8,128)} %param.7) | copy-start | bytes 1179652
Sparse Core Ops, SparseCore 0:
  10.2 63.1 all-gather.1

commit v10 on v9

--- a/solution.py
+++ b/solution.py
@@ -32,6 +32,17 @@
     bit = 1
     while bit < count:
         block = block + swap(block, axis, count, bit)
+        bit *= 2
+    return block
+
+
+def tree_sum_under(block, axis, pieces):
+    count = lax.axis_size(axis)
+    bit = 1
+    while bit < count:
+        arrived = swap(block, axis, count, bit)
+        arrived, _ = lax.optimization_barrier((arrived, pieces.pop(0)()))
+        block = block + arrived
         bit *= 2
     return block
 
@@ -164,7 +175,6 @@
         fold_ratio,
         lambda: normal_rows(panel_first, white, row_width, 0, None),
     )
-    normal_tile = normal_rows(panel_second, white, row_width, half_rows, normal_tile)
     panel = jnp.concatenate([panel_first, panel_second], axis=1)
     panel_wide = panel.astype(jnp.float32)
     jacobi = (jnp.sum(jnp.square(panel_wide), axis=0) + 1e-06)[:, None]
@@ -175,7 +185,28 @@
     residual = probes
     scaled = residual / jacobi
     direction = scaled / center_value
-    scaled_image = tree_sum(jnp.dot(panel_wide, scaled, precision=lax.Precision.HIGH), "row")
+    partial_image = jnp.dot(panel_wide, scaled, precision=lax.Precision.HIGH)
+    if is_power_of_two(row_count) and row_count > 1:
+        step_count = row_count.bit_length() - 1
+        piece_rows = half_rows // step_count
+        tile = {"normal": normal_tile}
+
+        def piece(index):
+            def run():
+                start = index * piece_rows
+                stop = half_rows if index == step_count - 1 else start + piece_rows
+                tile["normal"] = normal_rows(
+                    panel_second[:, start:stop], white, row_width, half_rows + start, tile["normal"]
+                )
+                return tile["normal"]
+
+            return run
+
+        scaled_image = tree_sum_under(partial_image, "row", [piece(i) for i in range(step_count)])
+        normal_tile = tile["normal"]
+    else:
+        normal_tile = normal_rows(panel_second, white, row_width, half_rows, normal_tile)
+        scaled_image = tree_sum(partial_image, "row")
     image = scaled_image / center_value
     solution = jnp.zeros_like(residual)
     for sweep_index in range(SWEEPS):

time: 155 us -> 156 us (level)
  waiting for transfers between devices: 78.9 us -> 73.1 us
  starting transfers between devices: 13.2 us -> 16.4 us
  Pallas kernels: 28 us -> 31 us
  other arithmetic: 5.49 us -> 7.63 us
    ppermute x5, waiting for transfers between devices: 5.95 us -> 0.09 us  [swap(): return lax.ppermute(block, axis, [(i, i ^ bit) for i in range(count)])]
    pallas_call x2 -> x4, Pallas kernels: 28 us -> 31 us  [normal_rows(): pl.pallas_call(kernel, grid=(width // tile_cols, rows // tile_rows), in_s...]
    ppermute x5, starting transfers between devices: 0.83 us -> 3.37 us  [swap(): return lax.ppermute(block, axis, [(i, i ^ bit) for i in range(count)])]
    select_n x4, other arithmetic: 3.5 us -> 5.56 us  [tree_broadcast(): jnp.where((offset & ~done == 0) & (offset & bit != 0), arrived, block)]
    unnamed x16 -> x10, local copies, waits for them, and re-layouts: 1.83 us -> 0.21 us
  transfers between devices with their start and end apart: 10 -> 10, of which waited for: 4 -> 3; matrix products, arithmetic and copies ran while one was open for 6% -> 6% of each run, Pallas kernels for 18% -> 20%
where the time goes in v10:
time: 156 us; the launch traced here: 155 us
  waiting for transfers between devices  73.1 us (47%)
  Pallas kernels  31 us (20%)
  starting transfers between devices  16.4 us (11%)
  between operations  15.8 us (10%)
  matrix products  8.11 us (5%)
  other arithmetic  7.63 us (5%)
  local copies, waits for them, and re-layouts  3.44 us (2%)
    all_gather x1, waiting for transfers between devices, body(): whole_panel = lax.all_gather(design, 'row', axis=0, tiled=True)  63.4 us
    pallas_call x4, Pallas kernels, normal_rows(): pl.pallas_call(kernel, grid=(width // tile_cols, rows // tile_rows), in_s...  31 us
    ppermute x4, starting transfers between devices, tree_broadcast(): arrived = lax.ppermute(block, ('row', 'col'), pairs)  13 us
    ppermute x4, waiting for transfers between devices, tree_broadcast(): arrived = lax.ppermute(block, ('row', 'col'), pairs)  8.92 us
    select_n x4, other arithmetic, tree_broadcast(): jnp.where((offset & ~done == 0) & (offset & bit != 0), arrived, block)  5.56 us
    ppermute x5, starting transfers between devices, swap(): return lax.ppermute(block, axis, [(i, i ^ bit) for i in range(count)])  3.37 us
  transfers between devices with their start and end apart: 10, of which 3 were waited for; matrix products, arithmetic and copies ran while one was open for 6% of the time, Pallas kernels for 20%

profile of v10, /device:TPU:0, one launch (start us, length us, event | category | flops | bytes accessed | tf_op | source)
XLA Modules:
  0.0 155.5 jit_solution(1412691336822535035)
XLA Ops:
  7.2 0.0 all-gather.2.cloned.1.call-start
  7.2 0.7 all-gather.2.cloned.1.call-update
  7.9 0.7 concatenate.6
  8.6 0.1 broadcast_bitcast_fusion
  8.7 0.1 copy.10
  8.8 1.2 reshape.20
  10.0 63.4 %all-gather.2.cloned.1.call-done = bf16[256,6144]{1,0:T(8,128)(2,1)} async-done(((bf16[32,6144]{1,0:T(8,128)(2,1)}), bf16[256,6144]{1,0:T(8,128)(2,1)}) %all-gather.2.cloned.1.call-update) | async-done | bytes 3145744 | tf_op jit(solution)/shard_map/all_gather | solution.py:146
  73.4 3.0 %convolution_convert_fusion.right_ref = bf16[256,6144]{1,0:T(8,128)(2,1)S(1)} fusion(bf16[256,6144]{1,0:T(8,128)(2,1)} %all-gather.2.cloned.1.call-done, f32[256,511]{1,0:T(8,128)} %reshape.20), kind=kOutput, calls=%fused_computation.3 | convolution fusion | flops 807141376 | bytes 6553600 | tf_op jit(solution)/shard_map/dot_general | solution.py:147
  76.4 1.3 constant_dynamic-slice_fusion.1
  77.7 4.3 %collective-permute-start = (bf16[256,1536]{1,0:T(8,128)(2,1)}, bf16[256,1536]{1,0:T(8,128)(2,1)}, u32[]{:S(2)}, u32[]{:S(2)}) collective-permute-start(bf16[256,1536]{1,0:T(8,128)(2,1)} %get-tuple-element.22), channel_id=1, source_target_pairs={{0,2},{4,6},{9,11},{13,15},{18,16},{22,20},{27,25},{31,29}} | collective-permute-start | bytes 2359304 | tf_op jit(solution)/shard_map/ppermute | solution.py:79
  81.9 8.9 %collective-permute-done = bf16[256,1536]{1,0:T(8,128)(2,1)} collective-permute-done((bf16[256,1536]{1,0:T(8,128)(2,1)}, bf16[256,1536]{1,0:T(8,128)(2,1)}, u32[]{:S(2)}, u32[]{:S(2)}) %collective-permute-start) | collective-permute-done | bytes 786464 | tf_op jit(solution)/shard_map/ppermute | solution.py:79
  90.8 2.1 %broadcast_select_fusion.1 = bf16[256,1536]{1,0:T(8,128)(2,1)} fusion(bf16[256,1536]{1,0:T(8,128)(2,1)} %collective-permute-done, bf16[256,1536]{1,0:T(8,128)(2,1)} %get-tuple-element.22, pred[]{:T(512)S(6)} %and.43), kind=kLoop, calls=%fused_computation.18 | loop fusion | flops 393216 | bytes 2359297 | tf_op jit(solution)/shard_map/jit(_where)/select_n | solution.py:81
  92.9 2.2 %collective-permute-start.2 = (bf16[256,1536]{1,0:T(8,128)(2,1)}, bf16[256,1536]{1,0:T(8,128)(2,1)}, u32[]{:S(2)}, u32[]{:S(2)}) collective-permute-start(bf16[256,1536]{1,0:T(8,128)(2,1)} %broadcast_select_fusion.1), channel_id=1, source_target_pairs={{0,1},{2,3},{4,5},{6,7},{9,8},{11,10},{13,12},{15,14},{16,17},{18,... | collective-permute-start | bytes 2359304 | tf_op jit(solution)/shard_map/ppermute | solution.py:79
  95.1 4.4 %collective-permute-start.1 = (bf16[256,1536]{1,0:T(8,128)(2,1)}, bf16[256,1536]{1,0:T(8,128)(2,1)S(1)}, u32[]{:S(2)}, u32[]{:S(2)}) collective-permute-start(bf16[256,1536]{1,0:T(8,128)(2,1)} %get-tuple-element.12), channel_id=1, source_target_pairs={{0,2},{4,6},{9,11},{13,15},{18,16},{22,20},{27,25},{31,29}} | collective-permute-start | bytes 2359304 | tf_op jit(solution)/shard_map/ppermute | solution.py:79
  99.5 0.7 fusion.1
  100.2 0.0 collective-permute-done.2
  100.2 1.2 broadcast_select_fusion.3.left_ref
  101.5 0.0 copy-start
  101.5 0.0 copy-start.2
  101.5 14.0 %shard_map.68.rest_0_ = f32[3072,6144]{1,0:T(8,128)} custom-call(bf16[256,1536]{1,0:T(8,128)(2,1)S(1)} %broadcast_select_fusion.3.left_ref, bf16[256,6144]{1,0:T(8,128)(2,1)S(1)} %convolution_convert_fusion.right_ref), custom_call_target="tpu_custom_call" | custom-call | flops 4831838208 | bytes 41680896 | tf_op jit(solution)/shard_map/pallas_call | solution.py:116
  115.5 0.0 copy-done
  115.5 0.0 collective-permute-done.1
  115.5 0.0 copy-done.2
  115.5 1.0 broadcast_select_fusion
  116.5 2.2 %collective-permute-start.3 = (bf16[256,1536]{1,0:T(8,128)(2,1)}, bf16[256,1536]{1,0:T(8,128)(2,1)}, u32[]{:S(2)}, u32[]{:S(2)}) collective-permute-start(bf16[256,1536]{1,0:T(8,128)(2,1)} %broadcast_select_fusion), channel_id=1, source_target_pairs={{0,1},{2,3},{4,5},{6,7},{9,8},{11,10},{13,12},{15,14},{16,17},{18,... | collective-permute-start | bytes 2359304 | tf_op jit(solution)/shard_map/ppermute | solution.py:79
  118.7 1.8 %fusion = f32[256,256]{1,0:T(8,128)S(1)} fusion(bf16[256,6144]{1,0:T(8,128)(2,1)S(1)} %convolution_convert_fusion.right_ref, f32[6144]{0:T(1024)S(1)} %broadcast_add_fusion), kind=kOutput, calls=%fused_computation.2 | convolution fusion | flops 2419064832 | bytes 3432448 | tf_op jit(solution)/shard_map/dot_general | solution.py:155
  120.5 0.1 collective-permute-start.7
  122.1 0.0 copy-start.1
  122.1 0.0 copy-start.3
  122.2 0.1 collective-permute-done.7
  122.2 1.1 add.80
  123.3 0.1 collective-permute-start.8
  123.4 0.0 collective-permute-done.3
  123.4 1.2 broadcast_select_fusion.2
  124.6 0.1 fusion.22
  124.7 0.0 copy-done.1
  124.7 0.3 multiply_reduce_fusion
  125.1 0.0 copy-done.3
  125.1 1.0 fusion.9
  126.1 0.6 collective-permute-start.4
  126.7 5.6 %shard_map.69.rest_0_ = f32[3072,6144]{1,0:T(8,128)} custom-call(bf16[256,512]{1,0:T(8,128)(2,1)S(1)} %get-tuple-element.24.left_ref, bf16[256,6144]{1,0:T(8,128)(2,1)S(1)} %convolution_convert_fusion.right_ref, f32[3072,6144]{1,0:T(8,128)} %shard_map.68.rest_0_), custom_call_target="tpu_custom_call", output_to_operand_aliasing={{}: (2, {})} | custom-call | flops 1610612736 | bytes 15990784 | tf_op jit(solution)/shard_map/pallas_call | solution.py:116
  132.4 0.0 collective-permute-done.4
  132.4 0.1 collective-permute-start.5
  132.5 5.7 %shard_map.70.rest_0_ = f32[3072,6144]{1,0:T(8,128)} custom-call(bf16[256,512]{1,0:T(8,128)(2,1)S(1)} %get-tuple-element.25.left_ref, bf16[256,6144]{1,0:T(8,128)(2,1)S(1)} %convolution_convert_fusion.right_ref, f32[3072,6144]{1,0:T(8,128)} %shard_map.69.rest_0_), custom_call_target="tpu_custom_call", output_to_operand_aliasing={{}: (2, {})} | custom-call | flops 1610612736 | bytes 15990784 | tf_op jit(solution)/shard_map/pallas_call | solution.py:116
  138.1 0.0 collective-permute-done.5
  138.1 2.5 %collective-permute-start.6 = (f32[256,32]{0,1:T(8,128)S(1)}, f32[256,32]{0,1:T(8,128)S(1)}, u32[]{:S(2)}, u32[]{:S(2)}) collective-permute-start(f32[256,32]{0,1:T(8,128)S(1)} %add.74), channel_id=1, source_target_pairs={{0,16},{4,20},{8,24},{12,28},{16,0},{20,4},{24,8},{28,12},{1,17},{... | collective-permute-start | bytes 98312 | tf_op jit(solution)/shard_map/ppermute | solution.py:25
  140.7 5.6 %shard_map.71 = f32[3072,6144]{1,0:T(8,128)} custom-call(bf16[256,512]{1,0:T(8,128)(2,1)S(1)} %get-tuple-element.26.left_ref, bf16[256,6144]{1,0:T(8,128)(2,1)S(1)} %convolution_convert_fusion.right_ref, f32[3072,6144]{1,0:T(8,128)} %shard_map.70.rest_0_), custom_call_target="tpu_custom_call", output_to_operand_aliasing={{}: (2, {})} | custom-call | flops 1610612736 | bytes 15990784 | tf_op jit(solution)/shard_map/pallas_call | solution.py:116
  146.3 0.0 collective-permute-done.6
  146.3 0.6 convolution_subtract_fusion.1
  146.9 0.0 collective-permute-done.8
  146.9 0.3 fusion.8
  147.2 1.4 fusion.5
  (4 shorter events, 0.0 us)
Async XLA Ops:
  7.2 66.2 %all-gather.2.cloned.1.call-start = ((), (), s32[]{:S(2)}) async-start(), calls=%async_computation | async-start | bytes 3538944 | tf_op jit(solution)/shard_map/all_gather | solution.py:146
  77.7 13.2 %collective-permute-start = (bf16[256,1536]{1,0:T(8,128)(2,1)}, bf16[256,1536]{1,0:T(8,128)(2,1)}, u32[]{:S(2)}, u32[]{:S(2)}) collective-permute-start(bf16[256,1536]{1,0:T(8,128)(2,1)} %get-tuple-element.22), channel_id=1, source_target_pairs={{0,2},{4,6},{9,11},{13,15},{18,16},{22,20},{27,25},{31,29}} | collective-permute-start | bytes 2359304 | tf_op jit(solution)/shard_map/ppermute | solution.py:79
  92.9 7.3 %collective-permute-start.2 = (bf16[256,1536]{1,0:T(8,128)(2,1)}, bf16[256,1536]{1,0:T(8,128)(2,1)}, u32[]{:S(2)}, u32[]{:S(2)}) collective-permute-start(bf16[256,1536]{1,0:T(8,128)(2,1)} %broadcast_select_fusion.1), channel_id=1, source_target_pairs={{0,1},{2,3},{4,5},{6,7},{9,8},{11,10},{13,12},{15,14},{16,17},{18,... | collective-permute-start | bytes 2359304 | tf_op jit(solution)/shard_map/ppermute | solution.py:79
  95.1 20.4 %collective-permute-start.1 = (bf16[256,1536]{1,0:T(8,128)(2,1)}, bf16[256,1536]{1,0:T(8,128)(2,1)S(1)}, u32[]{:S(2)}, u32[]{:S(2)}) collective-permute-start(bf16[256,1536]{1,0:T(8,128)(2,1)} %get-tuple-element.12), channel_id=1, source_target_pairs={{0,2},{4,6},{9,11},{13,15},{18,16},{22,20},{27,25},{31,29}} | collective-permute-start | bytes 2359304 | tf_op jit(solution)/shard_map/ppermute | solution.py:79
  101.5 14.0 %copy-start = (bf16[256,1536]{1,0:T(8,128)(2,1)}, bf16[256,1536]{1,0:T(8,128)(2,1)S(1)}, u32[]{:S(2)}) copy-start(bf16[256,1536]{1,0:T(8,128)(2,1)S(1)} %broadcast_select_fusion.3.left_ref) | copy-start | bytes 2359300
  101.5 14.0 %copy-start.2 = (bf16[256,1536]{1,0:T(8,128)(2,1)S(1)}, bf16[256,1536]{1,0:T(8,128)(2,1)}, u32[]{:S(2)}) copy-start(bf16[256,1536]{1,0:T(8,128)(2,1)} %get-tuple-element.12) | copy-start | bytes 2359300
  116.5 6.9 %collective-permute-start.3 = (bf16[256,1536]{1,0:T(8,128)(2,1)}, bf16[256,1536]{1,0:T(8,128)(2,1)}, u32[]{:S(2)}, u32[]{:S(2)}) collective-permute-start(bf16[256,1536]{1,0:T(8,128)(2,1)} %broadcast_select_fusion), channel_id=1, source_target_pairs={{0,1},{2,3},{4,5},{6,7},{9,8},{11,10},{13,12},{15,14},{16,17},{18,... | collective-permute-start | bytes 2359304 | tf_op jit(solution)/shard_map/ppermute | solution.py:79
  120.5 1.7 %collective-permute-start.7 = (f32[256,256]{1,0:T(8,128)S(1)}, f32[256,256]{1,0:T(8,128)}, u32[]{:S(2)}, u32[]{:S(2)}) collective-permute-start(f32[256,256]{1,0:T(8,128)S(1)} %fusion), channel_id=1, source_target_pairs={{0,1},{1,0},{2,3},{3,2},{4,5},{5,4},{6,7},{7,6},{8,9},{9,8},{10,11... | collective-permute-start | bytes 786440 | tf_op jit(solution)/shard_map/ppermute | solution.py:25
  122.1 2.6 %copy-start.1 = (bf16[256,1536]{1,0:T(8,128)(2,1)S(1)}, bf16[256,1536]{1,0:T(8,128)(2,1)}, u32[]{:S(2)}) copy-start(bf16[256,1536]{1,0:T(8,128)(2,1)} %copy-done) | copy-start | bytes 2359300
  122.1 2.9 %copy-start.3 = (f32[3072,32]{0,1:T(8,128)S(1)}, f32[3072,32]{0,1:T(8,128)}, u32[]{:S(2)}) copy-start(f32[3072,32]{0,1:T(8,128)} %param.7) | copy-start | bytes 1179652
  123.3 23.6 %collective-permute-start.8 = (f32[256,256]{1,0:T(8,128)S(1)}, f32[256,256]{1,0:T(8,128)S(1)}, u32[]{:S(2)}, u32[]{:S(2)}) collective-permute-start(f32[256,256]{1,0:T(8,128)S(1)} %add.80), channel_id=1, source_target_pairs={{0,2},{1,3},{2,0},{3,1},{4,6},{5,7},{6,4},{7,5},{8,10},{9,11},{10,... | collective-permute-start | bytes 786440 | tf_op jit(solution)/shard_map/ppermute | solution.py:25
  126.1 6.3 %collective-permute-start.4 = (f32[256,32]{0,1:T(8,128)S(1)}, f32[256,32]{0,1:T(8,128)S(1)}, u32[]{:S(2)}, u32[]{:S(2)}) collective-permute-start(f32[256,32]{0,1:T(8,128)S(1)} %fusion.9), channel_id=1, source_target_pairs={{0,4},{4,0},{8,12},{12,8},{16,20},{20,16},{24,28},{28,24},{1,5},{5... | collective-permute-start | bytes 98312 | tf_op jit(solution)/shard_map/ppermute | solution.py:25
  132.4 5.7 %collective-permute-start.5 = (f32[256,32]{0,1:T(8,128)S(1)}, f32[256,32]{0,1:T(8,128)S(1)}, u32[]{:S(2)}, u32[]{:S(2)}) collective-permute-start(f32[256,32]{0,1:T(8,128)S(1)} %add.73), channel_id=1, source_target_pairs={{0,8},{4,12},{8,0},{12,4},{16,24},{20,28},{24,16},{28,20},{1,9},{5... | collective-permute-start | bytes 98312 | tf_op jit(solution)/shard_map/ppermute | solution.py:25
  138.1 8.2 %collective-permute-start.6 = (f32[256,32]{0,1:T(8,128)S(1)}, f32[256,32]{0,1:T(8,128)S(1)}, u32[]{:S(2)}, u32[]{:S(2)}) collective-permute-start(f32[256,32]{0,1:T(8,128)S(1)} %add.74), channel_id=1, source_target_pairs={{0,16},{4,20},{8,24},{12,28},{16,0},{20,4},{24,8},{28,12},{1,17},{... | collective-permute-start | bytes 98312 | tf_op jit(solution)/shard_map/ppermute | solution.py:25
Sparse Core Ops, SparseCore 0:
  10.2 63.1 all-gather.1

commit v11 on v9

--- a/solution.py
+++ b/solution.py
@@ -136,7 +136,13 @@
     white = jnp.dot(filter_matrix, whole_panel, preferred_element_type=jnp.float32).astype(
         jnp.bfloat16
     )
-    own_slice = lax.dynamic_slice_in_dim(white, row_index % fold_ratio * row_width, row_width, 1)
+    first_column = row_index % fold_ratio * row_width
+    half_rows = row_width // 2
+
+    def whiten_rows(start):
+        block = lax.dynamic_slice_in_dim(whole_panel, first_column + start, half_rows, 1)
+        return jnp.dot(filter_matrix, block, preferred_element_type=jnp.float32).astype(jnp.bfloat16)
+
 
     def couple():
         white_wide = held["white"].astype(jnp.float32)
@@ -146,17 +152,16 @@
         )
         return tree_sum(coupling, "col")
 
-    half_rows = row_width // 2
     held = {}
 
     def release_second(block):
         held["second"], held["white"], block = lax.optimization_barrier(
-            (own_slice[:, half_rows:], white, block)
+            (whiten_rows(half_rows), white, block)
         )
         return block
 
     panel_first, _ = tree_broadcast(
-        own_slice[:, :half_rows], fold_ratio, lambda: (), release_second
+        whiten_rows(0), fold_ratio, lambda: (), release_second
     )
     coupling = couple()
     panel_second, normal_tile = tree_broadcast(

time: 155 us -> 153 us (0.987)
  matrix products: 8.1 us -> 12.9 us
  waiting for transfers between devices: 78.9 us -> 74.3 us
  local copies, waits for them, and re-layouts: 4.98 us -> 2.9 us
    ppermute x4, waiting for transfers between devices: 8.89 us -> 3.5 us  [tree_broadcast(): arrived = lax.ppermute(block, ('row', 'col'), pairs)]
    dot_general x0 -> x2, matrix products: none -> 4.84 us  [whiten_rows(): jnp.dot(filter_matrix, block, preferred_element_type=jnp.float32)]
  transfers between devices with their start and end apart: 10 -> 10, of which waited for: 4 -> 4; matrix products, arithmetic and copies ran while one was open for 6% -> 9% of each run, Pallas kernels for 18% -> 18%
where the time goes in v11:
time: 153 us
  waiting for transfers between devices  74.3 us (49%)
  Pallas kernels  28 us (18%)
  between operations  15.9 us (10%)
  starting transfers between devices  13.1 us (9%)
  matrix products  12.9 us (8%)
  other arithmetic  5.48 us (4%)
  local copies, waits for them, and re-layouts  2.9 us (2%)
    all_gather x1, waiting for transfers between devices, body(): whole_panel = lax.all_gather(design, 'row', axis=0, tiled=True)  64.2 us
    pallas_call x2, Pallas kernels, normal_rows(): pl.pallas_call(kernel, grid=(width // tile_cols, rows // tile_rows), in_s...  28 us
    ppermute x4, starting transfers between devices, tree_broadcast(): arrived = lax.ppermute(block, ('row', 'col'), pairs)  12.2 us
    ppermute x5, waiting for transfers between devices, swap(): return lax.ppermute(block, axis, [(i, i ^ bit) for i in range(count)])  5.95 us
    dot_general x2, matrix products, whiten_rows(): jnp.dot(filter_matrix, block, preferred_element_type=jnp.float32)  4.84 us
    ppermute x4, waiting for transfers between devices, tree_broadcast(): arrived = lax.ppermute(block, ('row', 'col'), pairs)  3.5 us
    select_n x4, other arithmetic, tree_broadcast(): jnp.where((offset & ~done == 0) & (offset & bit != 0), arrived, block)  3.5 us
  transfers between devices with their start and end apart: 10, of which 4 were waited for; matrix products, arithmetic and copies ran while one was open for 9% of the time, Pallas kernels for 18%

profile of v11, /device:TPU:0, one launch (start us, length us, event | category | flops | bytes accessed | tf_op | source)
XLA Modules:
  0.0 152.6 jit_solution(16724406255835630758)
XLA Ops:
  7.2 0.0 all-gather.2.cloned.1.call-start
  7.2 0.7 all-gather.2.cloned.1.call-update
  7.9 0.7 concatenate.6
  8.6 0.1 broadcast_bitcast_fusion
  8.7 0.1 copy.8
  8.8 0.4 reshape.20
  9.2 0.0 copy-start.4
  9.2 64.2 %all-gather.2.cloned.1.call-done = bf16[256,6144]{1,0:T(8,128)(2,1)} async-done(((bf16[32,6144]{1,0:T(8,128)(2,1)}), bf16[256,6144]{1,0:T(8,128)(2,1)}) %all-gather.2.cloned.1.call-update) | async-done | bytes 3145744 | tf_op jit(solution)/shard_map/all_gather | solution.py:135
  73.4 2.4 %convolution_convert_fusion.1 = bf16[256,1536]{1,0:T(8,128)(2,1)} fusion(bf16[256,6144]{1,0:T(8,128)(2,1)} %all-gather.2.cloned.1.call-done, s32[]{:T(128)S(6)} %select_n.45, f32[256,511]{1,0:T(8,128)S(1)} %reshape.20), kind=kOutput, calls=%fused_computation.13 | convolution fusion | flops 201981952 | bytes 1835012 | tf_op jit(solution)/shard_map/dot_general | solution.py:144
  75.8 4.3 %collective-permute-start = (bf16[256,1536]{1,0:T(8,128)(2,1)}, bf16[256,1536]{1,0:T(8,128)(2,1)}, u32[]{:S(2)}, u32[]{:S(2)}) collective-permute-start(bf16[256,1536]{1,0:T(8,128)(2,1)} %convolution_convert_fusion.1), channel_id=1, source_target_pairs={{0,2},{4,6},{9,11},{13,15},{18,16},{22,20},{27,25},{31,29}} | collective-permute-start | bytes 2359304 | tf_op jit(solution)/shard_map/ppermute | solution.py:68
  80.0 0.0 copy-done.4
  80.0 2.4 %convolution_convert_fusion.2 = bf16[256,1536]{1,0:T(8,128)(2,1)} fusion(bf16[256,6144]{1,0:T(8,128)(2,1)} %all-gather.2.cloned.1.call-done, s32[]{:T(128)S(6)} %select_n.44, f32[256,511]{1,0:T(8,128)S(1)} %reshape.20), kind=kOutput, calls=%fused_computation.14 | convolution fusion | flops 201981952 | bytes 1835012 | tf_op jit(solution)/shard_map/dot_general | solution.py:144
  82.5 3.0 %convolution_convert_fusion.right_ref = bf16[256,6144]{1,0:T(8,128)(2,1)S(1)} fusion(bf16[256,6144]{1,0:T(8,128)(2,1)} %all-gather.2.cloned.1.call-done, f32[256,511]{1,0:T(8,128)} %copy-done.4), kind=kOutput, calls=%fused_computation.3 | convolution fusion | flops 807141376 | bytes 6553600 | tf_op jit(solution)/shard_map/dot_general | solution.py:136
  85.5 3.5 %collective-permute-done = bf16[256,1536]{1,0:T(8,128)(2,1)} collective-permute-done((bf16[256,1536]{1,0:T(8,128)(2,1)}, bf16[256,1536]{1,0:T(8,128)(2,1)}, u32[]{:S(2)}, u32[]{:S(2)}) %collective-permute-start) | collective-permute-done | bytes 786464 | tf_op jit(solution)/shard_map/ppermute | solution.py:68
  89.0 2.1 %broadcast_select_fusion.1 = bf16[256,1536]{1,0:T(8,128)(2,1)} fusion(bf16[256,1536]{1,0:T(8,128)(2,1)} %collective-permute-done, bf16[256,1536]{1,0:T(8,128)(2,1)} %convolution_convert_fusion.1, pred[]{:T(512)S(6)} %and.43), kind=kLoop, calls=%fused_computation.21 | loop fusion | flops 393216 | bytes 2359297 | tf_op jit(solution)/shard_map/jit(_where)/select_n | solution.py:70
  91.0 2.2 %collective-permute-start.2 = (bf16[256,1536]{1,0:T(8,128)(2,1)}, bf16[256,1536]{1,0:T(8,128)(2,1)}, u32[]{:S(2)}, u32[]{:S(2)}) collective-permute-start(bf16[256,1536]{1,0:T(8,128)(2,1)} %broadcast_select_fusion.1), channel_id=1, source_target_pairs={{0,1},{2,3},{4,5},{6,7},{9,8},{11,10},{13,12},{15,14},{16,17},{18,... | collective-permute-start | bytes 2359304 | tf_op jit(solution)/shard_map/ppermute | solution.py:68
  94.5 4.4 %collective-permute-start.1 = (bf16[256,1536]{1,0:T(8,128)(2,1)}, bf16[256,1536]{1,0:T(8,128)(2,1)S(1)}, u32[]{:S(2)}, u32[]{:S(2)}) collective-permute-start(bf16[256,1536]{1,0:T(8,128)(2,1)} %convolution_convert_fusion.2), channel_id=1, source_target_pairs={{0,2},{4,6},{9,11},{13,15},{18,16},{22,20},{27,25},{31,29}} | collective-permute-start | bytes 2359304 | tf_op jit(solution)/shard_map/ppermute | solution.py:68
  99.0 0.7 fusion.1
  99.7 0.0 collective-permute-done.2
  99.7 1.2 broadcast_select_fusion.3.left_ref
  100.9 0.0 copy-start
  100.9 0.0 copy-start.5
  100.9 14.0 %shard_map.68.rest_0_ = f32[3072,6144]{1,0:T(8,128)} custom-call(bf16[256,1536]{1,0:T(8,128)(2,1)S(1)} %broadcast_select_fusion.3.left_ref, bf16[256,6144]{1,0:T(8,128)(2,1)S(1)} %convolution_convert_fusion.right_ref), custom_call_target="tpu_custom_call" | custom-call | flops 4831838208 | bytes 41680896 | tf_op jit(solution)/shard_map/pallas_call | solution.py:105
  114.9 0.0 collective-permute-done.1
  114.9 0.0 copy-done.5
  115.0 0.1 broadcast_select_fusion
  115.0 1.3 collective-permute-start.3
  116.4 1.8 %fusion = f32[256,256]{1,0:T(8,128)S(1)} fusion(bf16[256,6144]{1,0:T(8,128)(2,1)S(1)} %convolution_convert_fusion.right_ref, f32[6144]{0:T(1024)S(1)} %broadcast_add_fusion), kind=kOutput, calls=%fused_computation.2 | convolution fusion | flops 2419064832 | bytes 3432448 | tf_op jit(solution)/shard_map/dot_general | solution.py:150
  118.2 0.0 copy-start.6
  118.2 0.1 collective-permute-start.7
  118.3 0.0 collective-permute-done.3
  118.3 0.1 broadcast_select_fusion.2.left_ref
  118.4 0.0 copy-start.2
  118.4 0.3 multiply_reduce_fusion
  118.8 0.0 copy-done
  118.8 0.4 copy-done.6
  119.2 1.0 fusion.10
  120.2 0.0 copy-done.2
  120.2 0.6 collective-permute-start.4
  120.9 3.4 %collective-permute-done.4 = f32[256,32]{0,1:T(8,128)S(1)} collective-permute-done((f32[256,32]{0,1:T(8,128)S(1)}, f32[256,32]{0,1:T(8,128)S(1)}, u32[]{:S(2)}, u32[]{:S(2)}) %collective-permute-start.4) | collective-permute-done | bytes 32800 | tf_op jit(solution)/shard_map/ppermute | solution.py:25
  124.2 0.0 collective-permute-start.5
  124.5 0.0 collective-permute-done.7
  124.5 1.0 add.90
  125.5 0.1 collective-permute-start.8
  125.6 2.6 %collective-permute-done.5 = f32[256,32]{0,1:T(8,128)S(1)} collective-permute-done((f32[256,32]{0,1:T(8,128)S(1)}, f32[256,32]{0,1:T(8,128)S(1)}, u32[]{:S(2)}, u32[]{:S(2)}) %collective-permute-start.5) | collective-permute-done | bytes 32800 | tf_op jit(solution)/shard_map/ppermute | solution.py:25
  128.2 0.0 copy-start.1
  128.2 0.1 collective-permute-start.6
  128.2 0.0 copy-start.3
  128.2 1.2 copy-done.3
  129.4 0.0 copy-start.7
  129.4 14.0 %shard_map.69 = f32[3072,6144]{1,0:T(8,128)} custom-call(bf16[256,1536]{1,0:T(8,128)(2,1)S(1)} %copy-done.3, bf16[256,6144]{1,0:T(8,128)(2,1)S(1)} %convolution_convert_fusion.right_ref, f32[3072,6144]{1,0:T(8,128)} %shard_map.68.rest_0_), custom_call_target="tpu_custom_call", output_to_operand_aliasing={{}: (2, {})} | custom-call | flops 4831838208 | bytes 41680896 | tf_op jit(solution)/shard_map/pallas_call | solution.py:105
  143.4 0.0 collective-permute-done.6
  143.4 0.0 copy-done.1
  143.4 0.0 copy-done.7
  143.4 0.6 convolution_subtract_fusion.1
  144.1 0.0 collective-permute-done.8
  144.1 0.3 fusion.7
  144.3 1.4 fusion.5
  (4 shorter events, 0.0 us)
Async XLA Ops:
  7.2 66.2 %all-gather.2.cloned.1.call-start = ((), (), s32[]{:S(2)}) async-start(), calls=%async_computation | async-start | bytes 3538944 | tf_op jit(solution)/shard_map/all_gather | solution.py:135
  9.2 70.8 %copy-start.4 = (f32[256,511]{1,0:T(8,128)}, f32[256,511]{1,0:T(8,128)S(1)}, u32[]{:S(2)}) copy-start(f32[256,511]{1,0:T(8,128)S(1)} %reshape.20) | copy-start | bytes 1569796
  75.8 13.2 %collective-permute-start = (bf16[256,1536]{1,0:T(8,128)(2,1)}, bf16[256,1536]{1,0:T(8,128)(2,1)}, u32[]{:S(2)}, u32[]{:S(2)}) collective-permute-start(bf16[256,1536]{1,0:T(8,128)(2,1)} %convolution_convert_fusion.1), channel_id=1, source_target_pairs={{0,2},{4,6},{9,11},{13,15},{18,16},{22,20},{27,25},{31,29}} | collective-permute-start | bytes 2359304 | tf_op jit(solution)/shard_map/ppermute | solution.py:68
  91.0 8.6 %collective-permute-start.2 = (bf16[256,1536]{1,0:T(8,128)(2,1)}, bf16[256,1536]{1,0:T(8,128)(2,1)}, u32[]{:S(2)}, u32[]{:S(2)}) collective-permute-start(bf16[256,1536]{1,0:T(8,128)(2,1)} %broadcast_select_fusion.1), channel_id=1, source_target_pairs={{0,1},{2,3},{4,5},{6,7},{9,8},{11,10},{13,12},{15,14},{16,17},{18,... | collective-permute-start | bytes 2359304 | tf_op jit(solution)/shard_map/ppermute | solution.py:68
  94.5 20.4 %collective-permute-start.1 = (bf16[256,1536]{1,0:T(8,128)(2,1)}, bf16[256,1536]{1,0:T(8,128)(2,1)S(1)}, u32[]{:S(2)}, u32[]{:S(2)}) collective-permute-start(bf16[256,1536]{1,0:T(8,128)(2,1)} %convolution_convert_fusion.2), channel_id=1, source_target_pairs={{0,2},{4,6},{9,11},{13,15},{18,16},{22,20},{27,25},{31,29}} | collective-permute-start | bytes 2359304 | tf_op jit(solution)/shard_map/ppermute | solution.py:68
  100.9 17.9 %copy-start = (bf16[256,1536]{1,0:T(8,128)(2,1)}, bf16[256,1536]{1,0:T(8,128)(2,1)S(1)}, u32[]{:S(2)}) copy-start(bf16[256,1536]{1,0:T(8,128)(2,1)S(1)} %broadcast_select_fusion.3.left_ref) | copy-start | bytes 2359300
  100.9 14.0 %copy-start.5 = (bf16[256,1536]{1,0:T(8,128)(2,1)S(1)}, bf16[256,1536]{1,0:T(8,128)(2,1)}, u32[]{:S(2)}) copy-start(bf16[256,1536]{1,0:T(8,128)(2,1)} %convolution_convert_fusion.2) | copy-start | bytes 2359300
  115.0 3.3 %collective-permute-start.3 = (bf16[256,1536]{1,0:T(8,128)(2,1)S(1)}, bf16[256,1536]{1,0:T(8,128)(2,1)S(1)}, u32[]{:S(2)}, u32[]{:S(2)}) collective-permute-start(bf16[256,1536]{1,0:T(8,128)(2,1)S(1)} %broadcast_select_fusion), channel_id=1, source_target_pairs={{0,1},{2,3},{4,5},{6,7},{9,8},{11,10},{13,12},{15,14},{16,17},{18,... | collective-permute-start | bytes 2359304 | tf_op jit(solution)/shard_map/ppermute | solution.py:68
  118.2 1.0 copy-start.6
  118.2 6.3 %collective-permute-start.7 = (f32[256,256]{1,0:T(8,128)S(1)}, f32[256,256]{1,0:T(8,128)}, u32[]{:S(2)}, u32[]{:S(2)}) collective-permute-start(f32[256,256]{1,0:T(8,128)S(1)} %fusion), channel_id=1, source_target_pairs={{0,1},{1,0},{2,3},{3,2},{4,5},{5,4},{6,7},{7,6},{8,9},{9,8},{10,11... | collective-permute-start | bytes 786440 | tf_op jit(solution)/shard_map/ppermute | solution.py:25
  118.4 1.8 %copy-start.2 = (bf16[256,1536]{1,0:T(8,128)(2,1)}, bf16[256,1536]{1,0:T(8,128)(2,1)S(1)}, u32[]{:S(2)}) copy-start(bf16[256,1536]{1,0:T(8,128)(2,1)S(1)} %broadcast_select_fusion.2.left_ref) | copy-start | bytes 2359300
  120.2 4.0 %collective-permute-start.4 = (f32[256,32]{0,1:T(8,128)S(1)}, f32[256,32]{0,1:T(8,128)S(1)}, u32[]{:S(2)}, u32[]{:S(2)}) collective-permute-start(f32[256,32]{0,1:T(8,128)S(1)} %fusion.10), channel_id=1, source_target_pairs={{0,4},{4,0},{8,12},{12,8},{16,20},{20,16},{24,28},{28,24},{1,5},{5... | collective-permute-start | bytes 98312 | tf_op jit(solution)/shard_map/ppermute | solution.py:25
  124.2 3.9 %collective-permute-start.5 = (f32[256,32]{0,1:T(8,128)S(1)}, f32[256,32]{0,1:T(8,128)S(1)}, u32[]{:S(2)}, u32[]{:S(2)}) collective-permute-start(f32[256,32]{0,1:T(8,128)S(1)} %add.83), channel_id=1, source_target_pairs={{0,8},{4,12},{8,0},{12,4},{16,24},{20,28},{24,16},{28,20},{1,9},{5... | collective-permute-start | bytes 98312 | tf_op jit(solution)/shard_map/ppermute | solution.py:25
  125.5 18.6 %collective-permute-start.8 = (f32[256,256]{1,0:T(8,128)S(1)}, f32[256,256]{1,0:T(8,128)S(1)}, u32[]{:S(2)}, u32[]{:S(2)}) collective-permute-start(f32[256,256]{1,0:T(8,128)S(1)} %add.90), channel_id=1, source_target_pairs={{0,2},{1,3},{2,0},{3,1},{4,6},{5,7},{6,4},{7,5},{8,10},{9,11},{10,... | collective-permute-start | bytes 786440 | tf_op jit(solution)/shard_map/ppermute | solution.py:25
  128.2 15.3 %copy-start.1 = (bf16[256,1536]{1,0:T(8,128)(2,1)S(1)}, bf16[256,1536]{1,0:T(8,128)(2,1)}, u32[]{:S(2)}) copy-start(bf16[256,1536]{1,0:T(8,128)(2,1)} %copy-done) | copy-start | bytes 2359300
  128.2 15.3 %collective-permute-start.6 = (f32[256,32]{0,1:T(8,128)S(1)}, f32[256,32]{0,1:T(8,128)S(1)}, u32[]{:S(2)}, u32[]{:S(2)}) collective-permute-start(f32[256,32]{0,1:T(8,128)S(1)} %add.84), channel_id=1, source_target_pairs={{0,16},{4,20},{8,24},{12,28},{16,0},{20,4},{24,8},{28,12},{1,17},{... | collective-permute-start | bytes 98312 | tf_op jit(solution)/shard_map/ppermute | solution.py:25
  128.2 1.2 copy-start.3
  129.4 14.0 %copy-start.7 = (f32[3072,32]{0,1:T(8,128)S(1)}, f32[3072,32]{0,1:T(8,128)}, u32[]{:S(2)}) copy-start(f32[3072,32]{0,1:T(8,128)} %param.7) | copy-start | bytes 1179652
Sparse Core Ops, SparseCore 0:
  10.2 63.1 all-gather.1

commit v12 on v11

--- a/solution.py
+++ b/solution.py
@@ -32,6 +32,23 @@
     bit = 1
     while bit < count:
         block = block + swap(block, axis, count, bit)
+        bit *= 2
+    return block
+
+
+def tree_gather(block, axis):
+    count = lax.axis_size(axis)
+    if not is_power_of_two(count):
+        return lax.all_gather(block, axis, axis=0, tiled=True)
+    index = lax.axis_index(axis)
+    bit = 1
+    while bit < count:
+        other = swap(block, axis, count, bit)
+        block = jnp.where(
+            index & bit == 0,
+            jnp.concatenate([block, other], axis=0),
+            jnp.concatenate([other, block], axis=0),
+        )
         bit *= 2
     return block
 
@@ -132,7 +149,14 @@
     panel_width = design.shape[1]
     row_width = panel_width // fold_ratio
     filter_matrix = whitening(filter_taps)
-    whole_panel = lax.all_gather(design, "row", axis=0, tiled=True)
+    offloaded = panel_width * 2 // 3 // 128 * 128
+    whole_panel = jnp.concatenate(
+        [
+            lax.all_gather(design[:, :offloaded], "row", axis=0, tiled=True),
+            tree_gather(design[:, offloaded:], "row"),
+        ],
+        axis=1,
+    )
     white = jnp.dot(filter_matrix, whole_panel, preferred_element_type=jnp.float32).astype(
         jnp.bfloat16
     )

time: 153 us -> 156 us (1.020)
  waiting for transfers between devices: 74.3 us -> 64.9 us
  starting transfers between devices: 13.1 us -> 21.7 us
  local copies, waits for them, and re-layouts: 2.9 us -> 6.32 us
    all_gather x1, waiting for transfers between devices: 64.2 us -> 19.3 us  [body(): lax.all_gather(design[:, :offloaded], 'row', axis=0, tiled=True)]
    ppermute x5 -> x8, waiting for transfers between devices: 5.95 us -> 41.4 us  [swap(): return lax.ppermute(block, axis, [(i, i ^ bit) for i in range(count)])]
    ppermute x5 -> x8, starting transfers between devices: 0.83 us -> 9.49 us  [swap(): return lax.ppermute(block, axis, [(i, i ^ bit) for i in range(count)])]
    slice x0 -> x2, local copies, waits for them, and re-layouts: none -> 2.59 us  [the longest x1 1.67 us: body(): design[:, :offloaded]]
  transfers between devices with their start and end apart: 10 -> 13, of which waited for: 4 -> 7; matrix products, arithmetic and copies ran while one was open for 9% -> 10% of each run, Pallas kernels for 18% -> 18%
where the time goes in v12:
time: 156 us; the launch traced here: 155 us
  waiting for transfers between devices  64.9 us (42%)
  Pallas kernels  28 us (18%)
  starting transfers between devices  21.7 us (14%)
  between operations  15.9 us (10%)
  matrix products  12.7 us (8%)
  local copies, waits for them, and re-layouts  6.32 us (4%)
  other arithmetic  5.88 us (4%)
    ppermute x8, waiting for transfers between devices, swap(): return lax.ppermute(block, axis, [(i, i ^ bit) for i in range(count)])  41.4 us
    pallas_call x2, Pallas kernels, normal_rows(): pl.pallas_call(kernel, grid=(width // tile_cols, rows // tile_rows), in_s...  28 us
    all_gather x1, waiting for transfers between devices, body(): lax.all_gather(design[:, :offloaded], 'row', axis=0, tiled=True)  19.3 us
    ppermute x4, starting transfers between devices, tree_broadcast(): arrived = lax.ppermute(block, ('row', 'col'), pairs)  12.2 us
    ppermute x8, starting transfers between devices, swap(): return lax.ppermute(block, axis, [(i, i ^ bit) for i in range(count)])  9.49 us
    dot_general x2, matrix products, whiten_rows(): jnp.dot(filter_matrix, block, preferred_element_type=jnp.float32)  5.36 us
    ppermute x4, waiting for transfers between devices, tree_broadcast(): arrived = lax.ppermute(block, ('row', 'col'), pairs)  4.1 us
    select_n x4, other arithmetic, tree_broadcast(): jnp.where((offset & ~done == 0) & (offset & bit != 0), arrived, block)  3.5 us
  transfers between devices with their start and end apart: 13, of which 7 were waited for; matrix products, arithmetic and copies ran while one was open for 10% of the time, Pallas kernels for 18%

profile of v12, /device:TPU:0, one launch (start us, length us, event | category | flops | bytes accessed | tf_op | source)
XLA Modules:
  0.0 155.4 jit_solution(3111480939131109233)
XLA Ops:
  7.2 0.0 all-gather.2.cloned.1.call-start
  7.2 1.7 %slice.14 = bf16[32,4096]{1,0:T(8,128)(2,1)} slice(bf16[32,6144]{1,0:T(8,128)(2,1)} %param.5), slice={[0:32], [0:4096]} | slice | bytes 524288 | tf_op jit(solution)/shard_map/slice | solution.py:155
  8.9 0.0 all-gather.2.cloned.1.call-update
  8.9 0.9 slice.15
  9.8 3.0 %collective-permute-start = (bf16[32,2048]{1,0:T(8,128)(2,1)S(1)}, bf16[32,2048]{1,0:T(8,128)(2,1)S(1)}, u32[]{:S(2)}, u32[]{:S(2)}) collective-permute-start(bf16[32,2048]{1,0:T(8,128)(2,1)S(1)} %slice.15), channel_id=1, source_target_pairs={{0,4},{4,0},{8,12},{12,8},{16,20},{20,16},{24,28},{28,24},{1,5},{5... | collective-permute-start | bytes 393224 | tf_op jit(solution)/shard_map/ppermute | solution.py:25
  12.9 3.5 %collective-permute-done = bf16[32,2048]{1,0:T(8,128)(2,1)S(1)} collective-permute-done((bf16[32,2048]{1,0:T(8,128)(2,1)S(1)}, bf16[32,2048]{1,0:T(8,128)(2,1)S(1)}, u32[]{:S(2)}, u32[]{:S(2)}) %collective-permute-start) | collective-permute-done | bytes 131104 | tf_op jit(solution)/shard_map/ppermute | solution.py:25
  16.4 1.9 %collective-permute-start.1 = (bf16[64,2048]{1,0:T(8,128)(2,1)S(1)}, bf16[64,2048]{1,0:T(8,128)(2,1)S(1)}, u32[]{:S(2)}, u32[]{:S(2)}) collective-permute-start(bf16[64,2048]{1,0:T(8,128)(2,1)S(1)} %maximum_select_fusion.2), channel_id=1, source_target_pairs={{0,8},{4,12},{8,0},{12,4},{16,24},{20,28},{24,16},{28,20},{1,9},{5... | collective-permute-start | bytes 786440 | tf_op jit(solution)/shard_map/ppermute | solution.py:25
  18.3 6.4 %collective-permute-done.1 = bf16[64,2048]{1,0:T(8,128)(2,1)S(1)} collective-permute-done((bf16[64,2048]{1,0:T(8,128)(2,1)S(1)}, bf16[64,2048]{1,0:T(8,128)(2,1)S(1)}, u32[]{:S(2)}, u32[]{:S(2)}) %collective-permute-start.1) | collective-permute-done | bytes 262176 | tf_op jit(solution)/shard_map/ppermute | solution.py:25
  24.6 0.1 maximum_select_fusion.1
  24.7 3.9 %collective-permute-start.2 = (bf16[128,2048]{1,0:T(8,128)(2,1)S(1)}, bf16[128,2048]{1,0:T(8,128)(2,1)S(1)}, u32[]{:S(2)}, u32[]{:S(2)}) collective-permute-start(bf16[128,2048]{1,0:T(8,128)(2,1)S(1)} %maximum_select_fusion.1), channel_id=1, source_target_pairs={{0,16},{4,20},{8,24},{12,28},{16,0},{20,4},{24,8},{28,12},{1,17},{... | collective-permute-start | bytes 1572872 | tf_op jit(solution)/shard_map/ppermute | solution.py:25
  28.6 0.7 concatenate.27
  29.3 0.1 broadcast_bitcast_fusion
  29.3 0.1 copy.8
  29.5 1.2 reshape.20
  30.7 25.5 %collective-permute-done.2 = bf16[128,2048]{1,0:T(8,128)(2,1)S(1)} collective-permute-done((bf16[128,2048]{1,0:T(8,128)(2,1)S(1)}, bf16[128,2048]{1,0:T(8,128)(2,1)S(1)}, u32[]{:S(2)}, u32[]{:S(2)}) %collective-permute-start.2) | collective-permute-done | bytes 524320 | tf_op jit(solution)/shard_map/ppermute | solution.py:25
  56.2 0.2 maximum_select_fusion
  56.5 0.0 copy-start.6
  56.5 19.3 %all-gather.2.cloned.1.call-done = bf16[256,4096]{1,0:T(8,128)(2,1)} async-done(((bf16[32,4096]{1,0:T(8,128)(2,1)}), bf16[256,4096]{1,0:T(8,128)(2,1)}) %all-gather.2.cloned.1.call-update) | async-done | bytes 2097168 | tf_op jit(solution)/shard_map/all_gather | solution.py:155
  75.8 2.8 %convolution_convert_fusion.1 = bf16[256,1536]{1,0:T(8,128)(2,1)} fusion(s32[]{:T(128)S(6)} %select_n.75, bf16[256,4096]{1,0:T(8,128)(2,1)} %all-gather.2.cloned.1.call-done, bf16[256,2048]{1,0:T(8,128)(2,1)S(1)} %maximum_select_fusion, f32[256,511]{1,0:T(8,128)} %reshape.20), kind=kOutput, calls=%fused_computation.18 | convolution fusion | flops 203554816 | bytes 4194308 | tf_op jit(solution)/shard_map/dot_general | solution.py:168
  78.6 4.3 %collective-permute-start.3 = (bf16[256,1536]{1,0:T(8,128)(2,1)}, bf16[256,1536]{1,0:T(8,128)(2,1)}, u32[]{:S(2)}, u32[]{:S(2)}) collective-permute-start(bf16[256,1536]{1,0:T(8,128)(2,1)} %convolution_convert_fusion.1), channel_id=1, source_target_pairs={{0,2},{4,6},{9,11},{13,15},{18,16},{22,20},{27,25},{31,29}} | collective-permute-start | bytes 2359304 | tf_op jit(solution)/shard_map/ppermute | solution.py:85
  82.9 0.0 copy-done.6
  82.9 0.0 copy-done.4
  82.9 2.6 %convolution_convert_fusion.2 = bf16[256,1536]{1,0:T(8,128)(2,1)} fusion(s32[]{:T(128)S(6)} %select_n.74, bf16[256,4096]{1,0:T(8,128)(2,1)S(1)} %copy-done.4, bf16[256,2048]{1,0:T(8,128)(2,1)S(1)} %maximum_select_fusion, f32[256,511]{1,0:T(8,128)} %reshape.20), kind=kOutput, calls=%fused_computation.19 | convolution fusion | flops 203554816 | bytes 4194308 | tf_op jit(solution)/shard_map/dot_general | solution.py:168
  85.5 0.0 copy-done.5
  85.5 0.0 copy-done.7
  85.5 2.2 %convolution_convert_fusion.right_ref = bf16[256,6144]{1,0:T(8,128)(2,1)S(1)} fusion(bf16[256,2048]{1,0:T(8,128)(2,1)} %copy-done.6, bf16[256,4096]{1,0:T(8,128)(2,1)S(1)} %copy-done.5, f32[256,511]{1,0:T(8,128)S(1)} %copy-done.7), kind=kOutput, calls=%fused_computation.3 | convolution fusion | flops 813432832 | bytes 6553600 | tf_op jit(solution)/shard_map/dot_general | solution.py:160
  87.7 4.1 %collective-permute-done.3 = bf16[256,1536]{1,0:T(8,128)(2,1)} collective-permute-done((bf16[256,1536]{1,0:T(8,128)(2,1)}, bf16[256,1536]{1,0:T(8,128)(2,1)}, u32[]{:S(2)}, u32[]{:S(2)}) %collective-permute-start.3) | collective-permute-done | bytes 786464 | tf_op jit(solution)/shard_map/ppermute | solution.py:85
  91.8 2.1 %broadcast_select_fusion.1 = bf16[256,1536]{1,0:T(8,128)(2,1)} fusion(bf16[256,1536]{1,0:T(8,128)(2,1)} %collective-permute-done.3, bf16[256,1536]{1,0:T(8,128)(2,1)} %convolution_convert_fusion.1, pred[]{:T(512)S(6)} %and.52), kind=kLoop, calls=%fused_computation.27 | loop fusion | flops 393216 | bytes 2359297 | tf_op jit(solution)/shard_map/jit(_where)/select_n | solution.py:87
  93.9 2.2 %collective-permute-start.5 = (bf16[256,1536]{1,0:T(8,128)(2,1)}, bf16[256,1536]{1,0:T(8,128)(2,1)}, u32[]{:S(2)}, u32[]{:S(2)}) collective-permute-start(bf16[256,1536]{1,0:T(8,128)(2,1)} %broadcast_select_fusion.1), channel_id=1, source_target_pairs={{0,1},{2,3},{4,5},{6,7},{9,8},{11,10},{13,12},{15,14},{16,17},{18,... | collective-permute-start | bytes 2359304 | tf_op jit(solution)/shard_map/ppermute | solution.py:85
  97.4 4.4 %collective-permute-start.4 = (bf16[256,1536]{1,0:T(8,128)(2,1)}, bf16[256,1536]{1,0:T(8,128)(2,1)S(1)}, u32[]{:S(2)}, u32[]{:S(2)}) collective-permute-start(bf16[256,1536]{1,0:T(8,128)(2,1)} %convolution_convert_fusion.2), channel_id=1, source_target_pairs={{0,2},{4,6},{9,11},{13,15},{18,16},{22,20},{27,25},{31,29}} | collective-permute-start | bytes 2359304 | tf_op jit(solution)/shard_map/ppermute | solution.py:85
  101.8 0.7 fusion.1
  102.5 0.0 collective-permute-done.5
  102.5 1.2 broadcast_select_fusion.3.left_ref
  103.7 0.0 copy-start
  103.7 0.0 copy-start.8
  103.7 14.0 %shard_map.68.rest_0_ = f32[3072,6144]{1,0:T(8,128)} custom-call(bf16[256,1536]{1,0:T(8,128)(2,1)S(1)} %broadcast_select_fusion.3.left_ref, bf16[256,6144]{1,0:T(8,128)(2,1)S(1)} %convolution_convert_fusion.right_ref), custom_call_target="tpu_custom_call" | custom-call | flops 4831838208 | bytes 41680896 | tf_op jit(solution)/shard_map/pallas_call | solution.py:122
  117.7 0.0 collective-permute-done.4
  117.8 0.1 broadcast_select_fusion
  117.8 1.3 collective-permute-start.6
  119.2 1.8 %fusion = f32[256,256]{1,0:T(8,128)S(1)} fusion(bf16[256,6144]{1,0:T(8,128)(2,1)S(1)} %convolution_convert_fusion.right_ref, f32[6144]{0:T(1024)S(1)} %broadcast_add_fusion), kind=kOutput, calls=%fused_computation.2 | convolution fusion | flops 2419064832 | bytes 3432448 | tf_op jit(solution)/shard_map/dot_general | solution.py:174
  121.0 0.0 copy-start.9
  121.0 0.1 collective-permute-start.10
  121.1 0.0 collective-permute-done.6
  121.1 0.1 broadcast_select_fusion.2.left_ref
  121.2 0.3 multiply_reduce_fusion
  121.6 0.0 copy-done
  121.6 0.4 copy-done.9
  122.0 1.0 fusion.12
  123.0 0.5 collective-permute-start.7
  123.6 3.5 %collective-permute-done.7 = f32[256,32]{0,1:T(8,128)S(1)} collective-permute-done((f32[256,32]{0,1:T(8,128)S(1)}, f32[256,32]{0,1:T(8,128)S(1)}, u32[]{:S(2)}, u32[]{:S(2)}) %collective-permute-start.7) | collective-permute-done | bytes 32800 | tf_op jit(solution)/shard_map/ppermute | solution.py:25
  127.0 0.0 collective-permute-start.8
  127.3 0.0 collective-permute-done.10
  127.3 1.0 add.90
  128.3 0.1 collective-permute-start.11
  128.4 2.6 %collective-permute-done.8 = f32[256,32]{0,1:T(8,128)S(1)} collective-permute-done((f32[256,32]{0,1:T(8,128)S(1)}, f32[256,32]{0,1:T(8,128)S(1)}, u32[]{:S(2)}, u32[]{:S(2)}) %collective-permute-start.8) | collective-permute-done | bytes 32800 | tf_op jit(solution)/shard_map/ppermute | solution.py:25
  131.0 0.1 collective-permute-start.9
  131.1 1.2 copy-done.3
  132.2 14.0 %shard_map.69 = f32[3072,6144]{1,0:T(8,128)} custom-call(bf16[256,1536]{1,0:T(8,128)(2,1)S(1)} %copy-done.3, bf16[256,6144]{1,0:T(8,128)(2,1)S(1)} %convolution_convert_fusion.right_ref, f32[3072,6144]{1,0:T(8,128)} %shard_map.68.rest_0_), custom_call_target="tpu_custom_call", output_to_operand_aliasing={{}: (2, {})} | custom-call | flops 4831838208 | bytes 41680896 | tf_op jit(solution)/shard_map/pallas_call | solution.py:122
  146.2 0.0 collective-permute-done.9
  146.2 0.0 copy-done.1
  146.2 0.6 convolution_subtract_fusion.1
  146.9 0.0 collective-permute-done.11
  146.9 0.3 fusion.7
  147.1 1.4 fusion.5
  (15 shorter events, 0.1 us)
Async XLA Ops:
  7.2 68.6 %all-gather.2.cloned.1.call-start = ((), (), s32[]{:S(2)}) async-start(), calls=%async_computation | async-start | bytes 2359296 | tf_op jit(solution)/shard_map/all_gather | solution.py:155
  9.8 6.5 %collective-permute-start = (bf16[32,2048]{1,0:T(8,128)(2,1)S(1)}, bf16[32,2048]{1,0:T(8,128)(2,1)S(1)}, u32[]{:S(2)}, u32[]{:S(2)}) collective-permute-start(bf16[32,2048]{1,0:T(8,128)(2,1)S(1)} %slice.15), channel_id=1, source_target_pairs={{0,4},{4,0},{8,12},{12,8},{16,20},{20,16},{24,28},{28,24},{1,5},{5... | collective-permute-start | bytes 393224 | tf_op jit(solution)/shard_map/ppermute | solution.py:25
  16.4 8.2 %collective-permute-start.1 = (bf16[64,2048]{1,0:T(8,128)(2,1)S(1)}, bf16[64,2048]{1,0:T(8,128)(2,1)S(1)}, u32[]{:S(2)}, u32[]{:S(2)}) collective-permute-start(bf16[64,2048]{1,0:T(8,128)(2,1)S(1)} %maximum_select_fusion.2), channel_id=1, source_target_pairs={{0,8},{4,12},{8,0},{12,4},{16,24},{20,28},{24,16},{28,20},{1,9},{5... | collective-permute-start | bytes 786440 | tf_op jit(solution)/shard_map/ppermute | solution.py:25
  24.7 31.5 %collective-permute-start.2 = (bf16[128,2048]{1,0:T(8,128)(2,1)S(1)}, bf16[128,2048]{1,0:T(8,128)(2,1)S(1)}, u32[]{:S(2)}, u32[]{:S(2)}) collective-permute-start(bf16[128,2048]{1,0:T(8,128)(2,1)S(1)} %maximum_select_fusion.1), channel_id=1, source_target_pairs={{0,16},{4,20},{8,24},{12,28},{16,0},{20,4},{24,8},{28,12},{1,17},{... | collective-permute-start | bytes 1572872 | tf_op jit(solution)/shard_map/ppermute | solution.py:25
  56.5 26.4 %copy-start.6 = (bf16[256,2048]{1,0:T(8,128)(2,1)}, bf16[256,2048]{1,0:T(8,128)(2,1)S(1)}, u32[]{:S(2)}) copy-start(bf16[256,2048]{1,0:T(8,128)(2,1)S(1)} %maximum_select_fusion) | copy-start | bytes 3145732
  75.8 7.1 %copy-start.4 = (bf16[256,4096]{1,0:T(8,128)(2,1)S(1)}, bf16[256,4096]{1,0:T(8,128)(2,1)}, u32[]{:S(2)}) copy-start(bf16[256,4096]{1,0:T(8,128)(2,1)} %all-gather.2.cloned.1.call-done) | copy-start | bytes 6291460
  78.6 13.2 %collective-permute-start.3 = (bf16[256,1536]{1,0:T(8,128)(2,1)}, bf16[256,1536]{1,0:T(8,128)(2,1)}, u32[]{:S(2)}, u32[]{:S(2)}) collective-permute-start(bf16[256,1536]{1,0:T(8,128)(2,1)} %convolution_convert_fusion.1), channel_id=1, source_target_pairs={{0,2},{4,6},{9,11},{13,15},{18,16},{22,20},{27,25},{31,29}} | collective-permute-start | bytes 2359304 | tf_op jit(solution)/shard_map/ppermute | solution.py:85
  82.9 2.6 %copy-start.5 = (bf16[256,4096]{1,0:T(8,128)(2,1)S(1)}, bf16[256,4096]{1,0:T(8,128)(2,1)}, u32[]{:S(2)}) copy-start(bf16[256,4096]{1,0:T(8,128)(2,1)} %all-gather.2.cloned.1.call-done) | copy-start | bytes 6291460
  82.9 2.6 %copy-start.7 = (f32[256,511]{1,0:T(8,128)S(1)}, f32[256,511]{1,0:T(8,128)}, u32[]{:S(2)}) copy-start(f32[256,511]{1,0:T(8,128)} %reshape.20) | copy-start | bytes 1569796
  93.9 8.6 %collective-permute-start.5 = (bf16[256,1536]{1,0:T(8,128)(2,1)}, bf16[256,1536]{1,0:T(8,128)(2,1)}, u32[]{:S(2)}, u32[]{:S(2)}) collective-permute-start(bf16[256,1536]{1,0:T(8,128)(2,1)} %broadcast_select_fusion.1), channel_id=1, source_target_pairs={{0,1},{2,3},{4,5},{6,7},{9,8},{11,10},{13,12},{15,14},{16,17},{18,... | collective-permute-start | bytes 2359304 | tf_op jit(solution)/shard_map/ppermute | solution.py:85
  97.4 20.4 %collective-permute-start.4 = (bf16[256,1536]{1,0:T(8,128)(2,1)}, bf16[256,1536]{1,0:T(8,128)(2,1)S(1)}, u32[]{:S(2)}, u32[]{:S(2)}) collective-permute-start(bf16[256,1536]{1,0:T(8,128)(2,1)} %convolution_convert_fusion.2), channel_id=1, source_target_pairs={{0,2},{4,6},{9,11},{13,15},{18,16},{22,20},{27,25},{31,29}} | collective-permute-start | bytes 2359304 | tf_op jit(solution)/shard_map/ppermute | solution.py:85
  103.7 17.9 %copy-start = (bf16[256,1536]{1,0:T(8,128)(2,1)}, bf16[256,1536]{1,0:T(8,128)(2,1)S(1)}, u32[]{:S(2)}) copy-start(bf16[256,1536]{1,0:T(8,128)(2,1)S(1)} %broadcast_select_fusion.3.left_ref) | copy-start | bytes 2359300
  103.7 14.0 %copy-start.8 = (bf16[256,1536]{1,0:T(8,128)(2,1)S(1)}, bf16[256,1536]{1,0:T(8,128)(2,1)}, u32[]{:S(2)}) copy-start(bf16[256,1536]{1,0:T(8,128)(2,1)} %convolution_convert_fusion.2) | copy-start | bytes 2359300
  117.8 3.3 %collective-permute-start.6 = (bf16[256,1536]{1,0:T(8,128)(2,1)S(1)}, bf16[256,1536]{1,0:T(8,128)(2,1)S(1)}, u32[]{:S(2)}, u32[]{:S(2)}) collective-permute-start(bf16[256,1536]{1,0:T(8,128)(2,1)S(1)} %broadcast_select_fusion), channel_id=1, source_target_pairs={{0,1},{2,3},{4,5},{6,7},{9,8},{11,10},{13,12},{15,14},{16,17},{18,... | collective-permute-start | bytes 2359304 | tf_op jit(solution)/shard_map/ppermute | solution.py:85
  121.0 1.0 copy-start.9
  121.0 6.3 %collective-permute-start.10 = (f32[256,256]{1,0:T(8,128)S(1)}, f32[256,256]{1,0:T(8,128)}, u32[]{:S(2)}, u32[]{:S(2)}) collective-permute-start(f32[256,256]{1,0:T(8,128)S(1)} %fusion), channel_id=1, source_target_pairs={{0,1},{1,0},{2,3},{3,2},{4,5},{5,4},{6,7},{7,6},{8,9},{9,8},{10,11... | collective-permute-start | bytes 786440 | tf_op jit(solution)/shard_map/ppermute | solution.py:25
  121.2 1.8 %copy-start.2 = (bf16[256,1536]{1,0:T(8,128)(2,1)}, bf16[256,1536]{1,0:T(8,128)(2,1)S(1)}, u32[]{:S(2)}) copy-start(bf16[256,1536]{1,0:T(8,128)(2,1)S(1)} %broadcast_select_fusion.2.left_ref) | copy-start | bytes 2359300
  123.0 4.0 %collective-permute-start.7 = (f32[256,32]{0,1:T(8,128)S(1)}, f32[256,32]{0,1:T(8,128)S(1)}, u32[]{:S(2)}, u32[]{:S(2)}) collective-permute-start(f32[256,32]{0,1:T(8,128)S(1)} %fusion.12), channel_id=1, source_target_pairs={{0,4},{4,0},{8,12},{12,8},{16,20},{20,16},{24,28},{28,24},{1,5},{5... | collective-permute-start | bytes 98312 | tf_op jit(solution)/shard_map/ppermute | solution.py:25
  127.0 3.9 %collective-permute-start.8 = (f32[256,32]{0,1:T(8,128)S(1)}, f32[256,32]{0,1:T(8,128)S(1)}, u32[]{:S(2)}, u32[]{:S(2)}) collective-permute-start(f32[256,32]{0,1:T(8,128)S(1)} %add.83), channel_id=1, source_target_pairs={{0,8},{4,12},{8,0},{12,4},{16,24},{20,28},{24,16},{28,20},{1,9},{5... | collective-permute-start | bytes 98312 | tf_op jit(solution)/shard_map/ppermute | solution.py:25
  128.3 18.6 %collective-permute-start.11 = (f32[256,256]{1,0:T(8,128)S(1)}, f32[256,256]{1,0:T(8,128)S(1)}, u32[]{:S(2)}, u32[]{:S(2)}) collective-permute-start(f32[256,256]{1,0:T(8,128)S(1)} %add.90), channel_id=1, source_target_pairs={{0,2},{1,3},{2,0},{3,1},{4,6},{5,7},{6,4},{7,5},{8,10},{9,11},{10,... | collective-permute-start | bytes 786440 | tf_op jit(solution)/shard_map/ppermute | solution.py:25
  131.0 15.3 %copy-start.1 = (bf16[256,1536]{1,0:T(8,128)(2,1)S(1)}, bf16[256,1536]{1,0:T(8,128)(2,1)}, u32[]{:S(2)}) copy-start(bf16[256,1536]{1,0:T(8,128)(2,1)} %copy-done) | copy-start | bytes 2359300
  131.0 15.3 %collective-permute-start.9 = (f32[256,32]{0,1:T(8,128)S(1)}, f32[256,32]{0,1:T(8,128)S(1)}, u32[]{:S(2)}, u32[]{:S(2)}) collective-permute-start(f32[256,32]{0,1:T(8,128)S(1)} %add.84), channel_id=1, source_target_pairs={{0,16},{4,20},{8,24},{12,28},{16,0},{20,4},{24,8},{28,12},{1,17},{... | collective-permute-start | bytes 98312 | tf_op jit(solution)/shard_map/ppermute | solution.py:25
  131.0 1.2 copy-start.3
  132.2 14.0 %copy-start.10 = (f32[3072,32]{0,1:T(8,128)S(1)}, f32[3072,32]{0,1:T(8,128)}, u32[]{:S(2)}) copy-start(f32[3072,32]{0,1:T(8,128)} %param.7) | copy-start | bytes 1179652
Sparse Core Ops, SparseCore 0:
  10.7 65.0 all-gather.1

commit v13 on v11

--- a/solution.py
+++ b/solution.py
@@ -85,8 +85,8 @@
 def normal_rows(left, right, total_rows, first_row, previous):
     epochs, rows = left.shape
     width = right.shape[1]
-    tile_rows = 512 if rows % 512 == 0 else rows
-    tile_cols = 2048 if width % 2048 == 0 else width
+    tile_rows = 256 if rows % 256 == 0 else rows
+    tile_cols = width
     row_offset = first_row // tile_rows
     in_specs = [
         pl.BlockSpec((epochs, tile_rows), lambda j, i: (0, i)),

time: 153 us -> 152 us (level)
  no operation moved by 1% of the time
where the time goes in v13:
time: 152 us; the launch traced here: 151 us
  waiting for transfers between devices  74.3 us (49%)
  Pallas kernels  26.8 us (18%)
  between operations  15.9 us (10%)
  starting transfers between devices  13.1 us (9%)
  matrix products  12.9 us (8%)
  other arithmetic  5.48 us (4%)
  local copies, waits for them, and re-layouts  2.9 us (2%)
    all_gather x1, waiting for transfers between devices, body(): whole_panel = lax.all_gather(design, 'row', axis=0, tiled=True)  64.2 us
    pallas_call x2, Pallas kernels, normal_rows(): pl.pallas_call(kernel, grid=(width // tile_cols, rows // tile_rows), in_s...  26.8 us
    ppermute x4, starting transfers between devices, tree_broadcast(): arrived = lax.ppermute(block, ('row', 'col'), pairs)  12.2 us
    ppermute x5, waiting for transfers between devices, swap(): return lax.ppermute(block, axis, [(i, i ^ bit) for i in range(count)])  5.95 us
    dot_general x2, matrix products, whiten_rows(): jnp.dot(filter_matrix, block, preferred_element_type=jnp.float32)  4.84 us
    ppermute x4, waiting for transfers between devices, tree_broadcast(): arrived = lax.ppermute(block, ('row', 'col'), pairs)  3.5 us
    select_n x4, other arithmetic, tree_broadcast(): jnp.where((offset & ~done == 0) & (offset & bit != 0), arrived, block)  3.5 us
  transfers between devices with their start and end apart: 10, of which 4 were waited for; matrix products, arithmetic and copies ran while one was open for 9% of the time, Pallas kernels for 18%

profile of v13, /device:TPU:0, one launch (start us, length us, event | category | flops | bytes accessed | tf_op | source)
XLA Modules:
  0.0 151.4 jit_solution(7559564643125347668)
XLA Ops:
  7.2 0.0 all-gather.2.cloned.1.call-start
  7.2 0.7 all-gather.2.cloned.1.call-update
  7.9 0.7 concatenate.6
  8.6 0.1 broadcast_bitcast_fusion
  8.7 0.1 copy.8
  8.8 0.4 reshape.20
  9.2 0.0 copy-start.4
  9.2 64.2 %all-gather.2.cloned.1.call-done = bf16[256,6144]{1,0:T(8,128)(2,1)} async-done(((bf16[32,6144]{1,0:T(8,128)(2,1)}), bf16[256,6144]{1,0:T(8,128)(2,1)}) %all-gather.2.cloned.1.call-update) | async-done | bytes 3145744 | tf_op jit(solution)/shard_map/all_gather | solution.py:135
  73.4 2.4 %convolution_convert_fusion.1 = bf16[256,1536]{1,0:T(8,128)(2,1)} fusion(bf16[256,6144]{1,0:T(8,128)(2,1)} %all-gather.2.cloned.1.call-done, s32[]{:T(128)S(6)} %select_n.45, f32[256,511]{1,0:T(8,128)S(1)} %reshape.20), kind=kOutput, calls=%fused_computation.13 | convolution fusion | flops 201981952 | bytes 1835012 | tf_op jit(solution)/shard_map/dot_general | solution.py:144
  75.8 4.3 %collective-permute-start = (bf16[256,1536]{1,0:T(8,128)(2,1)}, bf16[256,1536]{1,0:T(8,128)(2,1)}, u32[]{:S(2)}, u32[]{:S(2)}) collective-permute-start(bf16[256,1536]{1,0:T(8,128)(2,1)} %convolution_convert_fusion.1), channel_id=1, source_target_pairs={{0,2},{4,6},{9,11},{13,15},{18,16},{22,20},{27,25},{31,29}} | collective-permute-start | bytes 2359304 | tf_op jit(solution)/shard_map/ppermute | solution.py:68
  80.0 0.0 copy-done.4
  80.0 2.4 %convolution_convert_fusion.2 = bf16[256,1536]{1,0:T(8,128)(2,1)} fusion(bf16[256,6144]{1,0:T(8,128)(2,1)} %all-gather.2.cloned.1.call-done, s32[]{:T(128)S(6)} %select_n.44, f32[256,511]{1,0:T(8,128)S(1)} %reshape.20), kind=kOutput, calls=%fused_computation.14 | convolution fusion | flops 201981952 | bytes 1835012 | tf_op jit(solution)/shard_map/dot_general | solution.py:144
  82.5 3.0 %convolution_convert_fusion.right_ref = bf16[256,6144]{1,0:T(8,128)(2,1)S(1)} fusion(bf16[256,6144]{1,0:T(8,128)(2,1)} %all-gather.2.cloned.1.call-done, f32[256,511]{1,0:T(8,128)} %copy-done.4), kind=kOutput, calls=%fused_computation.3 | convolution fusion | flops 807141376 | bytes 6553600 | tf_op jit(solution)/shard_map/dot_general | solution.py:136
  85.5 3.5 %collective-permute-done = bf16[256,1536]{1,0:T(8,128)(2,1)} collective-permute-done((bf16[256,1536]{1,0:T(8,128)(2,1)}, bf16[256,1536]{1,0:T(8,128)(2,1)}, u32[]{:S(2)}, u32[]{:S(2)}) %collective-permute-start) | collective-permute-done | bytes 786464 | tf_op jit(solution)/shard_map/ppermute | solution.py:68
  89.0 2.1 %broadcast_select_fusion.1 = bf16[256,1536]{1,0:T(8,128)(2,1)} fusion(bf16[256,1536]{1,0:T(8,128)(2,1)} %collective-permute-done, bf16[256,1536]{1,0:T(8,128)(2,1)} %convolution_convert_fusion.1, pred[]{:T(512)S(6)} %and.43), kind=kLoop, calls=%fused_computation.21 | loop fusion | flops 393216 | bytes 2359297 | tf_op jit(solution)/shard_map/jit(_where)/select_n | solution.py:70
  91.0 2.2 %collective-permute-start.2 = (bf16[256,1536]{1,0:T(8,128)(2,1)}, bf16[256,1536]{1,0:T(8,128)(2,1)}, u32[]{:S(2)}, u32[]{:S(2)}) collective-permute-start(bf16[256,1536]{1,0:T(8,128)(2,1)} %broadcast_select_fusion.1), channel_id=1, source_target_pairs={{0,1},{2,3},{4,5},{6,7},{9,8},{11,10},{13,12},{15,14},{16,17},{18,... | collective-permute-start | bytes 2359304 | tf_op jit(solution)/shard_map/ppermute | solution.py:68
  94.5 4.4 %collective-permute-start.1 = (bf16[256,1536]{1,0:T(8,128)(2,1)}, bf16[256,1536]{1,0:T(8,128)(2,1)S(1)}, u32[]{:S(2)}, u32[]{:S(2)}) collective-permute-start(bf16[256,1536]{1,0:T(8,128)(2,1)} %convolution_convert_fusion.2), channel_id=1, source_target_pairs={{0,2},{4,6},{9,11},{13,15},{18,16},{22,20},{27,25},{31,29}} | collective-permute-start | bytes 2359304 | tf_op jit(solution)/shard_map/ppermute | solution.py:68
  99.0 0.7 fusion.1
  99.7 0.0 collective-permute-done.2
  99.7 1.2 broadcast_select_fusion.3.left_ref
  100.9 0.0 copy-start
  100.9 0.0 copy-start.5
  100.9 13.4 %shard_map.68.rest_0_ = f32[3072,6144]{1,0:T(8,128)} custom-call(bf16[256,1536]{1,0:T(8,128)(2,1)S(1)} %broadcast_select_fusion.3.left_ref, bf16[256,6144]{1,0:T(8,128)(2,1)S(1)} %convolution_convert_fusion.right_ref), custom_call_target="tpu_custom_call" | custom-call | flops 4831838208 | bytes 41680896 | tf_op jit(solution)/shard_map/pallas_call | solution.py:105
  114.3 0.0 collective-permute-done.1
  114.3 0.0 copy-done.5
  114.3 0.1 broadcast_select_fusion
  114.4 1.3 collective-permute-start.3
  115.8 1.8 %fusion = f32[256,256]{1,0:T(8,128)S(1)} fusion(bf16[256,6144]{1,0:T(8,128)(2,1)S(1)} %convolution_convert_fusion.right_ref, f32[6144]{0:T(1024)S(1)} %broadcast_add_fusion), kind=kOutput, calls=%fused_computation.2 | convolution fusion | flops 2419064832 | bytes 3432448 | tf_op jit(solution)/shard_map/dot_general | solution.py:150
  117.6 0.0 copy-start.6
  117.6 0.1 collective-permute-start.7
  117.7 0.0 collective-permute-done.3
  117.7 0.1 broadcast_select_fusion.2.left_ref
  117.8 0.0 copy-start.2
  117.8 0.3 multiply_reduce_fusion
  118.2 0.0 copy-done
  118.2 0.4 copy-done.6
  118.6 1.0 fusion.10
  119.6 0.0 copy-done.2
  119.6 0.6 collective-permute-start.4
  120.2 3.4 %collective-permute-done.4 = f32[256,32]{0,1:T(8,128)S(1)} collective-permute-done((f32[256,32]{0,1:T(8,128)S(1)}, f32[256,32]{0,1:T(8,128)S(1)}, u32[]{:S(2)}, u32[]{:S(2)}) %collective-permute-start.4) | collective-permute-done | bytes 32800 | tf_op jit(solution)/shard_map/ppermute | solution.py:25
  123.6 0.0 collective-permute-start.5
  123.9 0.0 collective-permute-done.7
  123.9 1.0 add.90
  124.9 0.1 collective-permute-start.8
  125.0 2.6 %collective-permute-done.5 = f32[256,32]{0,1:T(8,128)S(1)} collective-permute-done((f32[256,32]{0,1:T(8,128)S(1)}, f32[256,32]{0,1:T(8,128)S(1)}, u32[]{:S(2)}, u32[]{:S(2)}) %collective-permute-start.5) | collective-permute-done | bytes 32800 | tf_op jit(solution)/shard_map/ppermute | solution.py:25
  127.5 0.0 copy-start.1
  127.5 0.1 collective-permute-start.6
  127.6 0.0 copy-start.3
  127.6 1.2 copy-done.3
  128.8 0.0 copy-start.7
  128.8 13.4 %shard_map.69 = f32[3072,6144]{1,0:T(8,128)} custom-call(bf16[256,1536]{1,0:T(8,128)(2,1)S(1)} %copy-done.3, bf16[256,6144]{1,0:T(8,128)(2,1)S(1)} %convolution_convert_fusion.right_ref, f32[3072,6144]{1,0:T(8,128)} %shard_map.68.rest_0_), custom_call_target="tpu_custom_call", output_to_operand_aliasing={{}: (2, {})} | custom-call | flops 4831838208 | bytes 41680896 | tf_op jit(solution)/shard_map/pallas_call | solution.py:105
  142.2 0.0 collective-permute-done.6
  142.2 0.0 copy-done.1
  142.2 0.0 copy-done.7
  142.2 0.6 convolution_subtract_fusion.1
  142.8 0.0 collective-permute-done.8
  142.8 0.3 fusion.7
  143.1 1.4 fusion.5
  (4 shorter events, 0.0 us)
Async XLA Ops:
  7.2 66.2 %all-gather.2.cloned.1.call-start = ((), (), s32[]{:S(2)}) async-start(), calls=%async_computation | async-start | bytes 3538944 | tf_op jit(solution)/shard_map/all_gather | solution.py:135
  9.2 70.8 %copy-start.4 = (f32[256,511]{1,0:T(8,128)}, f32[256,511]{1,0:T(8,128)S(1)}, u32[]{:S(2)}) copy-start(f32[256,511]{1,0:T(8,128)S(1)} %reshape.20) | copy-start | bytes 1569796
  75.8 13.2 %collective-permute-start = (bf16[256,1536]{1,0:T(8,128)(2,1)}, bf16[256,1536]{1,0:T(8,128)(2,1)}, u32[]{:S(2)}, u32[]{:S(2)}) collective-permute-start(bf16[256,1536]{1,0:T(8,128)(2,1)} %convolution_convert_fusion.1), channel_id=1, source_target_pairs={{0,2},{4,6},{9,11},{13,15},{18,16},{22,20},{27,25},{31,29}} | collective-permute-start | bytes 2359304 | tf_op jit(solution)/shard_map/ppermute | solution.py:68
  91.0 8.6 %collective-permute-start.2 = (bf16[256,1536]{1,0:T(8,128)(2,1)}, bf16[256,1536]{1,0:T(8,128)(2,1)}, u32[]{:S(2)}, u32[]{:S(2)}) collective-permute-start(bf16[256,1536]{1,0:T(8,128)(2,1)} %broadcast_select_fusion.1), channel_id=1, source_target_pairs={{0,1},{2,3},{4,5},{6,7},{9,8},{11,10},{13,12},{15,14},{16,17},{18,... | collective-permute-start | bytes 2359304 | tf_op jit(solution)/shard_map/ppermute | solution.py:68
  94.5 19.8 %collective-permute-start.1 = (bf16[256,1536]{1,0:T(8,128)(2,1)}, bf16[256,1536]{1,0:T(8,128)(2,1)S(1)}, u32[]{:S(2)}, u32[]{:S(2)}) collective-permute-start(bf16[256,1536]{1,0:T(8,128)(2,1)} %convolution_convert_fusion.2), channel_id=1, source_target_pairs={{0,2},{4,6},{9,11},{13,15},{18,16},{22,20},{27,25},{31,29}} | collective-permute-start | bytes 2359304 | tf_op jit(solution)/shard_map/ppermute | solution.py:68
  100.9 17.3 %copy-start = (bf16[256,1536]{1,0:T(8,128)(2,1)}, bf16[256,1536]{1,0:T(8,128)(2,1)S(1)}, u32[]{:S(2)}) copy-start(bf16[256,1536]{1,0:T(8,128)(2,1)S(1)} %broadcast_select_fusion.3.left_ref) | copy-start | bytes 2359300
  100.9 13.4 %copy-start.5 = (bf16[256,1536]{1,0:T(8,128)(2,1)S(1)}, bf16[256,1536]{1,0:T(8,128)(2,1)}, u32[]{:S(2)}) copy-start(bf16[256,1536]{1,0:T(8,128)(2,1)} %convolution_convert_fusion.2) | copy-start | bytes 2359300
  114.4 3.3 %collective-permute-start.3 = (bf16[256,1536]{1,0:T(8,128)(2,1)S(1)}, bf16[256,1536]{1,0:T(8,128)(2,1)S(1)}, u32[]{:S(2)}, u32[]{:S(2)}) collective-permute-start(bf16[256,1536]{1,0:T(8,128)(2,1)S(1)} %broadcast_select_fusion), channel_id=1, source_target_pairs={{0,1},{2,3},{4,5},{6,7},{9,8},{11,10},{13,12},{15,14},{16,17},{18,... | collective-permute-start | bytes 2359304 | tf_op jit(solution)/shard_map/ppermute | solution.py:68
  117.6 1.0 copy-start.6
  117.6 6.3 %collective-permute-start.7 = (f32[256,256]{1,0:T(8,128)S(1)}, f32[256,256]{1,0:T(8,128)}, u32[]{:S(2)}, u32[]{:S(2)}) collective-permute-start(f32[256,256]{1,0:T(8,128)S(1)} %fusion), channel_id=1, source_target_pairs={{0,1},{1,0},{2,3},{3,2},{4,5},{5,4},{6,7},{7,6},{8,9},{9,8},{10,11... | collective-permute-start | bytes 786440 | tf_op jit(solution)/shard_map/ppermute | solution.py:25
  117.8 1.8 %copy-start.2 = (bf16[256,1536]{1,0:T(8,128)(2,1)}, bf16[256,1536]{1,0:T(8,128)(2,1)S(1)}, u32[]{:S(2)}) copy-start(bf16[256,1536]{1,0:T(8,128)(2,1)S(1)} %broadcast_select_fusion.2.left_ref) | copy-start | bytes 2359300
  119.6 4.0 %collective-permute-start.4 = (f32[256,32]{0,1:T(8,128)S(1)}, f32[256,32]{0,1:T(8,128)S(1)}, u32[]{:S(2)}, u32[]{:S(2)}) collective-permute-start(f32[256,32]{0,1:T(8,128)S(1)} %fusion.10), channel_id=1, source_target_pairs={{0,4},{4,0},{8,12},{12,8},{16,20},{20,16},{24,28},{28,24},{1,5},{5... | collective-permute-start | bytes 98312 | tf_op jit(solution)/shard_map/ppermute | solution.py:25
  123.6 3.9 %collective-permute-start.5 = (f32[256,32]{0,1:T(8,128)S(1)}, f32[256,32]{0,1:T(8,128)S(1)}, u32[]{:S(2)}, u32[]{:S(2)}) collective-permute-start(f32[256,32]{0,1:T(8,128)S(1)} %add.83), channel_id=1, source_target_pairs={{0,8},{4,12},{8,0},{12,4},{16,24},{20,28},{24,16},{28,20},{1,9},{5... | collective-permute-start | bytes 98312 | tf_op jit(solution)/shard_map/ppermute | solution.py:25
  124.9 18.0 %collective-permute-start.8 = (f32[256,256]{1,0:T(8,128)S(1)}, f32[256,256]{1,0:T(8,128)S(1)}, u32[]{:S(2)}, u32[]{:S(2)}) collective-permute-start(f32[256,256]{1,0:T(8,128)S(1)} %add.90), channel_id=1, source_target_pairs={{0,2},{1,3},{2,0},{3,1},{4,6},{5,7},{6,4},{7,5},{8,10},{9,11},{10,... | collective-permute-start | bytes 786440 | tf_op jit(solution)/shard_map/ppermute | solution.py:25
  127.5 14.7 %copy-start.1 = (bf16[256,1536]{1,0:T(8,128)(2,1)S(1)}, bf16[256,1536]{1,0:T(8,128)(2,1)}, u32[]{:S(2)}) copy-start(bf16[256,1536]{1,0:T(8,128)(2,1)} %copy-done) | copy-start | bytes 2359300
  127.5 14.7 %collective-permute-start.6 = (f32[256,32]{0,1:T(8,128)S(1)}, f32[256,32]{0,1:T(8,128)S(1)}, u32[]{:S(2)}, u32[]{:S(2)}) collective-permute-start(f32[256,32]{0,1:T(8,128)S(1)} %add.84), channel_id=1, source_target_pairs={{0,16},{4,20},{8,24},{12,28},{16,0},{20,4},{24,8},{28,12},{1,17},{... | collective-permute-start | bytes 98312 | tf_op jit(solution)/shard_map/ppermute | solution.py:25
  127.6 1.2 copy-start.3
  128.8 13.4 %copy-start.7 = (f32[3072,32]{0,1:T(8,128)S(1)}, f32[3072,32]{0,1:T(8,128)}, u32[]{:S(2)}) copy-start(f32[3072,32]{0,1:T(8,128)} %param.7) | copy-start | bytes 1179652
Sparse Core Ops, SparseCore 0:
  10.2 63.1 all-gather.1

commit v14 on v13

--- a/solution.py
+++ b/solution.py
@@ -85,7 +85,7 @@
 def normal_rows(left, right, total_rows, first_row, previous):
     epochs, rows = left.shape
     width = right.shape[1]
-    tile_rows = 256 if rows % 256 == 0 else rows
+    tile_rows = 512 if rows % 512 == 0 else rows
     tile_cols = width
     row_offset = first_row // tile_rows
     in_specs = [

time: 152 us -> 154 us (1.013)
  Pallas kernels: 26.8 us -> 29.2 us
    pallas_call x2, Pallas kernels: 26.8 us -> 29.2 us  [normal_rows(): pl.pallas_call(kernel, grid=(width // tile_cols, rows // tile_rows), in_s...]
  transfers between devices with their start and end apart: 10 -> 10, of which waited for: 4 -> 4; matrix products, arithmetic and copies ran while one was open for 9% -> 9% of each run, Pallas kernels for 18% -> 19%
where the time goes in v14:
time: 154 us
  waiting for transfers between devices  74.3 us (48%)
  Pallas kernels  29.2 us (19%)
  between operations  15.9 us (10%)
  starting transfers between devices  13.1 us (9%)
  matrix products  12.9 us (8%)
  other arithmetic  5.48 us (4%)
  local copies, waits for them, and re-layouts  2.9 us (2%)
    all_gather x1, waiting for transfers between devices, body(): whole_panel = lax.all_gather(design, 'row', axis=0, tiled=True)  64.2 us
    pallas_call x2, Pallas kernels, normal_rows(): pl.pallas_call(kernel, grid=(width // tile_cols, rows // tile_rows), in_s...  29.2 us
    ppermute x4, starting transfers between devices, tree_broadcast(): arrived = lax.ppermute(block, ('row', 'col'), pairs)  12.2 us
    ppermute x5, waiting for transfers between devices, swap(): return lax.ppermute(block, axis, [(i, i ^ bit) for i in range(count)])  5.95 us
    dot_general x2, matrix products, whiten_rows(): jnp.dot(filter_matrix, block, preferred_element_type=jnp.float32)  4.84 us
    ppermute x4, waiting for transfers between devices, tree_broadcast(): arrived = lax.ppermute(block, ('row', 'col'), pairs)  3.5 us
    select_n x4, other arithmetic, tree_broadcast(): jnp.where((offset & ~done == 0) & (offset & bit != 0), arrived, block)  3.5 us
  transfers between devices with their start and end apart: 10, of which 4 were waited for; matrix products, arithmetic and copies ran while one was open for 9% of the time, Pallas kernels for 19%

profile of v14, /device:TPU:0, one launch (start us, length us, event | category | flops | bytes accessed | tf_op | source)
XLA Modules:
  0.0 153.8 jit_solution(4126568809628807612)
XLA Ops:
  7.2 0.0 all-gather.2.cloned.1.call-start
  7.2 0.7 all-gather.2.cloned.1.call-update
  7.9 0.7 concatenate.6
  8.6 0.1 broadcast_bitcast_fusion
  8.7 0.1 copy.8
  8.8 0.4 reshape.20
  9.2 0.0 copy-start.4
  9.2 64.2 %all-gather.2.cloned.1.call-done = bf16[256,6144]{1,0:T(8,128)(2,1)} async-done(((bf16[32,6144]{1,0:T(8,128)(2,1)}), bf16[256,6144]{1,0:T(8,128)(2,1)}) %all-gather.2.cloned.1.call-update) | async-done | bytes 3145744 | tf_op jit(solution)/shard_map/all_gather | solution.py:135
  73.4 2.4 %convolution_convert_fusion.1 = bf16[256,1536]{1,0:T(8,128)(2,1)} fusion(bf16[256,6144]{1,0:T(8,128)(2,1)} %all-gather.2.cloned.1.call-done, s32[]{:T(128)S(6)} %select_n.45, f32[256,511]{1,0:T(8,128)S(1)} %reshape.20), kind=kOutput, calls=%fused_computation.13 | convolution fusion | flops 201981952 | bytes 1835012 | tf_op jit(solution)/shard_map/dot_general | solution.py:144
  75.8 4.3 %collective-permute-start = (bf16[256,1536]{1,0:T(8,128)(2,1)}, bf16[256,1536]{1,0:T(8,128)(2,1)}, u32[]{:S(2)}, u32[]{:S(2)}) collective-permute-start(bf16[256,1536]{1,0:T(8,128)(2,1)} %convolution_convert_fusion.1), channel_id=1, source_target_pairs={{0,2},{4,6},{9,11},{13,15},{18,16},{22,20},{27,25},{31,29}} | collective-permute-start | bytes 2359304 | tf_op jit(solution)/shard_map/ppermute | solution.py:68
  80.0 0.0 copy-done.4
  80.0 2.4 %convolution_convert_fusion.2 = bf16[256,1536]{1,0:T(8,128)(2,1)} fusion(bf16[256,6144]{1,0:T(8,128)(2,1)} %all-gather.2.cloned.1.call-done, s32[]{:T(128)S(6)} %select_n.44, f32[256,511]{1,0:T(8,128)S(1)} %reshape.20), kind=kOutput, calls=%fused_computation.14 | convolution fusion | flops 201981952 | bytes 1835012 | tf_op jit(solution)/shard_map/dot_general | solution.py:144
  82.5 3.0 %convolution_convert_fusion.right_ref = bf16[256,6144]{1,0:T(8,128)(2,1)S(1)} fusion(bf16[256,6144]{1,0:T(8,128)(2,1)} %all-gather.2.cloned.1.call-done, f32[256,511]{1,0:T(8,128)} %copy-done.4), kind=kOutput, calls=%fused_computation.3 | convolution fusion | flops 807141376 | bytes 6553600 | tf_op jit(solution)/shard_map/dot_general | solution.py:136
  85.5 3.5 %collective-permute-done = bf16[256,1536]{1,0:T(8,128)(2,1)} collective-permute-done((bf16[256,1536]{1,0:T(8,128)(2,1)}, bf16[256,1536]{1,0:T(8,128)(2,1)}, u32[]{:S(2)}, u32[]{:S(2)}) %collective-permute-start) | collective-permute-done | bytes 786464 | tf_op jit(solution)/shard_map/ppermute | solution.py:68
  89.0 2.1 %broadcast_select_fusion.1 = bf16[256,1536]{1,0:T(8,128)(2,1)} fusion(bf16[256,1536]{1,0:T(8,128)(2,1)} %collective-permute-done, bf16[256,1536]{1,0:T(8,128)(2,1)} %convolution_convert_fusion.1, pred[]{:T(512)S(6)} %and.43), kind=kLoop, calls=%fused_computation.21 | loop fusion | flops 393216 | bytes 2359297 | tf_op jit(solution)/shard_map/jit(_where)/select_n | solution.py:70
  91.0 2.2 %collective-permute-start.2 = (bf16[256,1536]{1,0:T(8,128)(2,1)}, bf16[256,1536]{1,0:T(8,128)(2,1)}, u32[]{:S(2)}, u32[]{:S(2)}) collective-permute-start(bf16[256,1536]{1,0:T(8,128)(2,1)} %broadcast_select_fusion.1), channel_id=1, source_target_pairs={{0,1},{2,3},{4,5},{6,7},{9,8},{11,10},{13,12},{15,14},{16,17},{18,... | collective-permute-start | bytes 2359304 | tf_op jit(solution)/shard_map/ppermute | solution.py:68
  94.5 4.4 %collective-permute-start.1 = (bf16[256,1536]{1,0:T(8,128)(2,1)}, bf16[256,1536]{1,0:T(8,128)(2,1)S(1)}, u32[]{:S(2)}, u32[]{:S(2)}) collective-permute-start(bf16[256,1536]{1,0:T(8,128)(2,1)} %convolution_convert_fusion.2), channel_id=1, source_target_pairs={{0,2},{4,6},{9,11},{13,15},{18,16},{22,20},{27,25},{31,29}} | collective-permute-start | bytes 2359304 | tf_op jit(solution)/shard_map/ppermute | solution.py:68
  99.0 0.7 fusion.1
  99.7 0.0 collective-permute-done.2
  99.7 1.2 broadcast_select_fusion.3.left_ref
  100.9 0.0 copy-start
  100.9 0.0 copy-start.5
  100.9 14.6 %shard_map.68.rest_0_ = f32[3072,6144]{1,0:T(8,128)} custom-call(bf16[256,1536]{1,0:T(8,128)(2,1)S(1)} %broadcast_select_fusion.3.left_ref, bf16[256,6144]{1,0:T(8,128)(2,1)S(1)} %convolution_convert_fusion.right_ref), custom_call_target="tpu_custom_call" | custom-call | flops 4831838208 | bytes 41680896 | tf_op jit(solution)/shard_map/pallas_call | solution.py:105
  115.5 0.0 collective-permute-done.1
  115.5 0.0 copy-done.5
  115.5 0.1 broadcast_select_fusion
  115.6 1.3 collective-permute-start.3
  117.0 1.8 %fusion = f32[256,256]{1,0:T(8,128)S(1)} fusion(bf16[256,6144]{1,0:T(8,128)(2,1)S(1)} %convolution_convert_fusion.right_ref, f32[6144]{0:T(1024)S(1)} %broadcast_add_fusion), kind=kOutput, calls=%fused_computation.2 | convolution fusion | flops 2419064832 | bytes 3432448 | tf_op jit(solution)/shard_map/dot_general | solution.py:150
  118.8 0.0 copy-start.6
  118.8 0.1 collective-permute-start.7
  118.9 0.0 collective-permute-done.3
  118.9 0.1 broadcast_select_fusion.2.left_ref
  119.0 0.0 copy-start.2
  119.0 0.3 multiply_reduce_fusion
  119.4 0.0 copy-done
  119.4 0.4 copy-done.6
  119.8 1.0 fusion.10
  120.8 0.0 copy-done.2
  120.8 0.6 collective-permute-start.4
  121.4 3.4 %collective-permute-done.4 = f32[256,32]{0,1:T(8,128)S(1)} collective-permute-done((f32[256,32]{0,1:T(8,128)S(1)}, f32[256,32]{0,1:T(8,128)S(1)}, u32[]{:S(2)}, u32[]{:S(2)}) %collective-permute-start.4) | collective-permute-done | bytes 32800 | tf_op jit(solution)/shard_map/ppermute | solution.py:25
  124.8 0.0 collective-permute-start.5
  125.1 0.0 collective-permute-done.7
  125.1 1.0 add.90
  126.1 0.1 collective-permute-start.8
  126.2 2.6 %collective-permute-done.5 = f32[256,32]{0,1:T(8,128)S(1)} collective-permute-done((f32[256,32]{0,1:T(8,128)S(1)}, f32[256,32]{0,1:T(8,128)S(1)}, u32[]{:S(2)}, u32[]{:S(2)}) %collective-permute-start.5) | collective-permute-done | bytes 32800 | tf_op jit(solution)/shard_map/ppermute | solution.py:25
  128.7 0.0 copy-start.1
  128.7 0.1 collective-permute-start.6
  128.8 0.0 copy-start.3
  128.8 1.2 copy-done.3
  130.0 0.0 copy-start.7
  130.0 14.6 %shard_map.69 = f32[3072,6144]{1,0:T(8,128)} custom-call(bf16[256,1536]{1,0:T(8,128)(2,1)S(1)} %copy-done.3, bf16[256,6144]{1,0:T(8,128)(2,1)S(1)} %convolution_convert_fusion.right_ref, f32[3072,6144]{1,0:T(8,128)} %shard_map.68.rest_0_), custom_call_target="tpu_custom_call", output_to_operand_aliasing={{}: (2, {})} | custom-call | flops 4831838208 | bytes 41680896 | tf_op jit(solution)/shard_map/pallas_call | solution.py:105
  144.6 0.0 collective-permute-done.6
  144.6 0.0 copy-done.1
  144.6 0.0 copy-done.7
  144.6 0.6 convolution_subtract_fusion.1
  145.2 0.0 collective-permute-done.8
  145.2 0.3 fusion.7
  145.5 1.4 fusion.5
  (4 shorter events, 0.0 us)
Async XLA Ops:
  7.2 66.2 %all-gather.2.cloned.1.call-start = ((), (), s32[]{:S(2)}) async-start(), calls=%async_computation | async-start | bytes 3538944 | tf_op jit(solution)/shard_map/all_gather | solution.py:135
  9.2 70.8 %copy-start.4 = (f32[256,511]{1,0:T(8,128)}, f32[256,511]{1,0:T(8,128)S(1)}, u32[]{:S(2)}) copy-start(f32[256,511]{1,0:T(8,128)S(1)} %reshape.20) | copy-start | bytes 1569796
  75.8 13.2 %collective-permute-start = (bf16[256,1536]{1,0:T(8,128)(2,1)}, bf16[256,1536]{1,0:T(8,128)(2,1)}, u32[]{:S(2)}, u32[]{:S(2)}) collective-permute-start(bf16[256,1536]{1,0:T(8,128)(2,1)} %convolution_convert_fusion.1), channel_id=1, source_target_pairs={{0,2},{4,6},{9,11},{13,15},{18,16},{22,20},{27,25},{31,29}} | collective-permute-start | bytes 2359304 | tf_op jit(solution)/shard_map/ppermute | solution.py:68
  91.0 8.6 %collective-permute-start.2 = (bf16[256,1536]{1,0:T(8,128)(2,1)}, bf16[256,1536]{1,0:T(8,128)(2,1)}, u32[]{:S(2)}, u32[]{:S(2)}) collective-permute-start(bf16[256,1536]{1,0:T(8,128)(2,1)} %broadcast_select_fusion.1), channel_id=1, source_target_pairs={{0,1},{2,3},{4,5},{6,7},{9,8},{11,10},{13,12},{15,14},{16,17},{18,... | collective-permute-start | bytes 2359304 | tf_op jit(solution)/shard_map/ppermute | solution.py:68
  94.5 21.0 %collective-permute-start.1 = (bf16[256,1536]{1,0:T(8,128)(2,1)}, bf16[256,1536]{1,0:T(8,128)(2,1)S(1)}, u32[]{:S(2)}, u32[]{:S(2)}) collective-permute-start(bf16[256,1536]{1,0:T(8,128)(2,1)} %convolution_convert_fusion.2), channel_id=1, source_target_pairs={{0,2},{4,6},{9,11},{13,15},{18,16},{22,20},{27,25},{31,29}} | collective-permute-start | bytes 2359304 | tf_op jit(solution)/shard_map/ppermute | solution.py:68
  100.9 18.5 %copy-start = (bf16[256,1536]{1,0:T(8,128)(2,1)}, bf16[256,1536]{1,0:T(8,128)(2,1)S(1)}, u32[]{:S(2)}) copy-start(bf16[256,1536]{1,0:T(8,128)(2,1)S(1)} %broadcast_select_fusion.3.left_ref) | copy-start | bytes 2359300
  100.9 14.6 %copy-start.5 = (bf16[256,1536]{1,0:T(8,128)(2,1)S(1)}, bf16[256,1536]{1,0:T(8,128)(2,1)}, u32[]{:S(2)}) copy-start(bf16[256,1536]{1,0:T(8,128)(2,1)} %convolution_convert_fusion.2) | copy-start | bytes 2359300
  115.6 3.3 %collective-permute-start.3 = (bf16[256,1536]{1,0:T(8,128)(2,1)S(1)}, bf16[256,1536]{1,0:T(8,128)(2,1)S(1)}, u32[]{:S(2)}, u32[]{:S(2)}) collective-permute-start(bf16[256,1536]{1,0:T(8,128)(2,1)S(1)} %broadcast_select_fusion), channel_id=1, source_target_pairs={{0,1},{2,3},{4,5},{6,7},{9,8},{11,10},{13,12},{15,14},{16,17},{18,... | collective-permute-start | bytes 2359304 | tf_op jit(solution)/shard_map/ppermute | solution.py:68
  118.8 1.0 copy-start.6
  118.8 6.3 %collective-permute-start.7 = (f32[256,256]{1,0:T(8,128)S(1)}, f32[256,256]{1,0:T(8,128)}, u32[]{:S(2)}, u32[]{:S(2)}) collective-permute-start(f32[256,256]{1,0:T(8,128)S(1)} %fusion), channel_id=1, source_target_pairs={{0,1},{1,0},{2,3},{3,2},{4,5},{5,4},{6,7},{7,6},{8,9},{9,8},{10,11... | collective-permute-start | bytes 786440 | tf_op jit(solution)/shard_map/ppermute | solution.py:25
  119.0 1.8 %copy-start.2 = (bf16[256,1536]{1,0:T(8,128)(2,1)}, bf16[256,1536]{1,0:T(8,128)(2,1)S(1)}, u32[]{:S(2)}) copy-start(bf16[256,1536]{1,0:T(8,128)(2,1)S(1)} %broadcast_select_fusion.2.left_ref) | copy-start | bytes 2359300
  120.8 4.0 %collective-permute-start.4 = (f32[256,32]{0,1:T(8,128)S(1)}, f32[256,32]{0,1:T(8,128)S(1)}, u32[]{:S(2)}, u32[]{:S(2)}) collective-permute-start(f32[256,32]{0,1:T(8,128)S(1)} %fusion.10), channel_id=1, source_target_pairs={{0,4},{4,0},{8,12},{12,8},{16,20},{20,16},{24,28},{28,24},{1,5},{5... | collective-permute-start | bytes 98312 | tf_op jit(solution)/shard_map/ppermute | solution.py:25
  124.8 3.9 %collective-permute-start.5 = (f32[256,32]{0,1:T(8,128)S(1)}, f32[256,32]{0,1:T(8,128)S(1)}, u32[]{:S(2)}, u32[]{:S(2)}) collective-permute-start(f32[256,32]{0,1:T(8,128)S(1)} %add.83), channel_id=1, source_target_pairs={{0,8},{4,12},{8,0},{12,4},{16,24},{20,28},{24,16},{28,20},{1,9},{5... | collective-permute-start | bytes 98312 | tf_op jit(solution)/shard_map/ppermute | solution.py:25
  126.1 19.2 %collective-permute-start.8 = (f32[256,256]{1,0:T(8,128)S(1)}, f32[256,256]{1,0:T(8,128)S(1)}, u32[]{:S(2)}, u32[]{:S(2)}) collective-permute-start(f32[256,256]{1,0:T(8,128)S(1)} %add.90), channel_id=1, source_target_pairs={{0,2},{1,3},{2,0},{3,1},{4,6},{5,7},{6,4},{7,5},{8,10},{9,11},{10,... | collective-permute-start | bytes 786440 | tf_op jit(solution)/shard_map/ppermute | solution.py:25
  128.7 15.9 %copy-start.1 = (bf16[256,1536]{1,0:T(8,128)(2,1)S(1)}, bf16[256,1536]{1,0:T(8,128)(2,1)}, u32[]{:S(2)}) copy-start(bf16[256,1536]{1,0:T(8,128)(2,1)} %copy-done) | copy-start | bytes 2359300
  128.7 15.9 %collective-permute-start.6 = (f32[256,32]{0,1:T(8,128)S(1)}, f32[256,32]{0,1:T(8,128)S(1)}, u32[]{:S(2)}, u32[]{:S(2)}) collective-permute-start(f32[256,32]{0,1:T(8,128)S(1)} %add.84), channel_id=1, source_target_pairs={{0,16},{4,20},{8,24},{12,28},{16,0},{20,4},{24,8},{28,12},{1,17},{... | collective-permute-start | bytes 98312 | tf_op jit(solution)/shard_map/ppermute | solution.py:25
  128.8 1.2 copy-start.3
  130.0 14.6 %copy-start.7 = (f32[3072,32]{0,1:T(8,128)S(1)}, f32[3072,32]{0,1:T(8,128)}, u32[]{:S(2)}) copy-start(f32[3072,32]{0,1:T(8,128)} %param.7) | copy-start | bytes 1179652
Sparse Core Ops, SparseCore 0:
  10.2 63.1 all-gather.1

commit v15 on v14

--- a/solution.py
+++ b/solution.py
@@ -85,7 +85,7 @@
 def normal_rows(left, right, total_rows, first_row, previous):
     epochs, rows = left.shape
     width = right.shape[1]
-    tile_rows = 512 if rows % 512 == 0 else rows
+    tile_rows = 128 if rows % 128 == 0 else rows
     tile_cols = width
     row_offset = first_row // tile_rows
     in_specs = [

time: 154 us -> 155 us (level)
  no operation moved by 1% of the time
where the time goes in v15:
time: 155 us; the launch traced here: 154 us
  waiting for transfers between devices  74.3 us (48%)
  Pallas kernels  29.5 us (19%)
  between operations  15.9 us (10%)
  starting transfers between devices  13.1 us (8%)
  matrix products  12.9 us (8%)
  other arithmetic  5.48 us (4%)
  local copies, waits for them, and re-layouts  2.9 us (2%)
    all_gather x1, waiting for transfers between devices, body(): whole_panel = lax.all_gather(design, 'row', axis=0, tiled=True)  64.2 us
    pallas_call x2, Pallas kernels, normal_rows(): pl.pallas_call(kernel, grid=(width // tile_cols, rows // tile_rows), in_s...  29.5 us
    ppermute x4, starting transfers between devices, tree_broadcast(): arrived = lax.ppermute(block, ('row', 'col'), pairs)  12.2 us
    ppermute x5, waiting for transfers between devices, swap(): return lax.ppermute(block, axis, [(i, i ^ bit) for i in range(count)])  5.97 us
    dot_general x2, matrix products, whiten_rows(): jnp.dot(filter_matrix, block, preferred_element_type=jnp.float32)  4.84 us
    ppermute x4, waiting for transfers between devices, tree_broadcast(): arrived = lax.ppermute(block, ('row', 'col'), pairs)  3.5 us
    select_n x4, other arithmetic, tree_broadcast(): jnp.where((offset & ~done == 0) & (offset & bit != 0), arrived, block)  3.5 us
  transfers between devices with their start and end apart: 10, of which 4 were waited for; matrix products, arithmetic and copies ran while one was open for 9% of the time, Pallas kernels for 19%

profile of v15, /device:TPU:0, one launch (start us, length us, event | category | flops | bytes accessed | tf_op | source)
XLA Modules:
  0.0 154.1 jit_solution(1412396204227568845)
XLA Ops:
  7.2 0.0 all-gather.2.cloned.1.call-start
  7.2 0.7 all-gather.2.cloned.1.call-update
  7.9 0.7 concatenate.6
  8.6 0.1 broadcast_bitcast_fusion
  8.7 0.1 copy.8
  8.8 0.4 reshape.20
  9.2 0.0 copy-start.4
  9.2 64.2 %all-gather.2.cloned.1.call-done = bf16[256,6144]{1,0:T(8,128)(2,1)} async-done(((bf16[32,6144]{1,0:T(8,128)(2,1)}), bf16[256,6144]{1,0:T(8,128)(2,1)}) %all-gather.2.cloned.1.call-update) | async-done | bytes 3145744 | tf_op jit(solution)/shard_map/all_gather | solution.py:135
  73.4 2.4 %convolution_convert_fusion.1 = bf16[256,1536]{1,0:T(8,128)(2,1)} fusion(bf16[256,6144]{1,0:T(8,128)(2,1)} %all-gather.2.cloned.1.call-done, s32[]{:T(128)S(6)} %select_n.45, f32[256,511]{1,0:T(8,128)S(1)} %reshape.20), kind=kOutput, calls=%fused_computation.13 | convolution fusion | flops 201981952 | bytes 1835012 | tf_op jit(solution)/shard_map/dot_general | solution.py:144
  75.8 4.3 %collective-permute-start = (bf16[256,1536]{1,0:T(8,128)(2,1)}, bf16[256,1536]{1,0:T(8,128)(2,1)}, u32[]{:S(2)}, u32[]{:S(2)}) collective-permute-start(bf16[256,1536]{1,0:T(8,128)(2,1)} %convolution_convert_fusion.1), channel_id=1, source_target_pairs={{0,2},{4,6},{9,11},{13,15},{18,16},{22,20},{27,25},{31,29}} | collective-permute-start | bytes 2359304 | tf_op jit(solution)/shard_map/ppermute | solution.py:68
  80.0 0.0 copy-done.4
  80.0 2.4 %convolution_convert_fusion.2 = bf16[256,1536]{1,0:T(8,128)(2,1)} fusion(bf16[256,6144]{1,0:T(8,128)(2,1)} %all-gather.2.cloned.1.call-done, s32[]{:T(128)S(6)} %select_n.44, f32[256,511]{1,0:T(8,128)S(1)} %reshape.20), kind=kOutput, calls=%fused_computation.14 | convolution fusion | flops 201981952 | bytes 1835012 | tf_op jit(solution)/shard_map/dot_general | solution.py:144
  82.5 3.0 %convolution_convert_fusion.right_ref = bf16[256,6144]{1,0:T(8,128)(2,1)S(1)} fusion(bf16[256,6144]{1,0:T(8,128)(2,1)} %all-gather.2.cloned.1.call-done, f32[256,511]{1,0:T(8,128)} %copy-done.4), kind=kOutput, calls=%fused_computation.3 | convolution fusion | flops 807141376 | bytes 6553600 | tf_op jit(solution)/shard_map/dot_general | solution.py:136
  85.5 3.5 %collective-permute-done = bf16[256,1536]{1,0:T(8,128)(2,1)} collective-permute-done((bf16[256,1536]{1,0:T(8,128)(2,1)}, bf16[256,1536]{1,0:T(8,128)(2,1)}, u32[]{:S(2)}, u32[]{:S(2)}) %collective-permute-start) | collective-permute-done | bytes 786464 | tf_op jit(solution)/shard_map/ppermute | solution.py:68
  89.0 2.1 %broadcast_select_fusion.1 = bf16[256,1536]{1,0:T(8,128)(2,1)} fusion(bf16[256,1536]{1,0:T(8,128)(2,1)} %collective-permute-done, bf16[256,1536]{1,0:T(8,128)(2,1)} %convolution_convert_fusion.1, pred[]{:T(512)S(6)} %and.43), kind=kLoop, calls=%fused_computation.21 | loop fusion | flops 393216 | bytes 2359297 | tf_op jit(solution)/shard_map/jit(_where)/select_n | solution.py:70
  91.0 2.2 %collective-permute-start.2 = (bf16[256,1536]{1,0:T(8,128)(2,1)}, bf16[256,1536]{1,0:T(8,128)(2,1)}, u32[]{:S(2)}, u32[]{:S(2)}) collective-permute-start(bf16[256,1536]{1,0:T(8,128)(2,1)} %broadcast_select_fusion.1), channel_id=1, source_target_pairs={{0,1},{2,3},{4,5},{6,7},{9,8},{11,10},{13,12},{15,14},{16,17},{18,... | collective-permute-start | bytes 2359304 | tf_op jit(solution)/shard_map/ppermute | solution.py:68
  94.5 4.4 %collective-permute-start.1 = (bf16[256,1536]{1,0:T(8,128)(2,1)}, bf16[256,1536]{1,0:T(8,128)(2,1)S(1)}, u32[]{:S(2)}, u32[]{:S(2)}) collective-permute-start(bf16[256,1536]{1,0:T(8,128)(2,1)} %convolution_convert_fusion.2), channel_id=1, source_target_pairs={{0,2},{4,6},{9,11},{13,15},{18,16},{22,20},{27,25},{31,29}} | collective-permute-start | bytes 2359304 | tf_op jit(solution)/shard_map/ppermute | solution.py:68
  99.0 0.7 fusion.1
  99.7 0.0 collective-permute-done.2
  99.7 1.2 broadcast_select_fusion.3.left_ref
  100.9 0.0 copy-start
  100.9 0.0 copy-start.5
  100.9 14.8 %shard_map.68.rest_0_ = f32[3072,6144]{1,0:T(8,128)} custom-call(bf16[256,1536]{1,0:T(8,128)(2,1)S(1)} %broadcast_select_fusion.3.left_ref, bf16[256,6144]{1,0:T(8,128)(2,1)S(1)} %convolution_convert_fusion.right_ref), custom_call_target="tpu_custom_call" | custom-call | flops 4831838208 | bytes 41680896 | tf_op jit(solution)/shard_map/pallas_call | solution.py:105
  115.7 0.0 collective-permute-done.1
  115.7 0.0 copy-done.5
  115.7 0.1 broadcast_select_fusion
  115.8 1.3 collective-permute-start.3
  117.1 1.8 %fusion = f32[256,256]{1,0:T(8,128)S(1)} fusion(bf16[256,6144]{1,0:T(8,128)(2,1)S(1)} %convolution_convert_fusion.right_ref, f32[6144]{0:T(1024)S(1)} %broadcast_add_fusion), kind=kOutput, calls=%fused_computation.2 | convolution fusion | flops 2419064832 | bytes 3432448 | tf_op jit(solution)/shard_map/dot_general | solution.py:150
  119.0 0.0 copy-start.6
  119.0 0.1 collective-permute-start.7
  119.1 0.0 collective-permute-done.3
  119.1 0.1 broadcast_select_fusion.2.left_ref
  119.2 0.0 copy-start.2
  119.2 0.3 multiply_reduce_fusion
  119.5 0.0 copy-done
  119.5 0.4 copy-done.6
  120.0 1.0 fusion.10
  121.0 0.0 copy-done.2
  121.0 0.6 collective-permute-start.4
  121.6 3.4 %collective-permute-done.4 = f32[256,32]{0,1:T(8,128)S(1)} collective-permute-done((f32[256,32]{0,1:T(8,128)S(1)}, f32[256,32]{0,1:T(8,128)S(1)}, u32[]{:S(2)}, u32[]{:S(2)}) %collective-permute-start.4) | collective-permute-done | bytes 32800 | tf_op jit(solution)/shard_map/ppermute | solution.py:25
  125.0 0.0 collective-permute-start.5
  125.2 0.0 collective-permute-done.7
  125.2 1.0 add.90
  126.2 0.1 collective-permute-start.8
  126.3 2.6 %collective-permute-done.5 = f32[256,32]{0,1:T(8,128)S(1)} collective-permute-done((f32[256,32]{0,1:T(8,128)S(1)}, f32[256,32]{0,1:T(8,128)S(1)}, u32[]{:S(2)}, u32[]{:S(2)}) %collective-permute-start.5) | collective-permute-done | bytes 32800 | tf_op jit(solution)/shard_map/ppermute | solution.py:25
  128.9 0.0 copy-start.1
  128.9 0.1 collective-permute-start.6
  129.0 0.0 copy-start.3
  129.0 1.2 copy-done.3
  130.2 0.0 copy-start.7
  130.2 14.7 %shard_map.69 = f32[3072,6144]{1,0:T(8,128)} custom-call(bf16[256,1536]{1,0:T(8,128)(2,1)S(1)} %copy-done.3, bf16[256,6144]{1,0:T(8,128)(2,1)S(1)} %convolution_convert_fusion.right_ref, f32[3072,6144]{1,0:T(8,128)} %shard_map.68.rest_0_), custom_call_target="tpu_custom_call", output_to_operand_aliasing={{}: (2, {})} | custom-call | flops 4831838208 | bytes 41680896 | tf_op jit(solution)/shard_map/pallas_call | solution.py:105
  144.9 0.0 collective-permute-done.6
  144.9 0.0 copy-done.1
  144.9 0.0 copy-done.7
  144.9 0.6 convolution_subtract_fusion.1
  145.5 0.0 collective-permute-done.8
  145.5 0.3 fusion.7
  145.8 1.4 fusion.5
  (4 shorter events, 0.0 us)
Async XLA Ops:
  7.2 66.2 %all-gather.2.cloned.1.call-start = ((), (), s32[]{:S(2)}) async-start(), calls=%async_computation | async-start | bytes 3538944 | tf_op jit(solution)/shard_map/all_gather | solution.py:135
  9.2 70.8 %copy-start.4 = (f32[256,511]{1,0:T(8,128)}, f32[256,511]{1,0:T(8,128)S(1)}, u32[]{:S(2)}) copy-start(f32[256,511]{1,0:T(8,128)S(1)} %reshape.20) | copy-start | bytes 1569796
  75.8 13.2 %collective-permute-start = (bf16[256,1536]{1,0:T(8,128)(2,1)}, bf16[256,1536]{1,0:T(8,128)(2,1)}, u32[]{:S(2)}, u32[]{:S(2)}) collective-permute-start(bf16[256,1536]{1,0:T(8,128)(2,1)} %convolution_convert_fusion.1), channel_id=1, source_target_pairs={{0,2},{4,6},{9,11},{13,15},{18,16},{22,20},{27,25},{31,29}} | collective-permute-start | bytes 2359304 | tf_op jit(solution)/shard_map/ppermute | solution.py:68
  91.0 8.6 %collective-permute-start.2 = (bf16[256,1536]{1,0:T(8,128)(2,1)}, bf16[256,1536]{1,0:T(8,128)(2,1)}, u32[]{:S(2)}, u32[]{:S(2)}) collective-permute-start(bf16[256,1536]{1,0:T(8,128)(2,1)} %broadcast_select_fusion.1), channel_id=1, source_target_pairs={{0,1},{2,3},{4,5},{6,7},{9,8},{11,10},{13,12},{15,14},{16,17},{18,... | collective-permute-start | bytes 2359304 | tf_op jit(solution)/shard_map/ppermute | solution.py:68
  94.5 21.1 %collective-permute-start.1 = (bf16[256,1536]{1,0:T(8,128)(2,1)}, bf16[256,1536]{1,0:T(8,128)(2,1)S(1)}, u32[]{:S(2)}, u32[]{:S(2)}) collective-permute-start(bf16[256,1536]{1,0:T(8,128)(2,1)} %convolution_convert_fusion.2), channel_id=1, source_target_pairs={{0,2},{4,6},{9,11},{13,15},{18,16},{22,20},{27,25},{31,29}} | collective-permute-start | bytes 2359304 | tf_op jit(solution)/shard_map/ppermute | solution.py:68
  100.9 18.6 %copy-start = (bf16[256,1536]{1,0:T(8,128)(2,1)}, bf16[256,1536]{1,0:T(8,128)(2,1)S(1)}, u32[]{:S(2)}) copy-start(bf16[256,1536]{1,0:T(8,128)(2,1)S(1)} %broadcast_select_fusion.3.left_ref) | copy-start | bytes 2359300
  100.9 14.8 %copy-start.5 = (bf16[256,1536]{1,0:T(8,128)(2,1)S(1)}, bf16[256,1536]{1,0:T(8,128)(2,1)}, u32[]{:S(2)}) copy-start(bf16[256,1536]{1,0:T(8,128)(2,1)} %convolution_convert_fusion.2) | copy-start | bytes 2359300
  115.8 3.3 %collective-permute-start.3 = (bf16[256,1536]{1,0:T(8,128)(2,1)S(1)}, bf16[256,1536]{1,0:T(8,128)(2,1)S(1)}, u32[]{:S(2)}, u32[]{:S(2)}) collective-permute-start(bf16[256,1536]{1,0:T(8,128)(2,1)S(1)} %broadcast_select_fusion), channel_id=1, source_target_pairs={{0,1},{2,3},{4,5},{6,7},{9,8},{11,10},{13,12},{15,14},{16,17},{18,... | collective-permute-start | bytes 2359304 | tf_op jit(solution)/shard_map/ppermute | solution.py:68
  119.0 1.0 copy-start.6
  119.0 6.3 %collective-permute-start.7 = (f32[256,256]{1,0:T(8,128)S(1)}, f32[256,256]{1,0:T(8,128)}, u32[]{:S(2)}, u32[]{:S(2)}) collective-permute-start(f32[256,256]{1,0:T(8,128)S(1)} %fusion), channel_id=1, source_target_pairs={{0,1},{1,0},{2,3},{3,2},{4,5},{5,4},{6,7},{7,6},{8,9},{9,8},{10,11... | collective-permute-start | bytes 786440 | tf_op jit(solution)/shard_map/ppermute | solution.py:25
  119.2 1.8 %copy-start.2 = (bf16[256,1536]{1,0:T(8,128)(2,1)}, bf16[256,1536]{1,0:T(8,128)(2,1)S(1)}, u32[]{:S(2)}) copy-start(bf16[256,1536]{1,0:T(8,128)(2,1)S(1)} %broadcast_select_fusion.2.left_ref) | copy-start | bytes 2359300
  121.0 4.0 %collective-permute-start.4 = (f32[256,32]{0,1:T(8,128)S(1)}, f32[256,32]{0,1:T(8,128)S(1)}, u32[]{:S(2)}, u32[]{:S(2)}) collective-permute-start(f32[256,32]{0,1:T(8,128)S(1)} %fusion.10), channel_id=1, source_target_pairs={{0,4},{4,0},{8,12},{12,8},{16,20},{20,16},{24,28},{28,24},{1,5},{5... | collective-permute-start | bytes 98312 | tf_op jit(solution)/shard_map/ppermute | solution.py:25
  125.0 3.9 %collective-permute-start.5 = (f32[256,32]{0,1:T(8,128)S(1)}, f32[256,32]{0,1:T(8,128)S(1)}, u32[]{:S(2)}, u32[]{:S(2)}) collective-permute-start(f32[256,32]{0,1:T(8,128)S(1)} %add.83), channel_id=1, source_target_pairs={{0,8},{4,12},{8,0},{12,4},{16,24},{20,28},{24,16},{28,20},{1,9},{5... | collective-permute-start | bytes 98312 | tf_op jit(solution)/shard_map/ppermute | solution.py:25
  126.2 19.3 %collective-permute-start.8 = (f32[256,256]{1,0:T(8,128)S(1)}, f32[256,256]{1,0:T(8,128)S(1)}, u32[]{:S(2)}, u32[]{:S(2)}) collective-permute-start(f32[256,256]{1,0:T(8,128)S(1)} %add.90), channel_id=1, source_target_pairs={{0,2},{1,3},{2,0},{3,1},{4,6},{5,7},{6,4},{7,5},{8,10},{9,11},{10,... | collective-permute-start | bytes 786440 | tf_op jit(solution)/shard_map/ppermute | solution.py:25
  128.9 16.0 %copy-start.1 = (bf16[256,1536]{1,0:T(8,128)(2,1)S(1)}, bf16[256,1536]{1,0:T(8,128)(2,1)}, u32[]{:S(2)}) copy-start(bf16[256,1536]{1,0:T(8,128)(2,1)} %copy-done) | copy-start | bytes 2359300
  128.9 16.0 %collective-permute-start.6 = (f32[256,32]{0,1:T(8,128)S(1)}, f32[256,32]{0,1:T(8,128)S(1)}, u32[]{:S(2)}, u32[]{:S(2)}) collective-permute-start(f32[256,32]{0,1:T(8,128)S(1)} %add.84), channel_id=1, source_target_pairs={{0,16},{4,20},{8,24},{12,28},{16,0},{20,4},{24,8},{28,12},{1,17},{... | collective-permute-start | bytes 98312 | tf_op jit(solution)/shard_map/ppermute | solution.py:25
  129.0 1.2 copy-start.3
  130.2 14.7 %copy-start.7 = (f32[3072,32]{0,1:T(8,128)S(1)}, f32[3072,32]{0,1:T(8,128)}, u32[]{:S(2)}) copy-start(f32[3072,32]{0,1:T(8,128)} %param.7) | copy-start | bytes 1179652
Sparse Core Ops, SparseCore 0:
  10.2 63.1 all-gather.1

commit v16 on v13

--- a/solution.py
+++ b/solution.py
@@ -86,7 +86,7 @@
     epochs, rows = left.shape
     width = right.shape[1]
     tile_rows = 256 if rows % 256 == 0 else rows
-    tile_cols = width
+    tile_cols = width // 2 if width % 256 == 0 else width
     row_offset = first_row // tile_rows
     in_specs = [
         pl.BlockSpec((epochs, tile_rows), lambda j, i: (0, i)),

time: 152 us -> 155 us (1.020)
  Pallas kernels: 26.8 us -> 29.8 us
    pallas_call x2, Pallas kernels: 26.8 us -> 29.8 us  [normal_rows(): pl.pallas_call(kernel, grid=(width // tile_cols, rows // tile_rows), in_s...]
  transfers between devices with their start and end apart: 10 -> 10, of which waited for: 4 -> 4; matrix products, arithmetic and copies ran while one was open for 9% -> 9% of each run, Pallas kernels for 18% -> 19%
where the time goes in v16:
time: 155 us; the launch traced here: 154 us
  waiting for transfers between devices  74.3 us (48%)
  Pallas kernels  29.8 us (19%)
  between operations  15.9 us (10%)
  starting transfers between devices  13.1 us (8%)
  matrix products  12.9 us (8%)
  other arithmetic  5.48 us (4%)
  local copies, waits for them, and re-layouts  2.9 us (2%)
    all_gather x1, waiting for transfers between devices, body(): whole_panel = lax.all_gather(design, 'row', axis=0, tiled=True)  64.2 us
    pallas_call x2, Pallas kernels, normal_rows(): pl.pallas_call(kernel, grid=(width // tile_cols, rows // tile_rows), in_s...  29.8 us
    ppermute x4, starting transfers between devices, tree_broadcast(): arrived = lax.ppermute(block, ('row', 'col'), pairs)  12.2 us
    ppermute x5, waiting for transfers between devices, swap(): return lax.ppermute(block, axis, [(i, i ^ bit) for i in range(count)])  5.95 us
    dot_general x2, matrix products, whiten_rows(): jnp.dot(filter_matrix, block, preferred_element_type=jnp.float32)  4.84 us
    ppermute x4, waiting for transfers between devices, tree_broadcast(): arrived = lax.ppermute(block, ('row', 'col'), pairs)  3.5 us
    select_n x4, other arithmetic, tree_broadcast(): jnp.where((offset & ~done == 0) & (offset & bit != 0), arrived, block)  3.5 us
  transfers between devices with their start and end apart: 10, of which 4 were waited for; matrix products, arithmetic and copies ran while one was open for 9% of the time, Pallas kernels for 19%

profile of v16, /device:TPU:0, one launch (start us, length us, event | category | flops | bytes accessed | tf_op | source)
XLA Modules:
  0.0 154.3 jit_solution(13557432586641113250)
XLA Ops:
  7.2 0.0 all-gather.2.cloned.1.call-start
  7.2 0.7 all-gather.2.cloned.1.call-update
  7.9 0.7 concatenate.6
  8.6 0.1 broadcast_bitcast_fusion
  8.7 0.1 copy.8
  8.8 0.4 reshape.20
  9.2 0.0 copy-start.4
  9.2 64.2 %all-gather.2.cloned.1.call-done = bf16[256,6144]{1,0:T(8,128)(2,1)} async-done(((bf16[32,6144]{1,0:T(8,128)(2,1)}), bf16[256,6144]{1,0:T(8,128)(2,1)}) %all-gather.2.cloned.1.call-update) | async-done | bytes 3145744 | tf_op jit(solution)/shard_map/all_gather | solution.py:135
  73.4 2.4 %convolution_convert_fusion.1 = bf16[256,1536]{1,0:T(8,128)(2,1)} fusion(bf16[256,6144]{1,0:T(8,128)(2,1)} %all-gather.2.cloned.1.call-done, s32[]{:T(128)S(6)} %select_n.45, f32[256,511]{1,0:T(8,128)S(1)} %reshape.20), kind=kOutput, calls=%fused_computation.13 | convolution fusion | flops 201981952 | bytes 1835012 | tf_op jit(solution)/shard_map/dot_general | solution.py:144
  75.8 4.3 %collective-permute-start = (bf16[256,1536]{1,0:T(8,128)(2,1)}, bf16[256,1536]{1,0:T(8,128)(2,1)}, u32[]{:S(2)}, u32[]{:S(2)}) collective-permute-start(bf16[256,1536]{1,0:T(8,128)(2,1)} %convolution_convert_fusion.1), channel_id=1, source_target_pairs={{0,2},{4,6},{9,11},{13,15},{18,16},{22,20},{27,25},{31,29}} | collective-permute-start | bytes 2359304 | tf_op jit(solution)/shard_map/ppermute | solution.py:68
  80.0 0.0 copy-done.4
  80.0 2.4 %convolution_convert_fusion.2 = bf16[256,1536]{1,0:T(8,128)(2,1)} fusion(bf16[256,6144]{1,0:T(8,128)(2,1)} %all-gather.2.cloned.1.call-done, s32[]{:T(128)S(6)} %select_n.44, f32[256,511]{1,0:T(8,128)S(1)} %reshape.20), kind=kOutput, calls=%fused_computation.14 | convolution fusion | flops 201981952 | bytes 1835012 | tf_op jit(solution)/shard_map/dot_general | solution.py:144
  82.5 3.0 %convolution_convert_fusion.right_ref = bf16[256,6144]{1,0:T(8,128)(2,1)S(1)} fusion(bf16[256,6144]{1,0:T(8,128)(2,1)} %all-gather.2.cloned.1.call-done, f32[256,511]{1,0:T(8,128)} %copy-done.4), kind=kOutput, calls=%fused_computation.3 | convolution fusion | flops 807141376 | bytes 6553600 | tf_op jit(solution)/shard_map/dot_general | solution.py:136
  85.5 3.5 %collective-permute-done = bf16[256,1536]{1,0:T(8,128)(2,1)} collective-permute-done((bf16[256,1536]{1,0:T(8,128)(2,1)}, bf16[256,1536]{1,0:T(8,128)(2,1)}, u32[]{:S(2)}, u32[]{:S(2)}) %collective-permute-start) | collective-permute-done | bytes 786464 | tf_op jit(solution)/shard_map/ppermute | solution.py:68
  89.0 2.1 %broadcast_select_fusion.1 = bf16[256,1536]{1,0:T(8,128)(2,1)} fusion(bf16[256,1536]{1,0:T(8,128)(2,1)} %collective-permute-done, bf16[256,1536]{1,0:T(8,128)(2,1)} %convolution_convert_fusion.1, pred[]{:T(512)S(6)} %and.43), kind=kLoop, calls=%fused_computation.21 | loop fusion | flops 393216 | bytes 2359297 | tf_op jit(solution)/shard_map/jit(_where)/select_n | solution.py:70
  91.0 2.2 %collective-permute-start.2 = (bf16[256,1536]{1,0:T(8,128)(2,1)}, bf16[256,1536]{1,0:T(8,128)(2,1)}, u32[]{:S(2)}, u32[]{:S(2)}) collective-permute-start(bf16[256,1536]{1,0:T(8,128)(2,1)} %broadcast_select_fusion.1), channel_id=1, source_target_pairs={{0,1},{2,3},{4,5},{6,7},{9,8},{11,10},{13,12},{15,14},{16,17},{18,... | collective-permute-start | bytes 2359304 | tf_op jit(solution)/shard_map/ppermute | solution.py:68
  94.5 4.4 %collective-permute-start.1 = (bf16[256,1536]{1,0:T(8,128)(2,1)}, bf16[256,1536]{1,0:T(8,128)(2,1)S(1)}, u32[]{:S(2)}, u32[]{:S(2)}) collective-permute-start(bf16[256,1536]{1,0:T(8,128)(2,1)} %convolution_convert_fusion.2), channel_id=1, source_target_pairs={{0,2},{4,6},{9,11},{13,15},{18,16},{22,20},{27,25},{31,29}} | collective-permute-start | bytes 2359304 | tf_op jit(solution)/shard_map/ppermute | solution.py:68
  99.0 0.7 fusion.1
  99.7 0.0 collective-permute-done.2
  99.7 1.2 broadcast_select_fusion.3.left_ref
  100.9 0.0 copy-start
  100.9 0.0 copy-start.5
  100.9 14.9 %shard_map.68.rest_0_ = f32[3072,6144]{1,0:T(8,128)} custom-call(bf16[256,1536]{1,0:T(8,128)(2,1)S(1)} %broadcast_select_fusion.3.left_ref, bf16[256,6144]{1,0:T(8,128)(2,1)S(1)} %convolution_convert_fusion.right_ref), custom_call_target="tpu_custom_call" | custom-call | flops 4831838208 | bytes 41680896 | tf_op jit(solution)/shard_map/pallas_call | solution.py:105
  115.8 0.0 collective-permute-done.1
  115.8 0.0 copy-done.5
  115.8 0.1 broadcast_select_fusion
  115.9 1.3 collective-permute-start.3
  117.3 1.8 %fusion = f32[256,256]{1,0:T(8,128)S(1)} fusion(bf16[256,6144]{1,0:T(8,128)(2,1)S(1)} %convolution_convert_fusion.right_ref, f32[6144]{0:T(1024)S(1)} %broadcast_add_fusion), kind=kOutput, calls=%fused_computation.2 | convolution fusion | flops 2419064832 | bytes 3432448 | tf_op jit(solution)/shard_map/dot_general | solution.py:150
  119.1 0.0 copy-start.6
  119.1 0.1 collective-permute-start.7
  119.2 0.0 collective-permute-done.3
  119.2 0.1 broadcast_select_fusion.2.left_ref
  119.3 0.0 copy-start.2
  119.3 0.3 multiply_reduce_fusion
  119.7 0.0 copy-done
  119.7 0.4 copy-done.6
  120.1 1.0 fusion.10
  121.1 0.0 copy-done.2
  121.1 0.6 collective-permute-start.4
  121.7 3.4 %collective-permute-done.4 = f32[256,32]{0,1:T(8,128)S(1)} collective-permute-done((f32[256,32]{0,1:T(8,128)S(1)}, f32[256,32]{0,1:T(8,128)S(1)}, u32[]{:S(2)}, u32[]{:S(2)}) %collective-permute-start.4) | collective-permute-done | bytes 32800 | tf_op jit(solution)/shard_map/ppermute | solution.py:25
  125.1 0.0 collective-permute-start.5
  125.4 0.0 collective-permute-done.7
  125.4 1.0 add.90
  126.4 0.1 collective-permute-start.8
  126.5 2.6 %collective-permute-done.5 = f32[256,32]{0,1:T(8,128)S(1)} collective-permute-done((f32[256,32]{0,1:T(8,128)S(1)}, f32[256,32]{0,1:T(8,128)S(1)}, u32[]{:S(2)}, u32[]{:S(2)}) %collective-permute-start.5) | collective-permute-done | bytes 32800 | tf_op jit(solution)/shard_map/ppermute | solution.py:25
  129.0 0.0 copy-start.1
  129.0 0.1 collective-permute-start.6
  129.1 0.0 copy-start.3
  129.1 1.2 copy-done.3
  130.3 0.0 copy-start.7
  130.3 14.9 %shard_map.69 = f32[3072,6144]{1,0:T(8,128)} custom-call(bf16[256,1536]{1,0:T(8,128)(2,1)S(1)} %copy-done.3, bf16[256,6144]{1,0:T(8,128)(2,1)S(1)} %convolution_convert_fusion.right_ref, f32[3072,6144]{1,0:T(8,128)} %shard_map.68.rest_0_), custom_call_target="tpu_custom_call", output_to_operand_aliasing={{}: (2, {})} | custom-call | flops 4831838208 | bytes 41680896 | tf_op jit(solution)/shard_map/pallas_call | solution.py:105
  145.2 0.0 collective-permute-done.6
  145.2 0.0 copy-done.1
  145.2 0.0 copy-done.7
  145.2 0.6 convolution_subtract_fusion.1
  145.8 0.0 collective-permute-done.8
  145.8 0.3 fusion.7
  146.1 1.4 fusion.5
  (4 shorter events, 0.0 us)
Async XLA Ops:
  7.2 66.2 %all-gather.2.cloned.1.call-start = ((), (), s32[]{:S(2)}) async-start(), calls=%async_computation | async-start | bytes 3538944 | tf_op jit(solution)/shard_map/all_gather | solution.py:135
  9.2 70.8 %copy-start.4 = (f32[256,511]{1,0:T(8,128)}, f32[256,511]{1,0:T(8,128)S(1)}, u32[]{:S(2)}) copy-start(f32[256,511]{1,0:T(8,128)S(1)} %reshape.20) | copy-start | bytes 1569796
  75.8 13.2 %collective-permute-start = (bf16[256,1536]{1,0:T(8,128)(2,1)}, bf16[256,1536]{1,0:T(8,128)(2,1)}, u32[]{:S(2)}, u32[]{:S(2)}) collective-permute-start(bf16[256,1536]{1,0:T(8,128)(2,1)} %convolution_convert_fusion.1), channel_id=1, source_target_pairs={{0,2},{4,6},{9,11},{13,15},{18,16},{22,20},{27,25},{31,29}} | collective-permute-start | bytes 2359304 | tf_op jit(solution)/shard_map/ppermute | solution.py:68
  91.0 8.6 %collective-permute-start.2 = (bf16[256,1536]{1,0:T(8,128)(2,1)}, bf16[256,1536]{1,0:T(8,128)(2,1)}, u32[]{:S(2)}, u32[]{:S(2)}) collective-permute-start(bf16[256,1536]{1,0:T(8,128)(2,1)} %broadcast_select_fusion.1), channel_id=1, source_target_pairs={{0,1},{2,3},{4,5},{6,7},{9,8},{11,10},{13,12},{15,14},{16,17},{18,... | collective-permute-start | bytes 2359304 | tf_op jit(solution)/shard_map/ppermute | solution.py:68
  94.5 21.3 %collective-permute-start.1 = (bf16[256,1536]{1,0:T(8,128)(2,1)}, bf16[256,1536]{1,0:T(8,128)(2,1)S(1)}, u32[]{:S(2)}, u32[]{:S(2)}) collective-permute-start(bf16[256,1536]{1,0:T(8,128)(2,1)} %convolution_convert_fusion.2), channel_id=1, source_target_pairs={{0,2},{4,6},{9,11},{13,15},{18,16},{22,20},{27,25},{31,29}} | collective-permute-start | bytes 2359304 | tf_op jit(solution)/shard_map/ppermute | solution.py:68
  100.9 18.8 %copy-start = (bf16[256,1536]{1,0:T(8,128)(2,1)}, bf16[256,1536]{1,0:T(8,128)(2,1)S(1)}, u32[]{:S(2)}) copy-start(bf16[256,1536]{1,0:T(8,128)(2,1)S(1)} %broadcast_select_fusion.3.left_ref) | copy-start | bytes 2359300
  100.9 14.9 %copy-start.5 = (bf16[256,1536]{1,0:T(8,128)(2,1)S(1)}, bf16[256,1536]{1,0:T(8,128)(2,1)}, u32[]{:S(2)}) copy-start(bf16[256,1536]{1,0:T(8,128)(2,1)} %convolution_convert_fusion.2) | copy-start | bytes 2359300
  115.9 3.3 %collective-permute-start.3 = (bf16[256,1536]{1,0:T(8,128)(2,1)S(1)}, bf16[256,1536]{1,0:T(8,128)(2,1)S(1)}, u32[]{:S(2)}, u32[]{:S(2)}) collective-permute-start(bf16[256,1536]{1,0:T(8,128)(2,1)S(1)} %broadcast_select_fusion), channel_id=1, source_target_pairs={{0,1},{2,3},{4,5},{6,7},{9,8},{11,10},{13,12},{15,14},{16,17},{18,... | collective-permute-start | bytes 2359304 | tf_op jit(solution)/shard_map/ppermute | solution.py:68
  119.1 1.0 copy-start.6
  119.1 6.3 %collective-permute-start.7 = (f32[256,256]{1,0:T(8,128)S(1)}, f32[256,256]{1,0:T(8,128)}, u32[]{:S(2)}, u32[]{:S(2)}) collective-permute-start(f32[256,256]{1,0:T(8,128)S(1)} %fusion), channel_id=1, source_target_pairs={{0,1},{1,0},{2,3},{3,2},{4,5},{5,4},{6,7},{7,6},{8,9},{9,8},{10,11... | collective-permute-start | bytes 786440 | tf_op jit(solution)/shard_map/ppermute | solution.py:25
  119.3 1.8 %copy-start.2 = (bf16[256,1536]{1,0:T(8,128)(2,1)}, bf16[256,1536]{1,0:T(8,128)(2,1)S(1)}, u32[]{:S(2)}) copy-start(bf16[256,1536]{1,0:T(8,128)(2,1)S(1)} %broadcast_select_fusion.2.left_ref) | copy-start | bytes 2359300
  121.1 4.0 %collective-permute-start.4 = (f32[256,32]{0,1:T(8,128)S(1)}, f32[256,32]{0,1:T(8,128)S(1)}, u32[]{:S(2)}, u32[]{:S(2)}) collective-permute-start(f32[256,32]{0,1:T(8,128)S(1)} %fusion.10), channel_id=1, source_target_pairs={{0,4},{4,0},{8,12},{12,8},{16,20},{20,16},{24,28},{28,24},{1,5},{5... | collective-permute-start | bytes 98312 | tf_op jit(solution)/shard_map/ppermute | solution.py:25
  125.1 3.9 %collective-permute-start.5 = (f32[256,32]{0,1:T(8,128)S(1)}, f32[256,32]{0,1:T(8,128)S(1)}, u32[]{:S(2)}, u32[]{:S(2)}) collective-permute-start(f32[256,32]{0,1:T(8,128)S(1)} %add.83), channel_id=1, source_target_pairs={{0,8},{4,12},{8,0},{12,4},{16,24},{20,28},{24,16},{28,20},{1,9},{5... | collective-permute-start | bytes 98312 | tf_op jit(solution)/shard_map/ppermute | solution.py:25
  126.4 19.5 %collective-permute-start.8 = (f32[256,256]{1,0:T(8,128)S(1)}, f32[256,256]{1,0:T(8,128)S(1)}, u32[]{:S(2)}, u32[]{:S(2)}) collective-permute-start(f32[256,256]{1,0:T(8,128)S(1)} %add.90), channel_id=1, source_target_pairs={{0,2},{1,3},{2,0},{3,1},{4,6},{5,7},{6,4},{7,5},{8,10},{9,11},{10,... | collective-permute-start | bytes 786440 | tf_op jit(solution)/shard_map/ppermute | solution.py:25
  129.0 16.2 %copy-start.1 = (bf16[256,1536]{1,0:T(8,128)(2,1)S(1)}, bf16[256,1536]{1,0:T(8,128)(2,1)}, u32[]{:S(2)}) copy-start(bf16[256,1536]{1,0:T(8,128)(2,1)} %copy-done) | copy-start | bytes 2359300
  129.0 16.2 %collective-permute-start.6 = (f32[256,32]{0,1:T(8,128)S(1)}, f32[256,32]{0,1:T(8,128)S(1)}, u32[]{:S(2)}, u32[]{:S(2)}) collective-permute-start(f32[256,32]{0,1:T(8,128)S(1)} %add.84), channel_id=1, source_target_pairs={{0,16},{4,20},{8,24},{12,28},{16,0},{20,4},{24,8},{28,12},{1,17},{... | collective-permute-start | bytes 98312 | tf_op jit(solution)/shard_map/ppermute | solution.py:25
  129.1 1.2 copy-start.3
  130.3 14.9 %copy-start.7 = (f32[3072,32]{0,1:T(8,128)S(1)}, f32[3072,32]{0,1:T(8,128)}, u32[]{:S(2)}) copy-start(f32[3072,32]{0,1:T(8,128)} %param.7) | copy-start | bytes 1179652
Sparse Core Ops, SparseCore 0:
  10.2 63.1 all-gather.1

commit v17 on v15

--- a/solution.py
+++ b/solution.py
@@ -85,7 +85,7 @@
 def normal_rows(left, right, total_rows, first_row, previous):
     epochs, rows = left.shape
     width = right.shape[1]
-    tile_rows = 128 if rows % 128 == 0 else rows
+    tile_rows = 384 if rows % 384 == 0 else rows
     tile_cols = width
     row_offset = first_row // tile_rows
     in_specs = [

time: 155 us -> 153 us (0.987)
  transfers between devices with their start and end apart: 10 -> 10, of which waited for: 4 -> 4; matrix products, arithmetic and copies ran while one was open for 9% -> 9% of each run, Pallas kernels for 19% -> 18%
where the time goes in v17:
time: 153 us
  waiting for transfers between devices  74.3 us (49%)
  Pallas kernels  28 us (18%)
  between operations  15.9 us (10%)
  starting transfers between devices  13.1 us (9%)
  matrix products  12.9 us (8%)
  other arithmetic  5.48 us (4%)
  local copies, waits for them, and re-layouts  2.9 us (2%)
    all_gather x1, waiting for transfers between devices, body(): whole_panel = lax.all_gather(design, 'row', axis=0, tiled=True)  64.2 us
    pallas_call x2, Pallas kernels, normal_rows(): pl.pallas_call(kernel, grid=(width // tile_cols, rows // tile_rows), in_s...  28 us
    ppermute x4, starting transfers between devices, tree_broadcast(): arrived = lax.ppermute(block, ('row', 'col'), pairs)  12.2 us
    ppermute x5, waiting for transfers between devices, swap(): return lax.ppermute(block, axis, [(i, i ^ bit) for i in range(count)])  5.95 us
    dot_general x2, matrix products, whiten_rows(): jnp.dot(filter_matrix, block, preferred_element_type=jnp.float32)  4.84 us
    ppermute x4, waiting for transfers between devices, tree_broadcast(): arrived = lax.ppermute(block, ('row', 'col'), pairs)  3.5 us
    select_n x4, other arithmetic, tree_broadcast(): jnp.where((offset & ~done == 0) & (offset & bit != 0), arrived, block)  3.5 us
  transfers between devices with their start and end apart: 10, of which 4 were waited for; matrix products, arithmetic and copies ran while one was open for 9% of the time, Pallas kernels for 18%

profile of v17, /device:TPU:0, one launch (start us, length us, event | category | flops | bytes accessed | tf_op | source)
XLA Modules:
  0.0 152.6 jit_solution(13469937889319732712)
XLA Ops:
  7.2 0.0 all-gather.2.cloned.1.call-start
  7.2 0.7 all-gather.2.cloned.1.call-update
  7.9 0.7 concatenate.6
  8.6 0.1 broadcast_bitcast_fusion
  8.7 0.1 copy.8
  8.8 0.4 reshape.20
  9.2 0.0 copy-start.4
  9.2 64.2 %all-gather.2.cloned.1.call-done = bf16[256,6144]{1,0:T(8,128)(2,1)} async-done(((bf16[32,6144]{1,0:T(8,128)(2,1)}), bf16[256,6144]{1,0:T(8,128)(2,1)}) %all-gather.2.cloned.1.call-update) | async-done | bytes 3145744 | tf_op jit(solution)/shard_map/all_gather | solution.py:135
  73.4 2.4 %convolution_convert_fusion.1 = bf16[256,1536]{1,0:T(8,128)(2,1)} fusion(bf16[256,6144]{1,0:T(8,128)(2,1)} %all-gather.2.cloned.1.call-done, s32[]{:T(128)S(6)} %select_n.45, f32[256,511]{1,0:T(8,128)S(1)} %reshape.20), kind=kOutput, calls=%fused_computation.13 | convolution fusion | flops 201981952 | bytes 1835012 | tf_op jit(solution)/shard_map/dot_general | solution.py:144
  75.8 4.3 %collective-permute-start = (bf16[256,1536]{1,0:T(8,128)(2,1)}, bf16[256,1536]{1,0:T(8,128)(2,1)}, u32[]{:S(2)}, u32[]{:S(2)}) collective-permute-start(bf16[256,1536]{1,0:T(8,128)(2,1)} %convolution_convert_fusion.1), channel_id=1, source_target_pairs={{0,2},{4,6},{9,11},{13,15},{18,16},{22,20},{27,25},{31,29}} | collective-permute-start | bytes 2359304 | tf_op jit(solution)/shard_map/ppermute | solution.py:68
  80.0 0.0 copy-done.4
  80.0 2.4 %convolution_convert_fusion.2 = bf16[256,1536]{1,0:T(8,128)(2,1)} fusion(bf16[256,6144]{1,0:T(8,128)(2,1)} %all-gather.2.cloned.1.call-done, s32[]{:T(128)S(6)} %select_n.44, f32[256,511]{1,0:T(8,128)S(1)} %reshape.20), kind=kOutput, calls=%fused_computation.14 | convolution fusion | flops 201981952 | bytes 1835012 | tf_op jit(solution)/shard_map/dot_general | solution.py:144
  82.5 3.0 %convolution_convert_fusion.right_ref = bf16[256,6144]{1,0:T(8,128)(2,1)S(1)} fusion(bf16[256,6144]{1,0:T(8,128)(2,1)} %all-gather.2.cloned.1.call-done, f32[256,511]{1,0:T(8,128)} %copy-done.4), kind=kOutput, calls=%fused_computation.3 | convolution fusion | flops 807141376 | bytes 6553600 | tf_op jit(solution)/shard_map/dot_general | solution.py:136
  85.5 3.5 %collective-permute-done = bf16[256,1536]{1,0:T(8,128)(2,1)} collective-permute-done((bf16[256,1536]{1,0:T(8,128)(2,1)}, bf16[256,1536]{1,0:T(8,128)(2,1)}, u32[]{:S(2)}, u32[]{:S(2)}) %collective-permute-start) | collective-permute-done | bytes 786464 | tf_op jit(solution)/shard_map/ppermute | solution.py:68
  89.0 2.1 %broadcast_select_fusion.1 = bf16[256,1536]{1,0:T(8,128)(2,1)} fusion(bf16[256,1536]{1,0:T(8,128)(2,1)} %collective-permute-done, bf16[256,1536]{1,0:T(8,128)(2,1)} %convolution_convert_fusion.1, pred[]{:T(512)S(6)} %and.43), kind=kLoop, calls=%fused_computation.21 | loop fusion | flops 393216 | bytes 2359297 | tf_op jit(solution)/shard_map/jit(_where)/select_n | solution.py:70
  91.0 2.2 %collective-permute-start.2 = (bf16[256,1536]{1,0:T(8,128)(2,1)}, bf16[256,1536]{1,0:T(8,128)(2,1)}, u32[]{:S(2)}, u32[]{:S(2)}) collective-permute-start(bf16[256,1536]{1,0:T(8,128)(2,1)} %broadcast_select_fusion.1), channel_id=1, source_target_pairs={{0,1},{2,3},{4,5},{6,7},{9,8},{11,10},{13,12},{15,14},{16,17},{18,... | collective-permute-start | bytes 2359304 | tf_op jit(solution)/shard_map/ppermute | solution.py:68
  94.5 4.4 %collective-permute-start.1 = (bf16[256,1536]{1,0:T(8,128)(2,1)}, bf16[256,1536]{1,0:T(8,128)(2,1)S(1)}, u32[]{:S(2)}, u32[]{:S(2)}) collective-permute-start(bf16[256,1536]{1,0:T(8,128)(2,1)} %convolution_convert_fusion.2), channel_id=1, source_target_pairs={{0,2},{4,6},{9,11},{13,15},{18,16},{22,20},{27,25},{31,29}} | collective-permute-start | bytes 2359304 | tf_op jit(solution)/shard_map/ppermute | solution.py:68
  99.0 0.7 fusion.1
  99.7 0.0 collective-permute-done.2
  99.7 1.2 broadcast_select_fusion.3.left_ref
  100.9 0.0 copy-start
  100.9 0.0 copy-start.5
  100.9 14.0 %shard_map.68.rest_0_ = f32[3072,6144]{1,0:T(8,128)} custom-call(bf16[256,1536]{1,0:T(8,128)(2,1)S(1)} %broadcast_select_fusion.3.left_ref, bf16[256,6144]{1,0:T(8,128)(2,1)S(1)} %convolution_convert_fusion.right_ref), custom_call_target="tpu_custom_call" | custom-call | flops 4831838208 | bytes 41680896 | tf_op jit(solution)/shard_map/pallas_call | solution.py:105
  114.9 0.0 collective-permute-done.1
  115.0 0.0 copy-done.5
  115.0 0.1 broadcast_select_fusion
  115.0 1.3 collective-permute-start.3
  116.4 1.8 %fusion = f32[256,256]{1,0:T(8,128)S(1)} fusion(bf16[256,6144]{1,0:T(8,128)(2,1)S(1)} %convolution_convert_fusion.right_ref, f32[6144]{0:T(1024)S(1)} %broadcast_add_fusion), kind=kOutput, calls=%fused_computation.2 | convolution fusion | flops 2419064832 | bytes 3432448 | tf_op jit(solution)/shard_map/dot_general | solution.py:150
  118.2 0.0 copy-start.6
  118.2 0.1 collective-permute-start.7
  118.3 0.0 collective-permute-done.3
  118.3 0.1 broadcast_select_fusion.2.left_ref
  118.4 0.0 copy-start.2
  118.4 0.3 multiply_reduce_fusion
  118.8 0.0 copy-done
  118.8 0.4 copy-done.6
  119.2 1.0 fusion.10
  120.2 0.0 copy-done.2
  120.2 0.6 collective-permute-start.4
  120.9 3.4 %collective-permute-done.4 = f32[256,32]{0,1:T(8,128)S(1)} collective-permute-done((f32[256,32]{0,1:T(8,128)S(1)}, f32[256,32]{0,1:T(8,128)S(1)}, u32[]{:S(2)}, u32[]{:S(2)}) %collective-permute-start.4) | collective-permute-done | bytes 32800 | tf_op jit(solution)/shard_map/ppermute | solution.py:25
  124.2 0.0 collective-permute-start.5
  124.5 0.0 collective-permute-done.7
  124.5 1.0 add.90
  125.5 0.1 collective-permute-start.8
  125.6 2.6 %collective-permute-done.5 = f32[256,32]{0,1:T(8,128)S(1)} collective-permute-done((f32[256,32]{0,1:T(8,128)S(1)}, f32[256,32]{0,1:T(8,128)S(1)}, u32[]{:S(2)}, u32[]{:S(2)}) %collective-permute-start.5) | collective-permute-done | bytes 32800 | tf_op jit(solution)/shard_map/ppermute | solution.py:25
  128.2 0.0 copy-start.1
  128.2 0.1 collective-permute-start.6
  128.2 0.0 copy-start.3
  128.2 1.2 copy-done.3
  129.4 0.0 copy-start.7
  129.4 14.0 %shard_map.69 = f32[3072,6144]{1,0:T(8,128)} custom-call(bf16[256,1536]{1,0:T(8,128)(2,1)S(1)} %copy-done.3, bf16[256,6144]{1,0:T(8,128)(2,1)S(1)} %convolution_convert_fusion.right_ref, f32[3072,6144]{1,0:T(8,128)} %shard_map.68.rest_0_), custom_call_target="tpu_custom_call", output_to_operand_aliasing={{}: (2, {})} | custom-call | flops 4831838208 | bytes 41680896 | tf_op jit(solution)/shard_map/pallas_call | solution.py:105
  143.4 0.0 collective-permute-done.6
  143.4 0.0 copy-done.1
  143.4 0.0 copy-done.7
  143.4 0.6 convolution_subtract_fusion.1
  144.1 0.0 collective-permute-done.8
  144.1 0.3 fusion.7
  144.3 1.4 fusion.5
  (4 shorter events, 0.0 us)
Async XLA Ops:
  7.2 66.2 %all-gather.2.cloned.1.call-start = ((), (), s32[]{:S(2)}) async-start(), calls=%async_computation | async-start | bytes 3538944 | tf_op jit(solution)/shard_map/all_gather | solution.py:135
  9.2 70.8 %copy-start.4 = (f32[256,511]{1,0:T(8,128)}, f32[256,511]{1,0:T(8,128)S(1)}, u32[]{:S(2)}) copy-start(f32[256,511]{1,0:T(8,128)S(1)} %reshape.20) | copy-start | bytes 1569796
  75.8 13.2 %collective-permute-start = (bf16[256,1536]{1,0:T(8,128)(2,1)}, bf16[256,1536]{1,0:T(8,128)(2,1)}, u32[]{:S(2)}, u32[]{:S(2)}) collective-permute-start(bf16[256,1536]{1,0:T(8,128)(2,1)} %convolution_convert_fusion.1), channel_id=1, source_target_pairs={{0,2},{4,6},{9,11},{13,15},{18,16},{22,20},{27,25},{31,29}} | collective-permute-start | bytes 2359304 | tf_op jit(solution)/shard_map/ppermute | solution.py:68
  91.0 8.6 %collective-permute-start.2 = (bf16[256,1536]{1,0:T(8,128)(2,1)}, bf16[256,1536]{1,0:T(8,128)(2,1)}, u32[]{:S(2)}, u32[]{:S(2)}) collective-permute-start(bf16[256,1536]{1,0:T(8,128)(2,1)} %broadcast_select_fusion.1), channel_id=1, source_target_pairs={{0,1},{2,3},{4,5},{6,7},{9,8},{11,10},{13,12},{15,14},{16,17},{18,... | collective-permute-start | bytes 2359304 | tf_op jit(solution)/shard_map/ppermute | solution.py:68
  94.5 20.4 %collective-permute-start.1 = (bf16[256,1536]{1,0:T(8,128)(2,1)}, bf16[256,1536]{1,0:T(8,128)(2,1)S(1)}, u32[]{:S(2)}, u32[]{:S(2)}) collective-permute-start(bf16[256,1536]{1,0:T(8,128)(2,1)} %convolution_convert_fusion.2), channel_id=1, source_target_pairs={{0,2},{4,6},{9,11},{13,15},{18,16},{22,20},{27,25},{31,29}} | collective-permute-start | bytes 2359304 | tf_op jit(solution)/shard_map/ppermute | solution.py:68
  100.9 17.9 %copy-start = (bf16[256,1536]{1,0:T(8,128)(2,1)}, bf16[256,1536]{1,0:T(8,128)(2,1)S(1)}, u32[]{:S(2)}) copy-start(bf16[256,1536]{1,0:T(8,128)(2,1)S(1)} %broadcast_select_fusion.3.left_ref) | copy-start | bytes 2359300
  100.9 14.0 %copy-start.5 = (bf16[256,1536]{1,0:T(8,128)(2,1)S(1)}, bf16[256,1536]{1,0:T(8,128)(2,1)}, u32[]{:S(2)}) copy-start(bf16[256,1536]{1,0:T(8,128)(2,1)} %convolution_convert_fusion.2) | copy-start | bytes 2359300
  115.0 3.3 %collective-permute-start.3 = (bf16[256,1536]{1,0:T(8,128)(2,1)S(1)}, bf16[256,1536]{1,0:T(8,128)(2,1)S(1)}, u32[]{:S(2)}, u32[]{:S(2)}) collective-permute-start(bf16[256,1536]{1,0:T(8,128)(2,1)S(1)} %broadcast_select_fusion), channel_id=1, source_target_pairs={{0,1},{2,3},{4,5},{6,7},{9,8},{11,10},{13,12},{15,14},{16,17},{18,... | collective-permute-start | bytes 2359304 | tf_op jit(solution)/shard_map/ppermute | solution.py:68
  118.2 1.0 copy-start.6
  118.2 6.3 %collective-permute-start.7 = (f32[256,256]{1,0:T(8,128)S(1)}, f32[256,256]{1,0:T(8,128)}, u32[]{:S(2)}, u32[]{:S(2)}) collective-permute-start(f32[256,256]{1,0:T(8,128)S(1)} %fusion), channel_id=1, source_target_pairs={{0,1},{1,0},{2,3},{3,2},{4,5},{5,4},{6,7},{7,6},{8,9},{9,8},{10,11... | collective-permute-start | bytes 786440 | tf_op jit(solution)/shard_map/ppermute | solution.py:25
  118.4 1.8 %copy-start.2 = (bf16[256,1536]{1,0:T(8,128)(2,1)}, bf16[256,1536]{1,0:T(8,128)(2,1)S(1)}, u32[]{:S(2)}) copy-start(bf16[256,1536]{1,0:T(8,128)(2,1)S(1)} %broadcast_select_fusion.2.left_ref) | copy-start | bytes 2359300
  120.2 4.0 %collective-permute-start.4 = (f32[256,32]{0,1:T(8,128)S(1)}, f32[256,32]{0,1:T(8,128)S(1)}, u32[]{:S(2)}, u32[]{:S(2)}) collective-permute-start(f32[256,32]{0,1:T(8,128)S(1)} %fusion.10), channel_id=1, source_target_pairs={{0,4},{4,0},{8,12},{12,8},{16,20},{20,16},{24,28},{28,24},{1,5},{5... | collective-permute-start | bytes 98312 | tf_op jit(solution)/shard_map/ppermute | solution.py:25
  124.2 3.9 %collective-permute-start.5 = (f32[256,32]{0,1:T(8,128)S(1)}, f32[256,32]{0,1:T(8,128)S(1)}, u32[]{:S(2)}, u32[]{:S(2)}) collective-permute-start(f32[256,32]{0,1:T(8,128)S(1)} %add.83), channel_id=1, source_target_pairs={{0,8},{4,12},{8,0},{12,4},{16,24},{20,28},{24,16},{28,20},{1,9},{5... | collective-permute-start | bytes 98312 | tf_op jit(solution)/shard_map/ppermute | solution.py:25
  125.5 18.6 %collective-permute-start.8 = (f32[256,256]{1,0:T(8,128)S(1)}, f32[256,256]{1,0:T(8,128)S(1)}, u32[]{:S(2)}, u32[]{:S(2)}) collective-permute-start(f32[256,256]{1,0:T(8,128)S(1)} %add.90), channel_id=1, source_target_pairs={{0,2},{1,3},{2,0},{3,1},{4,6},{5,7},{6,4},{7,5},{8,10},{9,11},{10,... | collective-permute-start | bytes 786440 | tf_op jit(solution)/shard_map/ppermute | solution.py:25
  128.2 15.3 %copy-start.1 = (bf16[256,1536]{1,0:T(8,128)(2,1)S(1)}, bf16[256,1536]{1,0:T(8,128)(2,1)}, u32[]{:S(2)}) copy-start(bf16[256,1536]{1,0:T(8,128)(2,1)} %copy-done) | copy-start | bytes 2359300
  128.2 15.3 %collective-permute-start.6 = (f32[256,32]{0,1:T(8,128)S(1)}, f32[256,32]{0,1:T(8,128)S(1)}, u32[]{:S(2)}, u32[]{:S(2)}) collective-permute-start(f32[256,32]{0,1:T(8,128)S(1)} %add.84), channel_id=1, source_target_pairs={{0,16},{4,20},{8,24},{12,28},{16,0},{20,4},{24,8},{28,12},{1,17},{... | collective-permute-start | bytes 98312 | tf_op jit(solution)/shard_map/ppermute | solution.py:25
  128.2 1.2 copy-start.3
  129.4 14.0 %copy-start.7 = (f32[3072,32]{0,1:T(8,128)S(1)}, f32[3072,32]{0,1:T(8,128)}, u32[]{:S(2)}) copy-start(f32[3072,32]{0,1:T(8,128)} %param.7) | copy-start | bytes 1179652
Sparse Core Ops, SparseCore 0:
  10.2 63.1 all-gather.1
